TPU v7x, 128 devices: a whole 4x4x4 slice. The times are simulated.
128 devices in a mesh: section: 4 (over x_hi, core), blk: 32 (over z, x_lo, y).
Axes of the slice: x: 4 (x_hi: 2, x_lo: 2; x = x_hi * 2 + x_lo), y: 4, z: 4, core: 2. Of those that a mesh axis runs over, the one named last changes fastest.
Arguments:
- prog_ids: int32 [5120, 256], P('blk'), may hold values from 0 to 383, as said below
- spec_ids: int32 [5120, 256], P('blk'), may hold values from 0 to 383
- prog_table: bfloat16 [384, 2048], replicated, may hold values from -6 to 6
- spec_table: bfloat16 [384, 2048], replicated, may hold values from -6 to 6
- layer_weights: bfloat16 [8192, 2048], P('section'), may hold values from -0.125 to 0.125
- gains: float32 [4, 2048], P('section'), may hold values from 0.5 to 1.5
- prog_proj: bfloat16 [2048, 768], replicated, may hold values from -0.125 to 0.125
- spec_proj: bfloat16 [2048, 768], replicated, may hold values from -0.125 to 0.125
Outputs:
- layer_grads: float32 [8192, 2048], P(('section', 'blk'))
Inputs may be any that keep to these rules, and one draw needn't show every extreme that they name: `prog_ids`: each program in the second half of the batch repeats, at most of its positions, the bytes of the program 5120/2 rows earlier; each program in an odd-numbered block of 160 rows repeats nearly all bytes of the program 160 rows earlier; each specification repeats most bytes of its own program.
All inputs are finite; a program needn't handle non-finite values.
Results may differ from a plain program's by a relative error of at most 0.0065.
Values may be sent and summed in bfloat16 or wider, within the bound.
No kernel may reach another device: no remote copies, remote signals or barrier semaphores. Data moves between devices by JAX's collectives and lax.ppermute only.
A program may use at most 128 MiB of HBM per device.

v0:
```python
import jax
import jax.numpy as jnp
from jax import lax
from jax.sharding import PartitionSpec as P

L = 256
MICRO = 1


logit_scale = 30.0
norm_eps = 1e-06


def shift_pairs(axis, pairs):
    return lambda value: lax.ppermute(value, axis, pairs)


def gather_rows(value, axis):
    count = lax.axis_size(axis)
    spread = jnp.broadcast_to(value[None], (count,) + value.shape)
    got = lax.all_to_all(spread, axis, 0, 0, tiled=True)
    return got.reshape((count * value.shape[0],) + value.shape[1:])


def layer_parts(hidden, weight, gain):
    wide = hidden.astype(jnp.float32)
    inverse = lax.rsqrt(jnp.mean(wide * wide, axis=1, keepdims=True) + norm_eps)
    normed = wide * inverse
    scaled = (normed * gain).astype(jnp.bfloat16)
    mixed = jnp.dot(scaled, weight, preferred_element_type=jnp.float32)
    return (wide, inverse, normed, scaled, mixed)


def layer_forward(hidden, weight, gain):
    wide, inverse, normed, scaled, mixed = layer_parts(hidden, weight, gain)
    return (wide + mixed * jax.nn.sigmoid(mixed)).astype(jnp.bfloat16)


def layer_backward(hidden, upstream, weight, gain):
    wide, inverse, normed, scaled, mixed = layer_parts(hidden, weight, gain)
    sigma = jax.nn.sigmoid(mixed)
    up_wide = upstream.astype(jnp.float32)
    dmixed = (up_wide * sigma * (1.0 + mixed * (1.0 - sigma))).astype(jnp.bfloat16)
    dnormed = (
        lax.dot_general(
            dmixed, weight, (((1,), (1,)), ((), ())), preferred_element_type=jnp.float32
        )
        * gain
    )
    dhidden = (
        up_wide + inverse * (dnormed - normed * jnp.mean(dnormed * normed, axis=1, keepdims=True))
    ).astype(jnp.bfloat16)
    return (dhidden, scaled, dmixed)


def embed_rows(hidden, proj):
    emb = jnp.dot(hidden, proj, preferred_element_type=jnp.float32)
    inverse = lax.rsqrt(jnp.sum(emb * emb, axis=1, keepdims=True) + norm_eps)
    unit = emb * inverse
    return (unit, inverse, unit.astype(jnp.bfloat16))


def embed_back(dkey, unit, inverse, proj):
    demb = (inverse * (dkey - unit * jnp.sum(unit * dkey, axis=1, keepdims=True))).astype(
        jnp.bfloat16
    )
    return lax.dot_general(
        demb, proj, (((1,), (1,)), ((), ())), preferred_element_type=jnp.float32
    ).astype(jnp.bfloat16)


def keep_where(buffer, value, index, valid):
    previous = lax.dynamic_index_in_dim(buffer, index, 0, keepdims=False)
    return lax.dynamic_update_index_in_dim(buffer, jnp.where(valid, value, previous), index, 0)


def local(prog_ids, spec_ids, prog_table, spec_table, layer_weights, gains, prog_proj, spec_proj):
    section_index = lax.axis_index("section")
    last_section = lax.axis_size("section") - 1
    top_section = last_section - 1
    spec_section = section_index == last_section
    token_ids = jnp.where(spec_section, spec_ids, prog_ids)
    table = jnp.where(spec_section, spec_table, prog_table)
    vocab_iota = jnp.arange(table.shape[0], dtype=jnp.int32)
    counts = jnp.sum(
        (token_ids[:, :, None] == vocab_iota[None, None, :]).astype(jnp.float32), axis=1
    ).astype(jnp.bfloat16)
    sample_rows = prog_ids.shape[0]
    micro_rows = sample_rows // MICRO
    width = layer_weights.shape[1]
    first_inputs = (jnp.dot(counts, table, preferred_element_type=jnp.float32) * (1.0 / L)).astype(
        jnp.bfloat16
    )
    first_inputs = first_inputs.reshape(MICRO, micro_rows, width)
    gain = gains[0]
    blank = jnp.zeros((MICRO, micro_rows, width), jnp.bfloat16)
    saved_inputs = blank
    tops = blank
    received = jnp.zeros((micro_rows, width), jnp.bfloat16)
    forward_offset = jnp.where(spec_section, 0, section_index)
    takes_bag = spec_section | (section_index == 0)
    to_next = shift_pairs("section", [(s, s + 1) for s in range(top_section)])
    for moment in range(MICRO + top_section):
        micro_index = moment - forward_offset
        in_range = (micro_index >= 0) & (micro_index < MICRO)
        clipped = jnp.clip(micro_index, 0, MICRO - 1)
        from_bag = lax.dynamic_index_in_dim(first_inputs, clipped, 0, keepdims=False)
        current = jnp.where(takes_bag, from_bag, received)
        saved_inputs = keep_where(saved_inputs, current, clipped, in_range)
        output = layer_forward(current, layer_weights, gain)
        tops = keep_where(tops, output, clipped, in_range)
        if moment + 1 < MICRO + top_section:
            received = to_next(output)
    proj = jnp.where(spec_section, spec_proj, prog_proj)
    unit, inverse, key = embed_rows(tops.reshape(sample_rows, width), proj)
    swap = shift_pairs("section", [(top_section, last_section), (last_section, top_section)])
    partner_key = swap(key)
    others = gather_rows(partner_key, "blk")
    scores = logit_scale * lax.dot_general(
        key, others, (((1,), (1,)), ((), ())), preferred_element_type=jnp.float32
    )
    row_max = jnp.max(scores, axis=1, keepdims=True)
    lse = row_max + jnp.log(jnp.sum(jnp.exp(scores - row_max), axis=1, keepdims=True))
    lse_down = shift_pairs("section", [(last_section, top_section)])(lse)
    lse_all = gather_rows(lse_down, "blk").reshape(1, -1)
    shift = jnp.where(spec_section, lse, lse_all)
    probs = jnp.exp(scores - shift).astype(jnp.bfloat16)
    dkey = logit_scale * (
        jnp.dot(probs, others, preferred_element_type=jnp.float32)
        - partner_key.astype(jnp.float32)
    )
    top_grad = embed_back(dkey, unit, inverse, proj).reshape(MICRO, micro_rows, width)
    saved_scaled = blank
    saved_dmixed = blank
    starts_grad = section_index >= top_section
    backward_offset = jnp.where(starts_grad, 0, top_section - section_index)
    to_previous = shift_pairs("section", [(s, s - 1) for s in range(1, top_section + 1)])
    incoming = jnp.zeros((micro_rows, width), jnp.bfloat16)
    for moment in range(MICRO + top_section):
        if moment > 0:
            incoming = to_previous(dhidden)
        micro_index = moment - backward_offset
        in_range = (micro_index >= 0) & (micro_index < MICRO)
        clipped = jnp.clip(micro_index, 0, MICRO - 1)
        upstream = jnp.where(
            starts_grad, lax.dynamic_index_in_dim(top_grad, clipped, 0, keepdims=False), incoming
        )
        hidden = lax.dynamic_index_in_dim(saved_inputs, clipped, 0, keepdims=False)
        dhidden, scaled, dmixed = layer_backward(hidden, upstream, layer_weights, gain)
        saved_scaled = keep_where(saved_scaled, scaled, clipped, in_range)
        saved_dmixed = keep_where(saved_dmixed, dmixed, clipped, in_range)
    scaled_all = saved_scaled.reshape(sample_rows, width)
    dmixed_all = saved_dmixed.reshape(sample_rows, width)
    partial = lax.dot_general(
        scaled_all, dmixed_all, (((0,), (0,)), ((), ())), preferred_element_type=jnp.float32
    )
    count = lax.axis_size("blk")
    pieces = partial.astype(jnp.bfloat16).reshape(count, width // count, width)
    landed = lax.all_to_all(pieces, "blk", 0, 0, tiled=True)
    return jnp.sum(landed.astype(jnp.float32), axis=0)


def solution(mesh):
    return jax.shard_map(
        local,
        mesh=mesh,
        in_specs=(
            P("blk", None),
            P("blk", None),
            P(),
            P(),
            P("section", None),
            P("section", None),
            P(),
            P(),
        ),
        out_specs=P(("section", "blk"), None),
        check_vma=False,
    )
```

profile of v0, /device:TPU:1, one launch (start us, length us, event | category | flops | bytes accessed | tf_op | source)
XLA Modules:
  0.0 366.5 jit_solution(1098043385294263811)
XLA Ops:
  0.0 0.9 broadcast_select_fusion.9
  0.9 8.7 %convert_reduce_fusion = bf16[160,384]{1,0:T(8,128)(2,1)S(1)} fusion(s32[160,256]{1,0:T(8,128)S(1)} %broadcast_select_fusion.9), kind=kLoop, calls=%fused_computation | loop fusion | flops 47124480 | bytes 286720 | tf_op jit(solution)/shard_map/reduce_sum | solution.py:85
  9.6 2.1 fusion.26
  11.8 5.3 %fusion.29 = bf16[160,2048]{1,0:T(8,128)(2,1)S(1)} fusion(bf16[2048,2048]{1,0:T(8,128)(2,1)} %param.12, f32[2048]{0:T(1024)S(1)} %bitcast.23, f32[160]{0:T(256)S(1)} %add_rsqrt_fusion.4, bf16[160,2048]{1,0:T(8,128)(2,1)S(1)} %get-tuple-element.12, pred[]{:T(512)S(6)} %or.3), kind=kOutput, calls=%fused_computation.56 | convolution fusion | flops 1346437120 | bytes 9708161 | tf_op jit(solution)/shard_map/dot_general | solution.py:30
  17.2 6.0 %collective-permute-start = (bf16[160,2048]{1,0:T(8,128)(2,1)S(1)}, bf16[160,2048]{1,0:T(8,128)(2,1)S(1)}, u32[]{:S(2)}, u32[]{:S(2)}) collective-permute-start(bf16[160,2048]{1,0:T(8,128)(2,1)S(1)} %fusion.29), channel_id=1, source_target_pairs={{0,32},{32,64},{1,33},{33,65},{2,34},{34,66},{3,35},{35,67},{4,36}... | collective-permute-start | bytes 1966088 | tf_op jit(solution)/shard_map/ppermute | solution.py:15
  23.2 7.5 %collective-permute-done = bf16[160,2048]{1,0:T(8,128)(2,1)S(1)} collective-permute-done((bf16[160,2048]{1,0:T(8,128)(2,1)S(1)}, bf16[160,2048]{1,0:T(8,128)(2,1)S(1)}, u32[]{:S(2)}, u32[]{:S(2)}) %collective-permute-start) | collective-permute-done | bytes 655392 | tf_op jit(solution)/shard_map/ppermute | solution.py:15
  31.1 1.9 fusion.33
  33.0 5.9 %collective-permute-start.1 = (bf16[160,2048]{1,0:T(8,128)(2,1)S(1)}, bf16[160,2048]{1,0:T(8,128)(2,1)S(1)}, u32[]{:S(2)}, u32[]{:S(2)}) collective-permute-start(bf16[160,2048]{1,0:T(8,128)(2,1)S(1)} %fusion.33), channel_id=1, source_target_pairs={{0,32},{32,64},{1,33},{33,65},{2,34},{34,66},{3,35},{35,67},{4,36}... | collective-permute-start | bytes 1966088 | tf_op jit(solution)/shard_map/ppermute | solution.py:15
  38.9 7.5 %collective-permute-done.1 = bf16[160,2048]{1,0:T(8,128)(2,1)S(1)} collective-permute-done((bf16[160,2048]{1,0:T(8,128)(2,1)S(1)}, bf16[160,2048]{1,0:T(8,128)(2,1)S(1)}, u32[]{:S(2)}, u32[]{:S(2)}) %collective-permute-start.1) | collective-permute-done | bytes 655392 | tf_op jit(solution)/shard_map/ppermute | solution.py:15
  46.7 7.0 %multiply_reduce_fusion.1 = (f32[160]{0:T(256)S(1)}, f32[160,768]{1,0:T(8,128)S(1)}) fusion(bf16[2048,768]{1,0:T(8,128)(2,1)} %param.15, bf16[2048,768]{1,0:T(8,128)(2,1)} %param.14, pred[]{:T(512)S(6)} %eq.19, bf16[2048,2048]{1,0:T(8,128)(2,1)} %param.12, bf16[160,2048]{1,0:T(8,128)(2,1)S(1)} %get-tuple-element.6, bf16[160,2048]{1,0:T(8,128)(2,1)} %copy-done.11, ...), kind=kOutput, calls=%fused_computation.98 | convolution fusion | flops 1851899776 | bytes 17147140 | tf_op jit(solution)/shard_map/dot_general | solution.py:57
  54.5 0.7 collective-permute-start.2
  55.2 4.1 %broadcast_in_dim.60 = bf16[32,160,768]{2,1,0:T(8,128)(2,1)} broadcast(bf16[160,768]{1,0:T(8,128)(2,1)S(1)} %collective-permute-done.2), dimensions={1,2} | broadcast | bytes 8110080 | tf_op jit(solution)/shard_map/broadcast_in_dim | solution.py:20
  59.2 8.2 %all-to-all-start = ((bf16[32,160,768]{2,1,0:T(8,128)(2,1)}), bf16[32,160,768]{2,1,0:T(8,128)(2,1)}, u32[]{:S(2)}, u32[]{:S(2)}) async-start(bf16[32,160,768]{2,1,0:T(8,128)(2,1)} %broadcast_in_dim.60), calls=%async_computation | async-start | bytes 15728640 | tf_op jit(solution)/shard_map/all_to_all | solution.py:21
  67.4 1.3 fusion.19
  68.8 98.1 %all-to-all-done = bf16[32,160,768]{2,1,0:T(8,128)(2,1)} async-done(((bf16[32,160,768]{2,1,0:T(8,128)(2,1)}), bf16[32,160,768]{2,1,0:T(8,128)(2,1)}, u32[]{:S(2)}, u32[]{:S(2)}) %all-to-all-start) | async-done | bytes 7864352 | tf_op jit(solution)/shard_map/all_to_all | solution.py:21
  166.8 6.0 %fusion.92 = (f32[160]{0:T(256)S(1)}, f32[160,5120]{1,0:T(8,128)S(1)}) fusion(bf16[160,768]{1,0:T(8,128)(2,1)S(1)} %multiply_convert_fusion.3, bf16[5120,768]{1,0:T(8,128)(2,1)} %bitcast.1), kind=kOutput, calls=%fused_computation.121 | convolution fusion | flops 1259929472 | bytes 11387520 | tf_op jit(solution)/shard_map/dot_general | solution.py:119
  173.5 0.7 collective-permute-start.3
  175.4 6.9 %all-to-all-start.1 = ((f32[32,160,1]{1,2,0:T(1,128)}), f32[32,160,1]{1,2,0:T(1,128)S(1)}, u32[]{:S(2)}, u32[]{:S(2)}) async-start(f32[32,160,1]{1,2,0:T(1,128)} %broadcast_in_dim.63), calls=%async_computation.1 | async-start | bytes 65536 | tf_op jit(solution)/shard_map/all_to_all | solution.py:21
  182.3 6.4 %fusion.77 = f32[160,2048]{1,0:T(8,128)} fusion(bf16[2048,2048]{1,0:T(8,128)(2,1)} %param.12, bf16[160,2048]{1,0:T(8,128)(2,1)} %get-tuple-element.8, f32[160]{0:T(256)} %add_rsqrt_fusion.2, f32[2048]{0:T(1024)} %bitcast.22), kind=kOutput, calls=%fused_computation.105 | convolution fusion | flops 1343488000 | bytes 10363520 | tf_op jit(solution)/shard_map/dot_general | solution.py:30
  189.3 0.7 reduce
  190.0 0.8 broadcast_in_dim.64
  190.9 5.1 %multiply_reduce_fusion = (f32[160]{0:T(256)S(1)}, f32[160,768]{1,0:T(8,128)S(1)}) fusion(f32[160,768]{1,0:T(8,128)} %copy-done.1, f32[160]{0:T(256)} %copy-done.6, bf16[160,768]{1,0:T(8,128)(2,1)S(1)} %copy-done.4, bf16[5120,768]{1,0:T(8,128)(2,1)} %bitcast.1, f32[160,5120]{1,0:T(8,128)S(1)} %get-tuple-element.16, f32[5120]{0:T(1024)S(1)} %broadcast_in_dim.64, ...), kind=kOutput, calls=%fused_computation.97 | convolution fusion | flops 1261485952 | bytes 12392321 | tf_op jit(solution)/shard_map/dot_general | solution.py:129
  196.3 1.3 convolution_convert_fusion.1
  197.8 6.8 %fusion.13 = (f32[160]{0:T(256)S(1)}, f32[160,2048]{1,0:T(8,128)S(1)}) fusion(bf16[160,2048]{1,0:T(8,128)(2,1)S(1)} %copy-done, f32[160]{0:T(256)S(1)} %copy-done.5, f32[2048]{0:T(1024)S(1)} %bitcast.26, bf16[2048,2048]{1,0:T(8,128)(2,1)} %param.12, f32[160,2048]{1,0:T(8,128)S(1)} %copy-done.14, bf16[160,2048]{1,0:T(8,128)(2,1)S(1)} %convolution_convert_fusion.1, ...), kind=kOutput, calls=%fused_computation.40 | convolution fusion | flops 1347420032 | bytes 12330241 | tf_op jit(solution)/shard_map/dot_general | solution.py:45
  205.0 1.9 collective-permute-start.4
  207.0 42.6 %collective-permute-done.4 = bf16[160,2048]{1,0:T(8,128)(2,1)S(1)} collective-permute-done((bf16[160,2048]{1,0:T(8,128)(2,1)S(1)}, bf16[160,2048]{1,0:T(8,128)(2,1)S(1)}, u32[]{:S(2)}, u32[]{:S(2)}) %collective-permute-start.4) | collective-permute-done | bytes 655392 | tf_op jit(solution)/shard_map/ppermute | solution.py:15
  249.6 3.1 fusion.16
  253.1 2.1 collective-permute-start.5
  255.3 18.6 %collective-permute-done.5 = bf16[160,2048]{1,0:T(8,128)(2,1)S(1)} collective-permute-done((bf16[160,2048]{1,0:T(8,128)(2,1)S(1)}, bf16[160,2048]{1,0:T(8,128)(2,1)S(1)}, u32[]{:S(2)}, u32[]{:S(2)}) %collective-permute-start.5) | collective-permute-done | bytes 655392 | tf_op jit(solution)/shard_map/ppermute | solution.py:15
  273.9 4.1 %convolution_convert_fusion = bf16[2048,2048]{1,0:T(8,128)(2,1)S(1)} fusion(f32[160,2048]{1,0:T(8,128)} %fusion.77, bf16[160,2048]{1,0:T(8,128)(2,1)S(1)} %convolution_convert_fusion.1, bf16[160,2048]{1,0:T(8,128)(2,1)S(1)} %collective-permute-done.5, pred[]{:T(512)S(6)} %ge.21, pred[]{:T(512)S(6)} %and.24, pred[]{:T(512)S(6)} %and.23, pred[]{:T(512)S(6)} %and.19, ...), kind=kOutput, calls=%fused_computation.3 | convolution fusion | flops 1356529664 | bytes 12329604 | tf_op jit(solution)/shard_map/dot_general | solution.py:154
  278.0 85.6 %all_to_all.15 = bf16[32,64,2048]{2,1,0:T(8,128)(2,1)S(1)} all-to-all(bf16[32,64,2048]{2,1,0:T(8,128)(2,1)S(1)} %bitcast.15), channel_id=1, replica_groups=mesh['section'=4,'blk'=32] {'blk'}, dimensions={0} | all-to-all | bytes 16777216 | tf_op jit(solution)/shard_map/all_to_all | solution.py:159
  363.6 2.9 convert_reduce_fusion.1
  (58 shorter events, 5.2 us)
Async XLA Ops:
  9.6 2.1 copy-start.12
  11.8 19.3 %slice-start = ((s8[8388608]{0:T(1024)(128)(4,1)}), s8[4194304]{0:T(1024)(128)(4,1)S(1)}, s32[]{:S(2)}) async-start(s8[8388608]{0:T(1024)(128)(4,1)} %bitcast.18), calls=%async_computation.3 | async-start | bytes 8388608
  11.8 19.2 %slice-start.1 = ((s8[8388608]{0:T(1024)(128)(4,1)}), s8[4194304]{0:T(1024)(128)(4,1)S(1)}, s32[]{:S(2)}) async-start(s8[8388608]{0:T(1024)(128)(4,1)} %bitcast.18), calls=%async_computation.4 | async-start | bytes 8388608
  17.2 13.5 %collective-permute-start = (bf16[160,2048]{1,0:T(8,128)(2,1)S(1)}, bf16[160,2048]{1,0:T(8,128)(2,1)S(1)}, u32[]{:S(2)}, u32[]{:S(2)}) collective-permute-start(bf16[160,2048]{1,0:T(8,128)(2,1)S(1)} %fusion.29), channel_id=1, source_target_pairs={{0,32},{32,64},{1,33},{33,65},{2,34},{34,66},{3,35},{35,67},{4,36}... | collective-permute-start | bytes 1966088 | tf_op jit(solution)/shard_map/ppermute | solution.py:15
  33.0 5.9 %copy-start.11 = (bf16[160,2048]{1,0:T(8,128)(2,1)}, bf16[160,2048]{1,0:T(8,128)(2,1)S(1)}, u32[]{:S(2)}) copy-start(bf16[160,2048]{1,0:T(8,128)(2,1)S(1)} %fusion.33) | copy-start | bytes 1966084
  33.0 13.4 %collective-permute-start.1 = (bf16[160,2048]{1,0:T(8,128)(2,1)S(1)}, bf16[160,2048]{1,0:T(8,128)(2,1)S(1)}, u32[]{:S(2)}, u32[]{:S(2)}) collective-permute-start(bf16[160,2048]{1,0:T(8,128)(2,1)S(1)} %fusion.33), channel_id=1, source_target_pairs={{0,32},{32,64},{1,33},{33,65},{2,34},{34,66},{3,35},{35,67},{4,36}... | collective-permute-start | bytes 1966088 | tf_op jit(solution)/shard_map/ppermute | solution.py:15
  53.7 5.5 %copy-start.1 = (f32[160,768]{1,0:T(8,128)}, f32[160,768]{1,0:T(8,128)S(1)}, u32[]{:S(2)}) copy-start(f32[160,768]{1,0:T(8,128)S(1)} %get-tuple-element.14) | copy-start | bytes 1474564
  53.7 0.6 copy-start.6
  54.5 0.7 collective-permute-start.2
  55.2 4.1 %copy-start.3 = (bf16[160,768]{1,0:T(8,128)(2,1)}, bf16[160,768]{1,0:T(8,128)(2,1)S(1)}, u32[]{:S(2)}) copy-start(bf16[160,768]{1,0:T(8,128)(2,1)S(1)} %collective-permute-done.2) | copy-start | bytes 737284
  59.2 107.6 %all-to-all-start = ((bf16[32,160,768]{2,1,0:T(8,128)(2,1)}), bf16[32,160,768]{2,1,0:T(8,128)(2,1)}, u32[]{:S(2)}, u32[]{:S(2)}) async-start(bf16[32,160,768]{2,1,0:T(8,128)(2,1)} %broadcast_in_dim.60), calls=%async_computation | async-start | bytes 15728640 | tf_op jit(solution)/shard_map/all_to_all | solution.py:21
  173.5 8.8 %copy-start.8 = (f32[160]{0:T(256)}, f32[160]{0:T(256)S(1)}, u32[]{:S(2)}) copy-start(f32[160]{0:T(256)S(1)} %log_add_fusion) | copy-start | bytes 1924
  173.5 1.3 collective-permute-start.3
  175.4 13.9 %all-to-all-start.1 = ((f32[32,160,1]{1,2,0:T(1,128)}), f32[32,160,1]{1,2,0:T(1,128)S(1)}, u32[]{:S(2)}, u32[]{:S(2)}) async-start(f32[32,160,1]{1,2,0:T(1,128)} %broadcast_in_dim.63), calls=%async_computation.1 | async-start | bytes 65536 | tf_op jit(solution)/shard_map/all_to_all | solution.py:21
  182.3 8.6 %copy-start.4 = (bf16[160,768]{1,0:T(8,128)(2,1)S(1)}, bf16[160,768]{1,0:T(8,128)(2,1)}, u32[]{:S(2)}) copy-start(bf16[160,768]{1,0:T(8,128)(2,1)} %copy-done.3) | copy-start | bytes 737284
  190.8 5.2 %copy-start.2 = (f32[160,768]{1,0:T(8,128)S(1)}, f32[160,768]{1,0:T(8,128)}, u32[]{:S(2)}) copy-start(f32[160,768]{1,0:T(8,128)} %copy-done.1) | copy-start | bytes 1474564
  190.8 5.2 %copy-start.7 = (f32[160]{0:T(256)S(1)}, f32[160]{0:T(256)}, u32[]{:S(2)}) copy-start(f32[160]{0:T(256)} %copy-done.6) | copy-start | bytes 1924
  190.8 5.2 %copy-start.9 = (bf16[2048,768]{1,0:T(8,128)(2,1)S(1)}, bf16[2048,768]{1,0:T(8,128)(2,1)}, u32[]{:S(2)}) copy-start(bf16[2048,768]{1,0:T(8,128)(2,1)} %param.15) | copy-start | bytes 9437188
  190.9 5.4 %copy-start.10 = (bf16[2048,768]{1,0:T(8,128)(2,1)S(1)}, bf16[2048,768]{1,0:T(8,128)(2,1)}, u32[]{:S(2)}) copy-start(bf16[2048,768]{1,0:T(8,128)(2,1)} %param.14) | copy-start | bytes 9437188
  196.2 1.3 copy-start
  196.2 1.3 copy-start.5
  196.2 1.3 copy-start.13
  196.2 1.5 copy-start.14
  196.2 53.3 %slice-start.2 = ((s8[8388608]{0:T(1024)(128)(4,1)}), s8[4194304]{0:T(1024)(128)(4,1)S(1)}, s32[]{:S(2)}) async-start(s8[8388608]{0:T(1024)(128)(4,1)} %bitcast.20), calls=%async_computation.5 | async-start | bytes 8388608
  197.8 51.8 %slice-start.3 = ((s8[8388608]{0:T(1024)(128)(4,1)}), s8[4194304]{0:T(1024)(128)(4,1)S(1)}, s32[]{:S(2)}) async-start(s8[8388608]{0:T(1024)(128)(4,1)} %bitcast.20), calls=%async_computation.6 | async-start | bytes 8388608
  205.0 44.5 %collective-permute-start.4 = (bf16[160,2048]{1,0:T(8,128)(2,1)S(1)}, bf16[160,2048]{1,0:T(8,128)(2,1)S(1)}, u32[]{:S(2)}, u32[]{:S(2)}) collective-permute-start(bf16[160,2048]{1,0:T(8,128)(2,1)S(1)} %fusion.22), channel_id=1, source_target_pairs={{32,0},{64,32},{33,1},{65,33},{34,2},{66,34},{35,3},{67,35},{36,4}... | collective-permute-start | bytes 1966088 | tf_op jit(solution)/shard_map/ppermute | solution.py:15
  253.1 20.7 %collective-permute-start.5 = (bf16[160,2048]{1,0:T(8,128)(2,1)S(1)}, bf16[160,2048]{1,0:T(8,128)(2,1)S(1)}, u32[]{:S(2)}, u32[]{:S(2)}) collective-permute-start(bf16[160,2048]{1,0:T(8,128)(2,1)S(1)} %fusion.25), channel_id=1, source_target_pairs={{32,0},{64,32},{33,1},{65,33},{34,2},{66,34},{35,3},{67,35},{36,4}... | collective-permute-start | bytes 1966088 | tf_op jit(solution)/shard_map/ppermute | solution.py:15
where the time goes:
time: 367 us
  waiting for transfers between devices  175 us (48%)
  blocking collectives  85.6 us (23%)
  matrix products  49.2 us (13%)
  starting transfers between devices  32.4 us (9%)
  other arithmetic  17.4 us (5%)
  local copies, waits for them, and re-layouts  6.62 us (2%)
    all_to_all x2, waiting for transfers between devices, gather_rows(): got = lax.all_to_all(spread, axis, 0, 0, tiled=True)  98.7 us
    all_to_all x1, blocking collectives, local(): landed = lax.all_to_all(pieces, 'blk', 0, 0, tiled=True)  85.6 us
    ppermute x6, waiting for transfers between devices, shift_pairs(): return lambda value: lax.ppermute(value, axis, pairs)  76.2 us
    ppermute x6, starting transfers between devices, shift_pairs(): return lambda value: lax.ppermute(value, axis, pairs)  17.3 us
    all_to_all x2, starting transfers between devices, gather_rows(): got = lax.all_to_all(spread, axis, 0, 0, tiled=True)  15.1 us
    dot_general x3, matrix products, layer_parts(): mixed = jnp.dot(scaled, weight, preferred_element_type=jnp.float32)  13.6 us
    dot_general x2, matrix products, layer_backward(): lax.dot_general(dmixed, weight, (((1,), (1,)), ((), ())), preferred_eleme...  9.94 us
    reduce_sum x1, other arithmetic, local(): jnp.sum((token_ids[:, :, None] == vocab_iota[None, None, :]).astype(jnp.f...  8.68 us
  transfers between devices with their start and end apart: 8, of which 6 were waited for; matrix products, arithmetic and copies ran while one was open for 2% of the time, Pallas kernels for 0%

commit v1 on v0

--- a/solution.py
+++ b/solution.py
@@ -99,7 +99,6 @@
     received = jnp.zeros((micro_rows, width), jnp.bfloat16)
     forward_offset = jnp.where(spec_section, 0, section_index)
     takes_bag = spec_section | (section_index == 0)
-    to_next = shift_pairs("section", [(s, s + 1) for s in range(top_section)])
     for moment in range(MICRO + top_section):
         micro_index = moment - forward_offset
         in_range = (micro_index >= 0) & (micro_index < MICRO)
@@ -109,8 +108,9 @@
         saved_inputs = keep_where(saved_inputs, current, clipped, in_range)
         output = layer_forward(current, layer_weights, gain)
         tops = keep_where(tops, output, clipped, in_range)
-        if moment + 1 < MICRO + top_section:
-            received = to_next(output)
+        senders = [s for s in range(top_section) if 0 <= moment - s < MICRO]
+        if senders:
+            received = shift_pairs("section", [(s, s + 1) for s in senders])(output)
     proj = jnp.where(spec_section, spec_proj, prog_proj)
     unit, inverse, key = embed_rows(tops.reshape(sample_rows, width), proj)
     swap = shift_pairs("section", [(top_section, last_section), (last_section, top_section)])
@@ -134,11 +134,12 @@
     saved_dmixed = blank
     starts_grad = section_index >= top_section
     backward_offset = jnp.where(starts_grad, 0, top_section - section_index)
-    to_previous = shift_pairs("section", [(s, s - 1) for s in range(1, top_section + 1)])
     incoming = jnp.zeros((micro_rows, width), jnp.bfloat16)
     for moment in range(MICRO + top_section):
-        if moment > 0:
-            incoming = to_previous(dhidden)
+        done = moment - 1
+        senders = [s for s in range(1, top_section + 1) if 0 <= done - (top_section - s) < MICRO]
+        if senders:
+            incoming = shift_pairs("section", [(s, s - 1) for s in senders])(dhidden)
         micro_index = moment - backward_offset
         in_range = (micro_index >= 0) & (micro_index < MICRO)
         clipped = jnp.clip(micro_index, 0, MICRO - 1)

time: 367 us -> 351 us (0.956)
  the two profiles are of different devices: /device:TPU:1 before, /device:TPU:8 now
where the time goes in v1:
time: 351 us
  waiting for transfers between devices  150 us (43%)
  blocking collectives  102 us (29%)
  matrix products  49 us (14%)
  starting transfers between devices  24.9 us (7%)
  other arithmetic  17.4 us (5%)
  local copies, waits for them, and re-layouts  6.71 us (2%)
    all_to_all x2, waiting for transfers between devices, gather_rows(): got = lax.all_to_all(spread, axis, 0, 0, tiled=True)  103 us
    all_to_all x1, blocking collectives, local(): landed = lax.all_to_all(pieces, 'blk', 0, 0, tiled=True)  102 us
    ppermute x6, waiting for transfers between devices, shift_pairs(): return lambda value: lax.ppermute(value, axis, pairs)  47.3 us
    all_to_all x2, starting transfers between devices, gather_rows(): got = lax.all_to_all(spread, axis, 0, 0, tiled=True)  18.8 us
    dot_general x3, matrix products, layer_parts(): mixed = jnp.dot(scaled, weight, preferred_element_type=jnp.float32)  13.6 us
    dot_general x2, matrix products, layer_backward(): lax.dot_general(dmixed, weight, (((1,), (1,)), ((), ())), preferred_eleme...  9.94 us
    reduce_sum x1, other arithmetic, local(): jnp.sum((token_ids[:, :, None] == vocab_iota[None, None, :]).astype(jnp.f...  8.68 us
  transfers between devices with their start and end apart: 8, of which 4 were waited for; matrix products, arithmetic and copies ran while one was open for 2% of the time, Pallas kernels for 0%

profile of v1, /device:TPU:8, one launch (start us, length us, event | category | flops | bytes accessed | tf_op | source)
XLA Modules:
  0.0 350.7 jit_solution(15593873193570278397)
XLA Ops:
  0.0 0.9 broadcast_select_fusion.9
  0.9 8.7 %convert_reduce_fusion = bf16[160,384]{1,0:T(8,128)(2,1)S(1)} fusion(s32[160,256]{1,0:T(8,128)S(1)} %broadcast_select_fusion.9), kind=kLoop, calls=%fused_computation | loop fusion | flops 47124480 | bytes 286720 | tf_op jit(solution)/shard_map/reduce_sum | solution.py:85
  9.6 2.1 fusion.26
  11.8 5.4 %fusion.29 = bf16[160,2048]{1,0:T(8,128)(2,1)S(1)} fusion(bf16[2048,2048]{1,0:T(8,128)(2,1)} %param.12, f32[2048]{0:T(1024)S(1)} %bitcast.23, f32[160]{0:T(256)S(1)} %add_rsqrt_fusion.4, bf16[160,2048]{1,0:T(8,128)(2,1)S(1)} %get-tuple-element.12, pred[]{:T(512)S(6)} %or.3), kind=kOutput, calls=%fused_computation.56 | convolution fusion | flops 1346437120 | bytes 9708161 | tf_op jit(solution)/shard_map/dot_general | solution.py:30
  17.2 1.8 collective-permute-start
  18.9 1.7 collective-permute-done
  21.0 1.9 fusion.33
  22.9 0.7 collective-permute-start.1
  24.0 6.8 %multiply_reduce_fusion.1 = (f32[160]{0:T(256)S(1)}, f32[160,768]{1,0:T(8,128)S(1)}) fusion(bf16[2048,768]{1,0:T(8,128)(2,1)} %param.15, bf16[2048,768]{1,0:T(8,128)(2,1)} %param.14, pred[]{:T(512)S(6)} %eq.19, bf16[2048,2048]{1,0:T(8,128)(2,1)} %param.12, bf16[160,2048]{1,0:T(8,128)(2,1)S(1)} %get-tuple-element.6, bf16[160,2048]{1,0:T(8,128)(2,1)} %copy-done.11, ...), kind=kOutput, calls=%fused_computation.98 | convolution fusion | flops 1851899776 | bytes 17147140 | tf_op jit(solution)/shard_map/dot_general | solution.py:57
  31.6 0.7 collective-permute-start.2
  32.3 4.1 %broadcast_in_dim.60 = bf16[32,160,768]{2,1,0:T(8,128)(2,1)} broadcast(bf16[160,768]{1,0:T(8,128)(2,1)S(1)} %collective-permute-done.2), dimensions={1,2} | broadcast | bytes 8110080 | tf_op jit(solution)/shard_map/broadcast_in_dim | solution.py:20
  36.4 9.5 %all-to-all-start = ((bf16[32,160,768]{2,1,0:T(8,128)(2,1)}), bf16[32,160,768]{2,1,0:T(8,128)(2,1)}, u32[]{:S(2)}, u32[]{:S(2)}) async-start(bf16[32,160,768]{2,1,0:T(8,128)(2,1)} %broadcast_in_dim.60), calls=%async_computation | async-start | bytes 15728640 | tf_op jit(solution)/shard_map/all_to_all | solution.py:21
  45.9 1.3 fusion.19
  47.2 102.2 %all-to-all-done = bf16[32,160,768]{2,1,0:T(8,128)(2,1)} async-done(((bf16[32,160,768]{2,1,0:T(8,128)(2,1)}), bf16[32,160,768]{2,1,0:T(8,128)(2,1)}, u32[]{:S(2)}, u32[]{:S(2)}) %all-to-all-start) | async-done | bytes 7864352 | tf_op jit(solution)/shard_map/all_to_all | solution.py:21
  149.4 6.0 %fusion.92 = (f32[160]{0:T(256)S(1)}, f32[160,5120]{1,0:T(8,128)S(1)}) fusion(bf16[160,768]{1,0:T(8,128)(2,1)S(1)} %multiply_convert_fusion.3, bf16[5120,768]{1,0:T(8,128)(2,1)} %bitcast.1), kind=kOutput, calls=%fused_computation.121 | convolution fusion | flops 1259929472 | bytes 11387520 | tf_op jit(solution)/shard_map/dot_general | solution.py:119
  156.1 0.7 collective-permute-start.3
  157.3 0.6 broadcast_in_dim.63
  157.9 9.3 %all-to-all-start.1 = ((f32[32,160,1]{1,2,0:T(1,128)}), f32[32,160,1]{1,2,0:T(1,128)S(1)}, u32[]{:S(2)}, u32[]{:S(2)}) async-start(f32[32,160,1]{1,2,0:T(1,128)} %broadcast_in_dim.63), calls=%async_computation.1 | async-start | bytes 65536 | tf_op jit(solution)/shard_map/all_to_all | solution.py:21
  167.3 6.4 %fusion.77 = f32[160,2048]{1,0:T(8,128)} fusion(bf16[2048,2048]{1,0:T(8,128)(2,1)} %param.12, bf16[160,2048]{1,0:T(8,128)(2,1)} %get-tuple-element.8, f32[160]{0:T(256)} %add_rsqrt_fusion.2, f32[2048]{0:T(1024)} %bitcast.22), kind=kOutput, calls=%fused_computation.105 | convolution fusion | flops 1343488000 | bytes 10363520 | tf_op jit(solution)/shard_map/dot_general | solution.py:30
  173.7 0.8 all-to-all-done.1
  174.4 0.7 reduce
  175.1 0.8 broadcast_in_dim.64
  176.0 5.1 %multiply_reduce_fusion = (f32[160]{0:T(256)S(1)}, f32[160,768]{1,0:T(8,128)S(1)}) fusion(f32[160,768]{1,0:T(8,128)} %copy-done.1, f32[160]{0:T(256)} %copy-done.6, bf16[160,768]{1,0:T(8,128)(2,1)S(1)} %copy-done.4, bf16[5120,768]{1,0:T(8,128)(2,1)} %bitcast.1, f32[160,5120]{1,0:T(8,128)S(1)} %get-tuple-element.16, f32[5120]{0:T(1024)S(1)} %broadcast_in_dim.64, ...), kind=kOutput, calls=%fused_computation.97 | convolution fusion | flops 1261485952 | bytes 12392321 | tf_op jit(solution)/shard_map/dot_general | solution.py:129
  181.4 1.3 convolution_convert_fusion.1
  182.9 6.8 %fusion.13 = (f32[160]{0:T(256)S(1)}, f32[160,2048]{1,0:T(8,128)S(1)}) fusion(bf16[160,2048]{1,0:T(8,128)(2,1)S(1)} %copy-done, f32[160]{0:T(256)S(1)} %copy-done.5, f32[2048]{0:T(1024)S(1)} %bitcast.26, bf16[2048,2048]{1,0:T(8,128)(2,1)} %param.12, f32[160,2048]{1,0:T(8,128)S(1)} %copy-done.14, bf16[160,2048]{1,0:T(8,128)(2,1)S(1)} %convolution_convert_fusion.1, ...), kind=kOutput, calls=%fused_computation.40 | convolution fusion | flops 1347420032 | bytes 12330241 | tf_op jit(solution)/shard_map/dot_general | solution.py:45
  190.2 0.7 collective-permute-start.4
  190.9 3.1 fusion.16
  194.5 1.5 collective-permute-start.5
  196.0 45.6 %collective-permute-done.5 = bf16[160,2048]{1,0:T(8,128)(2,1)S(1)} collective-permute-done((bf16[160,2048]{1,0:T(8,128)(2,1)S(1)}, bf16[160,2048]{1,0:T(8,128)(2,1)S(1)}, u32[]{:S(2)}, u32[]{:S(2)}) %collective-permute-start.5) | collective-permute-done | bytes 655392 | tf_op jit(solution)/shard_map/ppermute | solution.py:15
  241.7 4.1 %convolution_convert_fusion = bf16[2048,2048]{1,0:T(8,128)(2,1)S(1)} fusion(f32[160,2048]{1,0:T(8,128)} %fusion.77, bf16[160,2048]{1,0:T(8,128)(2,1)S(1)} %convolution_convert_fusion.1, bf16[160,2048]{1,0:T(8,128)(2,1)S(1)} %collective-permute-done.5, pred[]{:T(512)S(6)} %ge.21, pred[]{:T(512)S(6)} %and.24, pred[]{:T(512)S(6)} %and.23, pred[]{:T(512)S(6)} %and.19, ...), kind=kOutput, calls=%fused_computation.3 | convolution fusion | flops 1356529664 | bytes 12329604 | tf_op jit(solution)/shard_map/dot_general | solution.py:155
  245.7 102.0 %all_to_all.15 = bf16[32,64,2048]{2,1,0:T(8,128)(2,1)S(1)} all-to-all(bf16[32,64,2048]{2,1,0:T(8,128)(2,1)S(1)} %bitcast.15), channel_id=1, replica_groups=mesh['section'=4,'blk'=32] {'blk'}, dimensions={0} | all-to-all | bytes 16777216 | tf_op jit(solution)/shard_map/all_to_all | solution.py:160
  347.8 2.9 convert_reduce_fusion.1
  (58 shorter events, 4.0 us)
Async XLA Ops:
  9.6 2.2 copy-start.12
  11.8 9.2 %slice-start = ((s8[8388608]{0:T(1024)(128)(4,1)}), s8[4194304]{0:T(1024)(128)(4,1)S(1)}, s32[]{:S(2)}) async-start(s8[8388608]{0:T(1024)(128)(4,1)} %bitcast.18), calls=%async_computation.3 | async-start | bytes 8388608
  11.8 9.2 %slice-start.1 = ((s8[8388608]{0:T(1024)(128)(4,1)}), s8[4194304]{0:T(1024)(128)(4,1)S(1)}, s32[]{:S(2)}) async-start(s8[8388608]{0:T(1024)(128)(4,1)} %bitcast.18), calls=%async_computation.4 | async-start | bytes 8388608
  17.2 3.4 collective-permute-start
  22.9 0.8 copy-start.11
  22.9 0.8 collective-permute-start.1
  30.9 5.5 %copy-start.1 = (f32[160,768]{1,0:T(8,128)}, f32[160,768]{1,0:T(8,128)S(1)}, u32[]{:S(2)}) copy-start(f32[160,768]{1,0:T(8,128)S(1)} %get-tuple-element.14) | copy-start | bytes 1474564
  30.9 0.6 copy-start.6
  31.6 0.7 collective-permute-start.2
  32.3 4.1 %copy-start.3 = (bf16[160,768]{1,0:T(8,128)(2,1)}, bf16[160,768]{1,0:T(8,128)(2,1)S(1)}, u32[]{:S(2)}) copy-start(bf16[160,768]{1,0:T(8,128)(2,1)S(1)} %collective-permute-done.2) | copy-start | bytes 737284
  36.4 113.0 %all-to-all-start = ((bf16[32,160,768]{2,1,0:T(8,128)(2,1)}), bf16[32,160,768]{2,1,0:T(8,128)(2,1)}, u32[]{:S(2)}, u32[]{:S(2)}) async-start(bf16[32,160,768]{2,1,0:T(8,128)(2,1)} %broadcast_in_dim.60), calls=%async_computation | async-start | bytes 15728640 | tf_op jit(solution)/shard_map/all_to_all | solution.py:21
  156.1 11.2 %copy-start.8 = (f32[160]{0:T(256)}, f32[160]{0:T(256)S(1)}, u32[]{:S(2)}) copy-start(f32[160]{0:T(256)S(1)} %log_add_fusion) | copy-start | bytes 1924
  156.1 1.3 collective-permute-start.3
  157.9 16.5 %all-to-all-start.1 = ((f32[32,160,1]{1,2,0:T(1,128)}), f32[32,160,1]{1,2,0:T(1,128)S(1)}, u32[]{:S(2)}, u32[]{:S(2)}) async-start(f32[32,160,1]{1,2,0:T(1,128)} %broadcast_in_dim.63), calls=%async_computation.1 | async-start | bytes 65536 | tf_op jit(solution)/shard_map/all_to_all | solution.py:21
  167.3 8.7 %copy-start.4 = (bf16[160,768]{1,0:T(8,128)(2,1)S(1)}, bf16[160,768]{1,0:T(8,128)(2,1)}, u32[]{:S(2)}) copy-start(bf16[160,768]{1,0:T(8,128)(2,1)} %copy-done.3) | copy-start | bytes 737284
  176.0 5.2 %copy-start.2 = (f32[160,768]{1,0:T(8,128)S(1)}, f32[160,768]{1,0:T(8,128)}, u32[]{:S(2)}) copy-start(f32[160,768]{1,0:T(8,128)} %copy-done.1) | copy-start | bytes 1474564
  176.0 5.2 %copy-start.7 = (f32[160]{0:T(256)S(1)}, f32[160]{0:T(256)}, u32[]{:S(2)}) copy-start(f32[160]{0:T(256)} %copy-done.6) | copy-start | bytes 1924
  176.0 5.2 %copy-start.9 = (bf16[2048,768]{1,0:T(8,128)(2,1)S(1)}, bf16[2048,768]{1,0:T(8,128)(2,1)}, u32[]{:S(2)}) copy-start(bf16[2048,768]{1,0:T(8,128)(2,1)} %param.15) | copy-start | bytes 9437188
  176.0 5.4 %copy-start.10 = (bf16[2048,768]{1,0:T(8,128)(2,1)S(1)}, bf16[2048,768]{1,0:T(8,128)(2,1)}, u32[]{:S(2)}) copy-start(bf16[2048,768]{1,0:T(8,128)(2,1)} %param.14) | copy-start | bytes 9437188
  181.4 1.3 copy-start
  181.4 1.3 copy-start.5
  181.4 1.3 copy-start.13
  181.4 1.5 copy-start.14
  181.4 9.5 %slice-start.2 = ((s8[8388608]{0:T(1024)(128)(4,1)}), s8[4194304]{0:T(1024)(128)(4,1)S(1)}, s32[]{:S(2)}) async-start(s8[8388608]{0:T(1024)(128)(4,1)} %bitcast.20), calls=%async_computation.5 | async-start | bytes 8388608
  182.9 8.0 %slice-start.3 = ((s8[8388608]{0:T(1024)(128)(4,1)}), s8[4194304]{0:T(1024)(128)(4,1)S(1)}, s32[]{:S(2)}) async-start(s8[8388608]{0:T(1024)(128)(4,1)} %bitcast.20), calls=%async_computation.6 | async-start | bytes 8388608
  190.2 0.7 collective-permute-start.4
  194.5 47.2 %collective-permute-start.5 = (bf16[160,2048]{1,0:T(8,128)(2,1)S(1)}, bf16[160,2048]{1,0:T(8,128)(2,1)S(1)}, u32[]{:S(2)}, u32[]{:S(2)}) collective-permute-start(bf16[160,2048]{1,0:T(8,128)(2,1)S(1)} %fusion.25), channel_id=1, source_target_pairs={{32,0},{33,1},{34,2},{35,3},{36,4},{37,5},{38,6},{39,7},{40,8},{41... | collective-permute-start | bytes 1966088 | tf_op jit(solution)/shard_map/ppermute | solution.py:15

commit v2 on v1

--- a/solution.py
+++ b/solution.py
@@ -5,6 +5,7 @@
 
 L = 256
 MICRO = 1
+DIGIT = 32
 
 
 logit_scale = 30.0
@@ -81,10 +82,15 @@
     spec_section = section_index == last_section
     token_ids = jnp.where(spec_section, spec_ids, prog_ids)
     table = jnp.where(spec_section, spec_table, prog_table)
-    vocab_iota = jnp.arange(table.shape[0], dtype=jnp.int32)
-    counts = jnp.sum(
-        (token_ids[:, :, None] == vocab_iota[None, None, :]).astype(jnp.float32), axis=1
-    ).astype(jnp.bfloat16)
+    vocab = table.shape[0]
+    high = (token_ids // DIGIT)[:, :, None] == jnp.arange(vocab // DIGIT, dtype=jnp.int32)
+    low = (token_ids % DIGIT)[:, :, None] == jnp.arange(DIGIT, dtype=jnp.int32)
+    counts = jnp.einsum(
+        "bth,btl->bhl",
+        high.astype(jnp.bfloat16),
+        low.astype(jnp.bfloat16),
+        preferred_element_type=jnp.float32,
+    ).reshape(token_ids.shape[0], vocab).astype(jnp.bfloat16)
     sample_rows = prog_ids.shape[0]
     micro_rows = sample_rows // MICRO
     width = layer_weights.shape[1]

time: 351 us -> 344 us (0.980)
  other arithmetic: 17.4 us -> 8.84 us
    reduce_sum x1 -> x0, other arithmetic: 8.68 us -> none  [local(): jnp.sum((token_ids[:, :, None] == vocab_iota[None, None, :]).astype(jnp.f...]
where the time goes in v2:
time: 344 us
  waiting for transfers between devices  150 us (44%)
  blocking collectives  102 us (30%)
  matrix products  50.2 us (15%)
  starting transfers between devices  24.8 us (7%)
  other arithmetic  8.84 us (3%)
  local copies, waits for them, and re-layouts  7.18 us (2%)
    all_to_all x2, waiting for transfers between devices, gather_rows(): got = lax.all_to_all(spread, axis, 0, 0, tiled=True)  103 us
    all_to_all x1, blocking collectives, local(): landed = lax.all_to_all(pieces, 'blk', 0, 0, tiled=True)  102 us
    ppermute x6, waiting for transfers between devices, shift_pairs(): return lambda value: lax.ppermute(value, axis, pairs)  47.3 us
    all_to_all x2, starting transfers between devices, gather_rows(): got = lax.all_to_all(spread, axis, 0, 0, tiled=True)  18.8 us
    dot_general x3, matrix products, layer_parts(): mixed = jnp.dot(scaled, weight, preferred_element_type=jnp.float32)  13.6 us
    dot_general x2, matrix products, layer_backward(): lax.dot_general(dmixed, weight, (((1,), (1,)), ((), ())), preferred_eleme...  9.94 us
  transfers between devices with their start and end apart: 8, of which 4 were waited for; matrix products, arithmetic and copies ran while one was open for 2% of the time, Pallas kernels for 0%

profile of v2, /device:TPU:8, one launch (start us, length us, event | category | flops | bytes accessed | tf_op | source)
XLA Modules:
  0.0 343.8 jit_solution(6365145218784030294)
XLA Ops:
  0.0 1.1 add_select_fusion.1
  1.1 1.3 fusion.14
  2.8 2.1 fusion.29
  4.9 5.4 %fusion.32 = bf16[160,2048]{1,0:T(8,128)(2,1)S(1)} fusion(bf16[2048,2048]{1,0:T(8,128)(2,1)} %param.12, f32[2048]{0:T(1024)S(1)} %bitcast.25, f32[160]{0:T(256)S(1)} %add_rsqrt_fusion.4, bf16[160,2048]{1,0:T(8,128)(2,1)S(1)} %get-tuple-element.14, pred[]{:T(512)S(6)} %or.3), kind=kOutput, calls=%fused_computation.59 | convolution fusion | flops 1346437120 | bytes 9708161 | tf_op jit(solution)/shard_map/dot_general | solution.py:31
  10.3 1.8 collective-permute-start
  12.1 1.7 collective-permute-done
  14.1 1.9 fusion.36
  16.0 0.7 collective-permute-start.1
  17.2 6.8 %multiply_reduce_fusion.1 = (f32[160]{0:T(256)S(1)}, f32[160,768]{1,0:T(8,128)S(1)}) fusion(bf16[2048,768]{1,0:T(8,128)(2,1)} %param.15, bf16[2048,768]{1,0:T(8,128)(2,1)} %param.14, pred[]{:T(512)S(6)} %eq.34, bf16[2048,2048]{1,0:T(8,128)(2,1)} %param.12, bf16[160,2048]{1,0:T(8,128)(2,1)S(1)} %get-tuple-element.6, bf16[160,2048]{1,0:T(8,128)(2,1)} %copy-done.12, ...), kind=kOutput, calls=%fused_computation.102 | convolution fusion | flops 1851899776 | bytes 17147140 | tf_op jit(solution)/shard_map/dot_general | solution.py:58
  24.7 0.7 collective-permute-start.2
  25.5 4.0 %broadcast_in_dim.37 = bf16[32,160,768]{2,1,0:T(8,128)(2,1)} broadcast(bf16[160,768]{1,0:T(8,128)(2,1)S(1)} %collective-permute-done.2), dimensions={1,2} | broadcast | bytes 8110080 | tf_op jit(solution)/shard_map/broadcast_in_dim | solution.py:21
  29.5 9.5 %all-to-all-start = ((bf16[32,160,768]{2,1,0:T(8,128)(2,1)}), bf16[32,160,768]{2,1,0:T(8,128)(2,1)}, u32[]{:S(2)}, u32[]{:S(2)}) async-start(bf16[32,160,768]{2,1,0:T(8,128)(2,1)} %broadcast_in_dim.37), calls=%async_computation | async-start | bytes 15728640 | tf_op jit(solution)/shard_map/all_to_all | solution.py:22
  39.1 1.3 fusion.22
  40.4 102.2 %all-to-all-done = bf16[32,160,768]{2,1,0:T(8,128)(2,1)} async-done(((bf16[32,160,768]{2,1,0:T(8,128)(2,1)}), bf16[32,160,768]{2,1,0:T(8,128)(2,1)}, u32[]{:S(2)}, u32[]{:S(2)}) %all-to-all-start) | async-done | bytes 7864352 | tf_op jit(solution)/shard_map/all_to_all | solution.py:22
  142.5 6.0 %fusion.97 = (f32[160]{0:T(256)S(1)}, f32[160,5120]{1,0:T(8,128)S(1)}) fusion(bf16[160,768]{1,0:T(8,128)(2,1)S(1)} %multiply_convert_fusion.3, bf16[5120,768]{1,0:T(8,128)(2,1)} %bitcast.2), kind=kOutput, calls=%fused_computation.132 | convolution fusion | flops 1259929472 | bytes 11387520 | tf_op jit(solution)/shard_map/dot_general | solution.py:125
  149.2 0.7 collective-permute-start.3
  150.5 0.6 broadcast_in_dim.65
  151.1 9.2 %all-to-all-start.1 = ((f32[32,160,1]{1,2,0:T(1,128)}), f32[32,160,1]{1,2,0:T(1,128)S(1)}, u32[]{:S(2)}, u32[]{:S(2)}) async-start(f32[32,160,1]{1,2,0:T(1,128)} %broadcast_in_dim.65), calls=%async_computation.1 | async-start | bytes 65536 | tf_op jit(solution)/shard_map/all_to_all | solution.py:22
  160.4 6.4 %fusion.81 = f32[160,2048]{1,0:T(8,128)} fusion(bf16[2048,2048]{1,0:T(8,128)(2,1)} %param.12, bf16[160,2048]{1,0:T(8,128)(2,1)} %get-tuple-element.8, f32[160]{0:T(256)} %add_rsqrt_fusion.2, f32[2048]{0:T(1024)} %bitcast.24), kind=kOutput, calls=%fused_computation.114 | convolution fusion | flops 1343488000 | bytes 10363520 | tf_op jit(solution)/shard_map/dot_general | solution.py:31
  166.7 0.8 all-to-all-done.1
  167.5 0.7 reduce
  168.2 0.8 broadcast_in_dim.66
  169.1 5.1 %multiply_reduce_fusion = (f32[160]{0:T(256)S(1)}, f32[160,768]{1,0:T(8,128)S(1)}) fusion(f32[160,768]{1,0:T(8,128)} %copy-done.1, f32[160]{0:T(256)} %copy-done.6, bf16[160,768]{1,0:T(8,128)(2,1)S(1)} %copy-done.4, bf16[5120,768]{1,0:T(8,128)(2,1)} %bitcast.2, f32[160,5120]{1,0:T(8,128)S(1)} %get-tuple-element.18, f32[5120]{0:T(1024)S(1)} %broadcast_in_dim.66, ...), kind=kOutput, calls=%fused_computation.101 | convolution fusion | flops 1261485952 | bytes 12392321 | tf_op jit(solution)/shard_map/dot_general | solution.py:135
  174.5 1.3 convolution_convert_fusion.1
  176.0 6.8 %fusion.16 = (f32[160]{0:T(256)S(1)}, f32[160,2048]{1,0:T(8,128)S(1)}) fusion(bf16[160,2048]{1,0:T(8,128)(2,1)S(1)} %copy-done, f32[160]{0:T(256)S(1)} %copy-done.5, f32[2048]{0:T(1024)S(1)} %bitcast.28, bf16[2048,2048]{1,0:T(8,128)(2,1)} %param.12, f32[160,2048]{1,0:T(8,128)S(1)} %copy-done.15, bf16[160,2048]{1,0:T(8,128)(2,1)S(1)} %convolution_convert_fusion.1, ...), kind=kOutput, calls=%fused_computation.43 | convolution fusion | flops 1347420032 | bytes 12330241 | tf_op jit(solution)/shard_map/dot_general | solution.py:46
  183.3 0.9 collective-permute-start.4
  184.2 3.1 fusion.19
  187.8 1.3 collective-permute-start.5
  189.1 45.7 %collective-permute-done.5 = bf16[160,2048]{1,0:T(8,128)(2,1)S(1)} collective-permute-done((bf16[160,2048]{1,0:T(8,128)(2,1)S(1)}, bf16[160,2048]{1,0:T(8,128)(2,1)S(1)}, u32[]{:S(2)}, u32[]{:S(2)}) %collective-permute-start.5) | collective-permute-done | bytes 655392 | tf_op jit(solution)/shard_map/ppermute | solution.py:16
  234.8 4.1 %convolution_convert_fusion = bf16[2048,2048]{1,0:T(8,128)(2,1)S(1)} fusion(f32[160,2048]{1,0:T(8,128)} %fusion.81, bf16[160,2048]{1,0:T(8,128)(2,1)S(1)} %convolution_convert_fusion.1, bf16[160,2048]{1,0:T(8,128)(2,1)S(1)} %collective-permute-done.5, pred[]{:T(512)S(6)} %ge.21, pred[]{:T(512)S(6)} %and.36, pred[]{:T(512)S(6)} %and.35, pred[]{:T(512)S(6)} %and.29, ...), kind=kOutput, calls=%fused_computation.1 | convolution fusion | flops 1356529664 | bytes 12329604 | tf_op jit(solution)/shard_map/dot_general | solution.py:161
  238.9 102.0 %all_to_all.15 = bf16[32,64,2048]{2,1,0:T(8,128)(2,1)S(1)} all-to-all(bf16[32,64,2048]{2,1,0:T(8,128)(2,1)S(1)} %bitcast.16), channel_id=1, replica_groups=mesh['section'=4,'blk'=32] {'blk'}, dimensions={0} | all-to-all | bytes 16777216 | tf_op jit(solution)/shard_map/all_to_all | solution.py:166
  340.9 2.9 convert_reduce_fusion
  (61 shorter events, 4.5 us)
Async XLA Ops:
  1.1 1.7 copy-start.11
  2.8 2.1 copy-start.13
  4.9 9.2 %slice-start = ((s8[8388608]{0:T(1024)(128)(4,1)}), s8[4194304]{0:T(1024)(128)(4,1)S(1)}, s32[]{:S(2)}) async-start(s8[8388608]{0:T(1024)(128)(4,1)} %bitcast.20), calls=%async_computation.3 | async-start | bytes 8388608
  4.9 9.2 %slice-start.1 = ((s8[8388608]{0:T(1024)(128)(4,1)}), s8[4194304]{0:T(1024)(128)(4,1)S(1)}, s32[]{:S(2)}) async-start(s8[8388608]{0:T(1024)(128)(4,1)} %bitcast.20), calls=%async_computation.4 | async-start | bytes 8388608
  10.3 3.5 %collective-permute-start = (bf16[160,2048]{1,0:T(8,128)(2,1)S(1)}, bf16[160,2048]{1,0:T(8,128)(2,1)S(1)}, u32[]{:S(2)}, u32[]{:S(2)}) collective-permute-start(bf16[160,2048]{1,0:T(8,128)(2,1)S(1)} %fusion.32), channel_id=1, source_target_pairs={{0,32},{1,33},{2,34},{3,35},{4,36},{5,37},{6,38},{7,39},{8,40},{9,... | collective-permute-start | bytes 1966088 | tf_op jit(solution)/shard_map/ppermute | solution.py:16
  16.0 0.8 copy-start.12
  16.0 0.8 collective-permute-start.1
  24.0 5.5 %copy-start.1 = (f32[160,768]{1,0:T(8,128)}, f32[160,768]{1,0:T(8,128)S(1)}, u32[]{:S(2)}) copy-start(f32[160,768]{1,0:T(8,128)S(1)} %get-tuple-element.16) | copy-start | bytes 1474564
  24.0 0.6 copy-start.6
  24.7 0.7 collective-permute-start.2
  25.4 4.1 %copy-start.3 = (bf16[160,768]{1,0:T(8,128)(2,1)}, bf16[160,768]{1,0:T(8,128)(2,1)S(1)}, u32[]{:S(2)}) copy-start(bf16[160,768]{1,0:T(8,128)(2,1)S(1)} %collective-permute-done.2) | copy-start | bytes 737284
  29.5 113.0 %all-to-all-start = ((bf16[32,160,768]{2,1,0:T(8,128)(2,1)}), bf16[32,160,768]{2,1,0:T(8,128)(2,1)}, u32[]{:S(2)}, u32[]{:S(2)}) async-start(bf16[32,160,768]{2,1,0:T(8,128)(2,1)} %broadcast_in_dim.37), calls=%async_computation | async-start | bytes 15728640 | tf_op jit(solution)/shard_map/all_to_all | solution.py:22
  149.2 11.1 %copy-start.8 = (f32[160]{0:T(256)}, f32[160]{0:T(256)S(1)}, u32[]{:S(2)}) copy-start(f32[160]{0:T(256)S(1)} %log_add_fusion) | copy-start | bytes 1924
  149.2 1.3 collective-permute-start.3
  151.1 16.4 %all-to-all-start.1 = ((f32[32,160,1]{1,2,0:T(1,128)}), f32[32,160,1]{1,2,0:T(1,128)S(1)}, u32[]{:S(2)}, u32[]{:S(2)}) async-start(f32[32,160,1]{1,2,0:T(1,128)} %broadcast_in_dim.65), calls=%async_computation.1 | async-start | bytes 65536 | tf_op jit(solution)/shard_map/all_to_all | solution.py:22
  160.3 8.7 %copy-start.4 = (bf16[160,768]{1,0:T(8,128)(2,1)S(1)}, bf16[160,768]{1,0:T(8,128)(2,1)}, u32[]{:S(2)}) copy-start(bf16[160,768]{1,0:T(8,128)(2,1)} %copy-done.3) | copy-start | bytes 737284
  169.1 5.2 %copy-start.2 = (f32[160,768]{1,0:T(8,128)S(1)}, f32[160,768]{1,0:T(8,128)}, u32[]{:S(2)}) copy-start(f32[160,768]{1,0:T(8,128)} %copy-done.1) | copy-start | bytes 1474564
  169.1 5.2 %copy-start.7 = (f32[160]{0:T(256)S(1)}, f32[160]{0:T(256)}, u32[]{:S(2)}) copy-start(f32[160]{0:T(256)} %copy-done.6) | copy-start | bytes 1924
  169.1 5.2 %copy-start.9 = (bf16[2048,768]{1,0:T(8,128)(2,1)S(1)}, bf16[2048,768]{1,0:T(8,128)(2,1)}, u32[]{:S(2)}) copy-start(bf16[2048,768]{1,0:T(8,128)(2,1)} %param.15) | copy-start | bytes 9437188
  169.1 5.4 %copy-start.10 = (bf16[2048,768]{1,0:T(8,128)(2,1)S(1)}, bf16[2048,768]{1,0:T(8,128)(2,1)}, u32[]{:S(2)}) copy-start(bf16[2048,768]{1,0:T(8,128)(2,1)} %param.14) | copy-start | bytes 9437188
  174.5 1.3 copy-start
  174.5 1.3 copy-start.5
  174.5 1.3 copy-start.14
  174.5 1.5 copy-start.15
  174.5 9.7 %slice-start.2 = ((s8[8388608]{0:T(1024)(128)(4,1)}), s8[4194304]{0:T(1024)(128)(4,1)S(1)}, s32[]{:S(2)}) async-start(s8[8388608]{0:T(1024)(128)(4,1)} %bitcast.22), calls=%async_computation.5 | async-start | bytes 8388608
  176.0 8.2 %slice-start.3 = ((s8[8388608]{0:T(1024)(128)(4,1)}), s8[4194304]{0:T(1024)(128)(4,1)S(1)}, s32[]{:S(2)}) async-start(s8[8388608]{0:T(1024)(128)(4,1)} %bitcast.22), calls=%async_computation.6 | async-start | bytes 8388608
  183.3 0.9 collective-permute-start.4
  187.8 47.0 %collective-permute-start.5 = (bf16[160,2048]{1,0:T(8,128)(2,1)S(1)}, bf16[160,2048]{1,0:T(8,128)(2,1)S(1)}, u32[]{:S(2)}, u32[]{:S(2)}) collective-permute-start(bf16[160,2048]{1,0:T(8,128)(2,1)S(1)} %fusion.28), channel_id=1, source_target_pairs={{32,0},{33,1},{34,2},{35,3},{36,4},{37,5},{38,6},{39,7},{40,8},{41... | collective-permute-start | bytes 1966088 | tf_op jit(solution)/shard_map/ppermute | solution.py:16

commit v3 on v2

--- a/solution.py
+++ b/solution.py
@@ -34,11 +34,14 @@
 
 def layer_forward(hidden, weight, gain):
     wide, inverse, normed, scaled, mixed = layer_parts(hidden, weight, gain)
-    return (wide + mixed * jax.nn.sigmoid(mixed)).astype(jnp.bfloat16)
+    return ((wide + mixed * jax.nn.sigmoid(mixed)).astype(jnp.bfloat16), mixed)
 
 
-def layer_backward(hidden, upstream, weight, gain):
-    wide, inverse, normed, scaled, mixed = layer_parts(hidden, weight, gain)
+def layer_backward(hidden, upstream, weight, gain, mixed):
+    wide = hidden.astype(jnp.float32)
+    inverse = lax.rsqrt(jnp.mean(wide * wide, axis=1, keepdims=True) + norm_eps)
+    normed = wide * inverse
+    scaled = (normed * gain).astype(jnp.bfloat16)
     sigma = jax.nn.sigmoid(mixed)
     up_wide = upstream.astype(jnp.float32)
     dmixed = (up_wide * sigma * (1.0 + mixed * (1.0 - sigma))).astype(jnp.bfloat16)
@@ -102,6 +105,7 @@
     blank = jnp.zeros((MICRO, micro_rows, width), jnp.bfloat16)
     saved_inputs = blank
     tops = blank
+    saved_mixed = jnp.zeros((MICRO, micro_rows, width), jnp.float32)
     received = jnp.zeros((micro_rows, width), jnp.bfloat16)
     forward_offset = jnp.where(spec_section, 0, section_index)
     takes_bag = spec_section | (section_index == 0)
@@ -112,8 +116,9 @@
         from_bag = lax.dynamic_index_in_dim(first_inputs, clipped, 0, keepdims=False)
         current = jnp.where(takes_bag, from_bag, received)
         saved_inputs = keep_where(saved_inputs, current, clipped, in_range)
-        output = layer_forward(current, layer_weights, gain)
+        output, mixed = layer_forward(current, layer_weights, gain)
         tops = keep_where(tops, output, clipped, in_range)
+        saved_mixed = keep_where(saved_mixed, mixed, clipped, in_range)
         senders = [s for s in range(top_section) if 0 <= moment - s < MICRO]
         if senders:
             received = shift_pairs("section", [(s, s + 1) for s in senders])(output)
@@ -153,7 +158,8 @@
             starts_grad, lax.dynamic_index_in_dim(top_grad, clipped, 0, keepdims=False), incoming
         )
         hidden = lax.dynamic_index_in_dim(saved_inputs, clipped, 0, keepdims=False)
-        dhidden, scaled, dmixed = layer_backward(hidden, upstream, layer_weights, gain)
+        mixed = lax.dynamic_index_in_dim(saved_mixed, clipped, 0, keepdims=False)
+        dhidden, scaled, dmixed = layer_backward(hidden, upstream, layer_weights, gain, mixed)
         saved_scaled = keep_where(saved_scaled, scaled, clipped, in_range)
         saved_dmixed = keep_where(saved_dmixed, dmixed, clipped, in_range)
     scaled_all = saved_scaled.reshape(sample_rows, width)

time: 344 us -> 305 us (0.89)
  waiting for transfers between devices: 150 us -> 41.4 us
  blocking collectives: 102 us -> 192 us
  starting transfers between devices: 24.8 us -> 13.5 us
  matrix products: 50.2 us -> 42.4 us
  local copies, waits for them, and re-layouts: 7.18 us -> 3.58 us
    all_to_all x2 -> x1, waiting for transfers between devices: 103 us -> 5.96 us  [gather_rows(): got = lax.all_to_all(spread, axis, 0, 0, tiled=True)]
    all_to_all x0 -> x1, blocking collectives: none -> 92.6 us  [gather_rows(): got = lax.all_to_all(spread, axis, 0, 0, tiled=True)]
    ppermute x6, waiting for transfers between devices: 47.3 us -> 35.5 us  [shift_pairs(): return lambda value: lax.ppermute(value, axis, pairs)]
    all_to_all x2 -> x1, starting transfers between devices: 18.8 us -> 7.48 us  [gather_rows(): got = lax.all_to_all(spread, axis, 0, 0, tiled=True)]
    dot_general x1, matrix products: 6.82 us -> 1.29 us  [embed_rows(): emb = jnp.dot(hidden, proj, preferred_element_type=jnp.float32)]
  transfers between devices with their start and end apart: 8 -> 7, of which waited for: 4 -> 3; matrix products, arithmetic and copies ran while one was open for 2% -> 0% of each run, Pallas kernels for 0% -> 0%
where the time goes in v3:
time: 305 us
  blocking collectives  192 us (63%)
  matrix products  42.4 us (14%)
  waiting for transfers between devices  41.4 us (14%)
  starting transfers between devices  13.5 us (4%)
  other arithmetic  10.9 us (4%)
  local copies, waits for them, and re-layouts  3.58 us (1%)
    all_to_all x1, blocking collectives, local(): landed = lax.all_to_all(pieces, 'blk', 0, 0, tiled=True)  99.8 us
    all_to_all x1, blocking collectives, gather_rows(): got = lax.all_to_all(spread, axis, 0, 0, tiled=True)  92.6 us
    ppermute x6, waiting for transfers between devices, shift_pairs(): return lambda value: lax.ppermute(value, axis, pairs)  35.5 us
    dot_general x3, matrix products, layer_parts(): mixed = jnp.dot(scaled, weight, preferred_element_type=jnp.float32)  14.8 us
    dot_general x2, matrix products, layer_backward(): lax.dot_general(dmixed, weight, (((1,), (1,)), ((), ())), preferred_eleme...  9.95 us
    all_to_all x1, starting transfers between devices, gather_rows(): got = lax.all_to_all(spread, axis, 0, 0, tiled=True)  7.48 us
  transfers between devices with their start and end apart: 7, of which 3 were waited for; matrix products, arithmetic and copies ran while one was open for 0% of the time, Pallas kernels for 0%

profile of v3, /device:TPU:8, one launch (start us, length us, event | category | flops | bytes accessed | tf_op | source)
XLA Modules:
  0.0 304.7 jit_solution(1585652063007313559)
XLA Ops:
  0.0 1.1 add_select_fusion.1
  1.1 1.3 fusion.14
  2.8 2.1 fusion.29
  4.9 5.4 %fusion.32 = (bf16[160,2048]{1,0:T(8,128)(2,1)S(1)}, f32[160,2048]{1,0:T(8,128)S(1)}) fusion(bf16[160,2048]{1,0:T(8,128)(2,1)S(1)} %get-tuple-element.13, pred[]{:T(512)S(6)} %or.3, bf16[2048,2048]{1,0:T(8,128)(2,1)} %param.12, f32[2048]{0:T(1024)S(1)} %bitcast.23, f32[160]{0:T(256)S(1)} %add_rsqrt_fusion.4), kind=kOutput, calls=%fused_computation.59 | convolution fusion | flops 1346437120 | bytes 11018881 | tf_op jit(solution)/shard_map/dot_general | solution.py:31
  10.3 1.8 collective-permute-start
  12.1 1.7 collective-permute-done
  14.1 3.2 %fusion.36 = (bf16[160,2048]{1,0:T(8,128)(2,1)}, f32[160,2048]{1,0:T(8,128)}) fusion(bf16[160,2048]{1,0:T(8,128)(2,1)S(1)} %get-tuple-element.9, bf16[2048,2048]{1,0:T(8,128)(2,1)S(1)} %bitcast.18, f32[160]{0:T(256)S(1)} %add_rsqrt_fusion.3, f32[2048]{0:T(1024)S(1)} %bitcast.24), kind=kOutput, calls=%fused_computation.63 | convolution fusion | flops 1345781760 | bytes 11018880 | tf_op jit(solution)/shard_map/dot_general | solution.py:31
  17.3 0.7 collective-permute-start.1
  18.0 2.0 fusion.22
  20.3 6.3 %select_select_fusion = (f32[160,2048]{1,0:T(8,128)}, f32[160,2048]{1,0:T(8,128)S(1)}) fusion(f32[160,2048]{1,0:T(8,128)S(1)} %copy-done.3, f32[160,2048]{1,0:T(8,128)S(1)} %get-tuple-element.15, pred[]{:T(512)S(6)} %and.34, pred[]{:T(512)S(6)} %and.33, pred[]{:T(512)S(6)} %and.30, bf16[2048,2048]{1,0:T(8,128)(2,1)} %param.12, ...), kind=kOutput, calls=%fused_computation.71 | convolution fusion | flops 1344471040 | bytes 14295683 | tf_op jit(solution)/shard_map/dot_general | solution.py:31
  26.6 1.3 multiply_reduce_fusion.1
  28.0 0.7 collective-permute-start.2
  28.7 0.9 broadcast_in_dim.41
  29.6 92.6 %all_to_all.15 = bf16[32,160,768]{2,1,0:T(8,128)(2,1)S(1)} all-to-all(bf16[32,160,768]{2,1,0:T(8,128)(2,1)S(1)} %broadcast_in_dim.41), channel_id=1, replica_groups=mesh['section'=4,'blk'=32] {'blk'}, dimensions={0} | all-to-all | bytes 15728640 | tf_op jit(solution)/shard_map/all_to_all | solution.py:22
  122.2 2.8 fusion.91
  125.9 0.7 collective-permute-start.3
  127.2 7.5 %all-to-all-start.1 = ((f32[32,160,1]{1,2,0:T(1,128)}), f32[32,160,1]{1,2,0:T(1,128)S(1)}, u32[]{:S(2)}, u32[]{:S(2)}) async-start(f32[32,160,1]{1,2,0:T(1,128)} %broadcast_in_dim.70), calls=%async_computation.1 | async-start | bytes 65536 | tf_op jit(solution)/shard_map/all_to_all | solution.py:22
  134.7 1.2 add_rsqrt_fusion.2
  135.9 6.0 %all-to-all-done.1 = f32[32,160,1]{1,2,0:T(1,128)S(1)} async-done(((f32[32,160,1]{1,2,0:T(1,128)}), f32[32,160,1]{1,2,0:T(1,128)S(1)}, u32[]{:S(2)}, u32[]{:S(2)}) %all-to-all-start.1) | async-done | bytes 20512 | tf_op jit(solution)/shard_map/all_to_all | solution.py:22
  141.9 0.7 reduce
  142.5 0.8 broadcast_in_dim.71
  143.4 5.1 %multiply_reduce_fusion = (f32[160]{0:T(256)S(1)}, f32[160,768]{1,0:T(8,128)S(1)}) fusion(f32[160,768]{1,0:T(8,128)} %copy-done.4, f32[160]{0:T(256)} %copy-done.9, bf16[160,768]{1,0:T(8,128)(2,1)S(1)} %collective-permute-done.2, bf16[5120,768]{1,0:T(8,128)(2,1)} %bitcast.16, f32[160,5120]{1,0:T(8,128)S(1)} %get-tuple-element.23, ...), kind=kOutput, calls=%fused_computation.109 | convolution fusion | flops 1261485952 | bytes 12392321 | tf_op jit(solution)/shard_map/dot_general | solution.py:140
  148.8 1.3 convolution_convert_fusion.1
  150.3 6.8 %fusion.16 = (f32[160]{0:T(256)S(1)}, f32[160,2048]{1,0:T(8,128)S(1)}) fusion(bf16[160,2048]{1,0:T(8,128)(2,1)S(1)} %copy-done.1, f32[160]{0:T(256)S(1)} %copy-done.8, f32[2048]{0:T(1024)S(1)} %bitcast.26, bf16[2048,2048]{1,0:T(8,128)(2,1)} %param.12, f32[160,2048]{1,0:T(8,128)S(1)} %copy-done.2, bf16[160,2048]{1,0:T(8,128)(2,1)S(1)} %convolution_convert_fusion.1, ...), kind=kOutput, calls=%fused_computation.43 | convolution fusion | flops 1347420032 | bytes 12330241 | tf_op jit(solution)/shard_map/dot_general | solution.py:49
  157.6 0.7 collective-permute-start.4
  158.3 3.1 %fusion.19 = (f32[160]{0:T(256)S(1)}, f32[160,2048]{1,0:T(8,128)S(1)}) fusion(bf16[160,2048]{1,0:T(8,128)(2,1)S(1)} %copy-done.1, f32[160]{0:T(256)S(1)} %copy-done.8, f32[2048]{0:T(1024)S(1)} %bitcast.27, bf16[2048,2048]{1,0:T(8,128)(2,1)S(1)} %bitcast.20, f32[160,2048]{1,0:T(8,128)S(1)} %copy-done.2, bf16[160,2048]{1,0:T(8,128)(2,1)S(1)} %convolution_convert_fusion.1, ...), kind=kOutput, calls=%fused_computation.46 | convolution fusion | flops 1347420032 | bytes 12985601 | tf_op jit(solution)/shard_map/dot_general | solution.py:49
  161.5 1.3 fusion.28
  162.8 1.5 collective-permute-start.5
  164.3 33.8 %collective-permute-done.5 = bf16[160,2048]{1,0:T(8,128)(2,1)} collective-permute-done((bf16[160,2048]{1,0:T(8,128)(2,1)}, bf16[160,2048]{1,0:T(8,128)(2,1)}, u32[]{:S(2)}, u32[]{:S(2)}) %collective-permute-start.5) | collective-permute-done | bytes 655392 | tf_op jit(solution)/shard_map/ppermute | solution.py:16
  198.1 3.9 %convolution_convert_fusion = bf16[2048,2048]{1,0:T(8,128)(2,1)S(1)} fusion(bf16[160,2048]{1,0:T(8,128)(2,1)S(1)} %copy-done.1, f32[160,2048]{1,0:T(8,128)S(1)} %copy-done.2, bf16[160,2048]{1,0:T(8,128)(2,1)S(1)} %convolution_convert_fusion.1, bf16[160,2048]{1,0:T(8,128)(2,1)} %collective-permute-done.5, f32[160]{0:T(256)S(1)} %copy-done.8, ...), kind=kOutput, calls=%fused_computation.1 | convolution fusion | flops 1356529664 | bytes 12329604 | tf_op jit(solution)/shard_map/dot_general | solution.py:167
  202.0 99.8 %all_to_all.16 = bf16[32,64,2048]{2,1,0:T(8,128)(2,1)S(1)} all-to-all(bf16[32,64,2048]{2,1,0:T(8,128)(2,1)S(1)} %bitcast.21), channel_id=1, replica_groups=mesh['section'=4,'blk'=32] {'blk'}, dimensions={0} | all-to-all | bytes 16777216 | tf_op jit(solution)/shard_map/all_to_all | solution.py:172
  301.8 2.9 convert_reduce_fusion
  (64 shorter events, 3.5 us)
Async XLA Ops:
  2.8 2.1 copy-start.6
  4.9 9.2 %slice-start = ((s8[8388608]{0:T(1024)(128)(4,1)}), s8[4194304]{0:T(1024)(128)(4,1)S(1)}, s32[]{:S(2)}) async-start(s8[8388608]{0:T(1024)(128)(4,1)} %bitcast.17), calls=%async_computation.3 | async-start | bytes 8388608
  4.9 9.2 %slice-start.1 = ((s8[8388608]{0:T(1024)(128)(4,1)}), s8[4194304]{0:T(1024)(128)(4,1)S(1)}, s32[]{:S(2)}) async-start(s8[8388608]{0:T(1024)(128)(4,1)} %bitcast.17), calls=%async_computation.4 | async-start | bytes 8388608
  10.3 1.8 copy-start.16
  10.3 3.5 %collective-permute-start = (bf16[160,2048]{1,0:T(8,128)(2,1)S(1)}, bf16[160,2048]{1,0:T(8,128)(2,1)S(1)}, u32[]{:S(2)}, u32[]{:S(2)}) collective-permute-start(bf16[160,2048]{1,0:T(8,128)(2,1)S(1)} %get-tuple-element.14), channel_id=1, source_target_pairs={{0,32},{1,33},{2,34},{3,35},{4,36},{5,37},{6,38},{7,39},{8,40},{9,... | collective-permute-start | bytes 1966088 | tf_op jit(solution)/shard_map/ppermute | solution.py:16
  17.3 0.7 collective-permute-start.1
  18.0 2.2 copy-start.3
  20.2 6.3 %copy-start.12 = (bf16[2048,768]{1,0:T(8,128)(2,1)S(1)}, bf16[2048,768]{1,0:T(8,128)(2,1)}, u32[]{:S(2)}) copy-start(bf16[2048,768]{1,0:T(8,128)(2,1)} %param.15) | copy-start | bytes 9437188
  20.2 6.3 %copy-start.14 = (bf16[2048,768]{1,0:T(8,128)(2,1)S(1)}, bf16[2048,768]{1,0:T(8,128)(2,1)}, u32[]{:S(2)}) copy-start(bf16[2048,768]{1,0:T(8,128)(2,1)} %param.14) | copy-start | bytes 9437188
  20.2 6.3 %copy-start.17 = (bf16[160,2048]{1,0:T(8,128)(2,1)S(1)}, bf16[160,2048]{1,0:T(8,128)(2,1)}, u32[]{:S(2)}) copy-start(bf16[160,2048]{1,0:T(8,128)(2,1)} %copy-done.16) | copy-start | bytes 1966084
  27.9 0.8 copy-start.4
  27.9 0.8 copy-start.9
  28.0 0.7 collective-permute-start.2
  122.2 3.1 %copy-start = (bf16[32,160,768]{2,1,0:T(8,128)(2,1)}, bf16[32,160,768]{2,1,0:T(8,128)(2,1)S(1)}, u32[]{:S(2)}) copy-start(bf16[32,160,768]{2,1,0:T(8,128)(2,1)S(1)} %all_to_all.15) | copy-start | bytes 23592964
  125.9 1.3 copy-start.11
  125.9 0.7 collective-permute-start.3
  127.2 14.7 %all-to-all-start.1 = ((f32[32,160,1]{1,2,0:T(1,128)}), f32[32,160,1]{1,2,0:T(1,128)S(1)}, u32[]{:S(2)}, u32[]{:S(2)}) async-start(f32[32,160,1]{1,2,0:T(1,128)} %broadcast_in_dim.70), calls=%async_computation.1 | async-start | bytes 65536 | tf_op jit(solution)/shard_map/all_to_all | solution.py:22
  143.4 5.2 %copy-start.5 = (f32[160,768]{1,0:T(8,128)S(1)}, f32[160,768]{1,0:T(8,128)}, u32[]{:S(2)}) copy-start(f32[160,768]{1,0:T(8,128)} %copy-done.4) | copy-start | bytes 1474564
  143.4 5.2 %copy-start.10 = (f32[160]{0:T(256)S(1)}, f32[160]{0:T(256)}, u32[]{:S(2)}) copy-start(f32[160]{0:T(256)} %copy-done.9) | copy-start | bytes 1924
  143.4 5.2 %copy-start.13 = (bf16[2048,768]{1,0:T(8,128)(2,1)S(1)}, bf16[2048,768]{1,0:T(8,128)(2,1)}, u32[]{:S(2)}) copy-start(bf16[2048,768]{1,0:T(8,128)(2,1)} %param.15) | copy-start | bytes 9437188
  143.4 5.4 %copy-start.15 = (bf16[2048,768]{1,0:T(8,128)(2,1)S(1)}, bf16[2048,768]{1,0:T(8,128)(2,1)}, u32[]{:S(2)}) copy-start(bf16[2048,768]{1,0:T(8,128)(2,1)} %param.14) | copy-start | bytes 9437188
  148.8 1.3 copy-start.1
  148.8 1.5 copy-start.2
  148.8 1.5 copy-start.7
  148.8 1.5 copy-start.8
  148.8 9.5 %slice-start.2 = ((s8[8388608]{0:T(1024)(128)(4,1)}), s8[4194304]{0:T(1024)(128)(4,1)S(1)}, s32[]{:S(2)}) async-start(s8[8388608]{0:T(1024)(128)(4,1)} %bitcast.19), calls=%async_computation.5 | async-start | bytes 8388608
  150.3 8.0 %slice-start.3 = ((s8[8388608]{0:T(1024)(128)(4,1)}), s8[4194304]{0:T(1024)(128)(4,1)S(1)}, s32[]{:S(2)}) async-start(s8[8388608]{0:T(1024)(128)(4,1)} %bitcast.19), calls=%async_computation.6 | async-start | bytes 8388608
  157.6 0.7 collective-permute-start.4
  162.8 35.3 %collective-permute-start.5 = (bf16[160,2048]{1,0:T(8,128)(2,1)}, bf16[160,2048]{1,0:T(8,128)(2,1)}, u32[]{:S(2)}, u32[]{:S(2)}) collective-permute-start(bf16[160,2048]{1,0:T(8,128)(2,1)} %fusion.28), channel_id=1, source_target_pairs={{32,0},{33,1},{34,2},{35,3},{36,4},{37,5},{38,6},{39,7},{40,8},{41... | collective-permute-start | bytes 1966088 | tf_op jit(solution)/shard_map/ppermute | solution.py:16

commit v4 on v3

--- a/solution.py
+++ b/solution.py
@@ -4,7 +4,7 @@
 from jax.sharding import PartitionSpec as P
 
 L = 256
-MICRO = 1
+MICRO = 2
 DIGIT = 32
 
 

time: 305 us -> 364 us (1.19)
  waiting for transfers between devices: 41.4 us -> 158 us
  blocking collectives: 192 us -> 101 us
  starting transfers between devices: 13.5 us -> 36.2 us
  matrix products: 42.4 us -> 48 us
  local copies, waits for them, and re-layouts: 3.58 us -> 9.11 us
    all_to_all x1 -> x0, blocking collectives: 92.6 us -> none  [gather_rows(): got = lax.all_to_all(spread, axis, 0, 0, tiled=True)]
    all_to_all x1 -> x2, waiting for transfers between devices: 5.96 us -> 95.7 us  [gather_rows(): got = lax.all_to_all(spread, axis, 0, 0, tiled=True)]
    ppermute x6 -> x8, waiting for transfers between devices: 35.5 us -> 62.4 us  [shift_pairs(): return lambda value: lax.ppermute(value, axis, pairs)]
    all_to_all x1 -> x2, starting transfers between devices: 7.48 us -> 26.6 us  [gather_rows(): got = lax.all_to_all(spread, axis, 0, 0, tiled=True)]
    ppermute x6 -> x8, starting transfers between devices: 6.01 us -> 9.55 us  [shift_pairs(): return lambda value: lax.ppermute(value, axis, pairs)]
    dot_general x2 -> x3, matrix products: 9.95 us -> 12 us  [layer_backward(): lax.dot_general(dmixed, weight, (((1,), (1,)), ((), ())), preferred_eleme...]
    dot_general x3 -> x4, matrix products: 14.8 us -> 15.9 us  [layer_parts(): mixed = jnp.dot(scaled, weight, preferred_element_type=jnp.float32)]
  transfers between devices with their start and end apart: 7 -> 10, of which waited for: 3 -> 6; matrix products, arithmetic and copies ran while one was open for 0% -> 1% of each run, Pallas kernels for 0% -> 0%
where the time goes in v4:
time: 364 us; the launch traced here: 363 us
  waiting for transfers between devices  158 us (43%)
  blocking collectives  101 us (28%)
  matrix products  48 us (13%)
  starting transfers between devices  36.2 us (10%)
  other arithmetic  10.6 us (3%)
  local copies, waits for them, and re-layouts  9.11 us (3%)
    all_to_all x1, blocking collectives, local(): landed = lax.all_to_all(pieces, 'blk', 0, 0, tiled=True)  101 us
    all_to_all x2, waiting for transfers between devices, gather_rows(): got = lax.all_to_all(spread, axis, 0, 0, tiled=True)  95.7 us
    ppermute x8, waiting for transfers between devices, shift_pairs(): return lambda value: lax.ppermute(value, axis, pairs)  62.4 us
    all_to_all x2, starting transfers between devices, gather_rows(): got = lax.all_to_all(spread, axis, 0, 0, tiled=True)  26.6 us
    dot_general x4, matrix products, layer_parts(): mixed = jnp.dot(scaled, weight, preferred_element_type=jnp.float32)  15.9 us
    dot_general x3, matrix products, layer_backward(): lax.dot_general(dmixed, weight, (((1,), (1,)), ((), ())), preferred_eleme...  12 us
    ppermute x8, starting transfers between devices, shift_pairs(): return lambda value: lax.ppermute(value, axis, pairs)  9.55 us
  transfers between devices with their start and end apart: 10, of which 6 were waited for; matrix products, arithmetic and copies ran while one was open for 1% of the time, Pallas kernels for 0%

profile of v4, /device:TPU:8, one launch (start us, length us, event | category | flops | bytes accessed | tf_op | source)
XLA Modules:
  0.0 363.4 jit_solution(14061931941805039821)
XLA Ops:
  0.0 1.2 add_select_fusion.1
  1.2 1.3 fusion.9
  2.9 2.0 fusion.2
  5.2 5.9 %bitcast_dynamic-update-slice_fusion.10 = (bf16[2,80,2048]{2,1,0:T(8,128)(2,1)S(1)}, bf16[80,2048]{1,0:T(8,128)(2,1)S(1)}, f32[80,2048]{1,0:T(8,128)}) fusion(bf16[2,80,2048]{2,1,0:T(8,128)(2,1)S(1)} %broadcast_in_dim.107.clone.1, s32[]{:T(128)S(6)} %min.25, pred[]{:T(512)S(6)} %and.36, bf16[2,80,2048]{2,1,0:T(8,128)(2,1)S(1)} %bitcast.307, pred[]{:T(512)S(6)} %or.3, ...), kind=kOutput, calls=%fused_computation.179 | convolution fusion | flops 673382400 | bytes 10365952 | tf_op jit(solution)/shard_map/dot_general | solution.py:31
  11.2 1.7 collective-permute-start
  13.2 1.0 collective-permute-done
  14.4 5.4 %bitcast_dynamic-update-slice_fusion.9 = (bf16[2,80,2048]{2,1,0:T(8,128)(2,1)S(1)}, bf16[80,2048]{1,0:T(8,128)(2,1)S(1)}, bf16[2,80,2048]{2,1,0:T(8,128)(2,1)S(1)}, f32[80,2048]{1,0:T(8,128)S(1)}) fusion(bf16[2,80,2048]{2,1,0:T(8,128)(2,1)S(1)} %get-tuple-element.17, s32[]{:T(128)S(6)} %min.26, bf16[1,80,2048]{2,1,0:T(8,128)(2,1)S(1)} %get-tuple-element.45, ...), kind=kOutput, calls=%fused_computation.177 | convolution fusion | flops 673218560 | bytes 11346437 | tf_op jit(solution)/shard_map/dot_general | solution.py:31
  19.8 2.3 collective-permute-start.1
  22.2 1.1 collective-permute-done.1
  23.5 1.9 bitcast_dynamic-update-slice_fusion.8
  26.5 2.7 bitcast_dynamic-update-slice_fusion.7
  29.3 1.0 multiply_reduce_fusion.1
  31.9 4.1 %broadcast_in_dim.115 = bf16[32,160,768]{2,1,0:T(8,128)(2,1)} broadcast(bf16[160,768]{1,0:T(8,128)(2,1)S(1)} %collective-permute-done.3), dimensions={1,2} | broadcast | bytes 8110080 | tf_op jit(solution)/shard_map/broadcast_in_dim | solution.py:21
  35.9 9.5 %all-to-all-start = ((bf16[32,160,768]{2,1,0:T(8,128)(2,1)}), bf16[32,160,768]{2,1,0:T(8,128)(2,1)}, u32[]{:S(2)}, u32[]{:S(2)}) async-start(bf16[32,160,768]{2,1,0:T(8,128)(2,1)} %broadcast_in_dim.115), calls=%async_computation | async-start | bytes 15728640 | tf_op jit(solution)/shard_map/all_to_all | solution.py:22
  45.6 1.1 bitcast_dynamic-update-slice_fusion.3
  48.1 88.6 %all-to-all-done = bf16[32,160,768]{2,1,0:T(8,128)(2,1)} async-done(((bf16[32,160,768]{2,1,0:T(8,128)(2,1)}), bf16[32,160,768]{2,1,0:T(8,128)(2,1)}, u32[]{:S(2)}, u32[]{:S(2)}) %all-to-all-start) | async-done | bytes 7864352 | tf_op jit(solution)/shard_map/all_to_all | solution.py:22
  136.7 6.0 %fusion.136 = (f32[160]{0:T(256)S(1)}, f32[160,5120]{1,0:T(8,128)S(1)}) fusion(bf16[160,768]{1,0:T(8,128)(2,1)S(1)} %multiply_convert_fusion.1, bf16[5120,768]{1,0:T(8,128)(2,1)} %bitcast.25), kind=kOutput, calls=%fused_computation.245 | convolution fusion | flops 1259929472 | bytes 11387520 | tf_op jit(solution)/shard_map/dot_general | solution.py:130
  142.8 1.8 copy-done
  146.6 17.1 %all-to-all-start.1 = ((f32[32,160,1]{1,2,0:T(1,128)}), f32[32,160,1]{1,2,0:T(1,128)S(1)}, u32[]{:S(2)}, u32[]{:S(2)}) async-start(f32[32,160,1]{1,2,0:T(1,128)} %broadcast_in_dim.118), calls=%async_computation.1 | async-start | bytes 65536 | tf_op jit(solution)/shard_map/all_to_all | solution.py:22
  163.7 7.2 %all-to-all-done.1 = f32[32,160,1]{1,2,0:T(1,128)S(1)} async-done(((f32[32,160,1]{1,2,0:T(1,128)}), f32[32,160,1]{1,2,0:T(1,128)S(1)}, u32[]{:S(2)}, u32[]{:S(2)}) %all-to-all-start.1) | async-done | bytes 20512 | tf_op jit(solution)/shard_map/all_to_all | solution.py:22
  171.1 6.1 %multiply_reduce_fusion = (f32[160]{0:T(256)S(1)}, f32[160,768]{1,0:T(8,128)S(1)}) fusion(f32[160,768]{1,0:T(8,128)S(1)} %copy-done.4, f32[160]{0:T(256)S(1)} %add_rsqrt_fusion, bf16[160,768]{1,0:T(8,128)(2,1)S(1)} %copy-done.6, bf16[5120,768]{1,0:T(8,128)(2,1)} %bitcast.25, f32[160,5120]{1,0:T(8,128)} %copy-done, f32[5120]{0:T(1024)S(1)} %broadcast_in_dim.119, ...), kind=kOutput, calls=%fused_computation.149 | convolution fusion | flops 1261485952 | bytes 12392321 | tf_op jit(solution)/shard_map/dot_general | solution.py:140
  177.2 1.2 convolution_convert_fusion
  178.5 6.4 %fusion.34 = (f32[80]{0:T(128)S(1)}, f32[80]{0:T(128)S(1)}, f32[80,2048]{1,0:T(8,128)S(1)}) fusion(f32[80]{0:T(128)S(1)} %add_rsqrt_fusion.5, bf16[2,80,2048]{2,1,0:T(8,128)(2,1)S(1)} %get-tuple-element.26, s32[]{:T(128)S(6)} %min.29, s32[]{:T(128)S(6)} %min.30, f32[2048]{0:T(1024)S(1)} %bitcast.318, bf16[2048,2048]{1,0:T(8,128)(2,1)} %param.12, ...), kind=kOutput, calls=%fused_computation.73 | convolution fusion | flops 674201472 | bytes 10693760 | tf_op jit(solution)/shard_map/dot_general | solution.py:49
  186.9 2.8 fusion.31
  190.0 1.5 collective-permute-start.6
  191.7 49.9 %collective-permute-done.6 = bf16[80,2048]{1,0:T(8,128)(2,1)S(1)} collective-permute-done((bf16[80,2048]{1,0:T(8,128)(2,1)S(1)}, bf16[80,2048]{1,0:T(8,128)(2,1)S(1)}, u32[]{:S(2)}, u32[]{:S(2)}) %collective-permute-start.6) | collective-permute-done | bytes 327712 | tf_op jit(solution)/shard_map/ppermute | solution.py:16
  242.0 2.8 fusion.28
  245.1 1.3 collective-permute-start.7
  246.6 10.4 %collective-permute-done.7 = bf16[80,2048]{1,0:T(8,128)(2,1)S(1)} collective-permute-done((bf16[80,2048]{1,0:T(8,128)(2,1)S(1)}, bf16[80,2048]{1,0:T(8,128)(2,1)S(1)}, u32[]{:S(2)}, u32[]{:S(2)}) %collective-permute-start.7) | collective-permute-done | bytes 327712 | tf_op jit(solution)/shard_map/ppermute | solution.py:16
  257.4 2.4 bitcast_convert_fusion
  259.8 100.6 %all_to_all.15 = bf16[32,64,2048]{2,1,0:T(8,128)(2,1)S(1)} all-to-all(bf16[32,64,2048]{2,1,0:T(8,128)(2,1)S(1)} %bitcast.297), channel_id=1, replica_groups=mesh['section'=4,'blk'=32] {'blk'}, dimensions={0} | all-to-all | bytes 16777216 | tf_op jit(solution)/shard_map/all_to_all | solution.py:172
  360.4 2.9 convert_reduce_fusion
  (97 shorter events, 11.3 us)
Async XLA Ops:
  0.0 2.9 copy-start.11
  2.4 2.8 copy-start.2
  11.2 3.0 collective-permute-start
  14.1 9.4 %slice-start = ((s8[8388608]{0:T(1024)(128)(4,1)}), s8[4194304]{0:T(1024)(128)(4,1)S(1)}, s32[]{:S(2)}) async-start(s8[8388608]{0:T(1024)(128)(4,1)} %bitcast.293), calls=%async_computation.3 | async-start | bytes 8388608
  14.4 9.2 %slice-start.1 = ((s8[8388608]{0:T(1024)(128)(4,1)}), s8[4194304]{0:T(1024)(128)(4,1)S(1)}, s32[]{:S(2)}) async-start(s8[8388608]{0:T(1024)(128)(4,1)} %bitcast.293), calls=%async_computation.4 | async-start | bytes 8388608
  19.8 3.5 collective-permute-start.1
  25.5 0.8 collective-permute-start.2
  26.5 2.7 copy-start.7
  26.5 2.8 copy-start.9
  30.4 5.6 %copy-start.3 = (f32[160,768]{1,0:T(8,128)}, f32[160,768]{1,0:T(8,128)S(1)}, u32[]{:S(2)}) copy-start(f32[160,768]{1,0:T(8,128)S(1)} %get-tuple-element.36) | copy-start | bytes 1474564
  30.5 0.7 collective-permute-start.3
  31.2 0.7 copy-start.5
  35.9 100.7 %all-to-all-start = ((bf16[32,160,768]{2,1,0:T(8,128)(2,1)}), bf16[32,160,768]{2,1,0:T(8,128)(2,1)}, u32[]{:S(2)}, u32[]{:S(2)}) async-start(bf16[32,160,768]{2,1,0:T(8,128)(2,1)} %broadcast_in_dim.115), calls=%async_computation | async-start | bytes 15728640 | tf_op jit(solution)/shard_map/all_to_all | solution.py:22
  46.9 1.1 copy-start.1
  142.7 1.8 copy-start
  142.7 28.3 %copy-start.4 = (f32[160,768]{1,0:T(8,128)S(1)}, f32[160,768]{1,0:T(8,128)}, u32[]{:S(2)}) copy-start(f32[160,768]{1,0:T(8,128)} %copy-done.3) | copy-start | bytes 1474564
  142.7 28.3 %copy-start.6 = (bf16[160,768]{1,0:T(8,128)(2,1)S(1)}, bf16[160,768]{1,0:T(8,128)(2,1)}, u32[]{:S(2)}) copy-start(bf16[160,768]{1,0:T(8,128)(2,1)} %copy-done.5) | copy-start | bytes 737284
  145.1 0.8 collective-permute-start.4
  146.6 24.3 %all-to-all-start.1 = ((f32[32,160,1]{1,2,0:T(1,128)}), f32[32,160,1]{1,2,0:T(1,128)S(1)}, u32[]{:S(2)}, u32[]{:S(2)}) async-start(f32[32,160,1]{1,2,0:T(1,128)} %broadcast_in_dim.118), calls=%async_computation.1 | async-start | bytes 65536 | tf_op jit(solution)/shard_map/all_to_all | solution.py:22
  171.1 6.1 %copy-start.8 = (bf16[2048,768]{1,0:T(8,128)(2,1)S(1)}, bf16[2048,768]{1,0:T(8,128)(2,1)}, u32[]{:S(2)}) copy-start(bf16[2048,768]{1,0:T(8,128)(2,1)} %param.15) | copy-start | bytes 9437188
  171.1 6.1 %copy-start.10 = (bf16[2048,768]{1,0:T(8,128)(2,1)S(1)}, bf16[2048,768]{1,0:T(8,128)(2,1)}, u32[]{:S(2)}) copy-start(bf16[2048,768]{1,0:T(8,128)(2,1)} %param.14) | copy-start | bytes 9437188
  177.2 9.7 %slice-start.2 = ((s8[8388608]{0:T(1024)(128)(4,1)}), s8[4194304]{0:T(1024)(128)(4,1)S(1)}, s32[]{:S(2)}) async-start(s8[8388608]{0:T(1024)(128)(4,1)} %bitcast.295), calls=%async_computation.5 | async-start | bytes 8388608
  178.5 8.4 %slice-start.3 = ((s8[8388608]{0:T(1024)(128)(4,1)}), s8[4194304]{0:T(1024)(128)(4,1)S(1)}, s32[]{:S(2)}) async-start(s8[8388608]{0:T(1024)(128)(4,1)} %bitcast.295), calls=%async_computation.6 | async-start | bytes 8388608
  185.2 1.3 collective-permute-start.5
  190.0 51.6 %collective-permute-start.6 = (bf16[80,2048]{1,0:T(8,128)(2,1)S(1)}, bf16[80,2048]{1,0:T(8,128)(2,1)S(1)}, u32[]{:S(2)}, u32[]{:S(2)}) collective-permute-start(bf16[80,2048]{1,0:T(8,128)(2,1)S(1)} %fusion.56), channel_id=1, source_target_pairs={{32,0},{64,32},{33,1},{65,33},{34,2},{66,34},{35,3},{67,35},{36,4}... | collective-permute-start | bytes 983048 | tf_op jit(solution)/shard_map/ppermute | solution.py:16
  245.1 12.0 %collective-permute-start.7 = (bf16[80,2048]{1,0:T(8,128)(2,1)S(1)}, bf16[80,2048]{1,0:T(8,128)(2,1)S(1)}, u32[]{:S(2)}, u32[]{:S(2)}) collective-permute-start(bf16[80,2048]{1,0:T(8,128)(2,1)S(1)} %fusion.59), channel_id=1, source_target_pairs={{32,0},{33,1},{34,2},{35,3},{36,4},{37,5},{38,6},{39,7},{40,8},{41... | collective-permute-start | bytes 983048 | tf_op jit(solution)/shard_map/ppermute | solution.py:16

commit v5 on v3

--- a/solution.py
+++ b/solution.py
@@ -34,14 +34,11 @@
 
 def layer_forward(hidden, weight, gain):
     wide, inverse, normed, scaled, mixed = layer_parts(hidden, weight, gain)
-    return ((wide + mixed * jax.nn.sigmoid(mixed)).astype(jnp.bfloat16), mixed)
+    return ((wide + mixed * jax.nn.sigmoid(mixed)).astype(jnp.bfloat16), mixed, scaled, inverse)
 
 
-def layer_backward(hidden, upstream, weight, gain, mixed):
-    wide = hidden.astype(jnp.float32)
-    inverse = lax.rsqrt(jnp.mean(wide * wide, axis=1, keepdims=True) + norm_eps)
-    normed = wide * inverse
-    scaled = (normed * gain).astype(jnp.bfloat16)
+def layer_backward(hidden, upstream, weight, gain, mixed, scaled, inverse):
+    normed = hidden.astype(jnp.float32) * inverse
     sigma = jax.nn.sigmoid(mixed)
     up_wide = upstream.astype(jnp.float32)
     dmixed = (up_wide * sigma * (1.0 + mixed * (1.0 - sigma))).astype(jnp.bfloat16)
@@ -106,6 +103,8 @@
     saved_inputs = blank
     tops = blank
     saved_mixed = jnp.zeros((MICRO, micro_rows, width), jnp.float32)
+    kept_scaled = blank
+    saved_inverse = jnp.zeros((MICRO, micro_rows, 1), jnp.float32)
     received = jnp.zeros((micro_rows, width), jnp.bfloat16)
     forward_offset = jnp.where(spec_section, 0, section_index)
     takes_bag = spec_section | (section_index == 0)
@@ -116,9 +115,11 @@
         from_bag = lax.dynamic_index_in_dim(first_inputs, clipped, 0, keepdims=False)
         current = jnp.where(takes_bag, from_bag, received)
         saved_inputs = keep_where(saved_inputs, current, clipped, in_range)
-        output, mixed = layer_forward(current, layer_weights, gain)
+        output, mixed, scaled, inverse = layer_forward(current, layer_weights, gain)
         tops = keep_where(tops, output, clipped, in_range)
         saved_mixed = keep_where(saved_mixed, mixed, clipped, in_range)
+        kept_scaled = keep_where(kept_scaled, scaled, clipped, in_range)
+        saved_inverse = keep_where(saved_inverse, inverse, clipped, in_range)
         senders = [s for s in range(top_section) if 0 <= moment - s < MICRO]
         if senders:
             received = shift_pairs("section", [(s, s + 1) for s in senders])(output)
@@ -159,7 +160,11 @@
         )
         hidden = lax.dynamic_index_in_dim(saved_inputs, clipped, 0, keepdims=False)
         mixed = lax.dynamic_index_in_dim(saved_mixed, clipped, 0, keepdims=False)
-        dhidden, scaled, dmixed = layer_backward(hidden, upstream, layer_weights, gain, mixed)
+        scaled = lax.dynamic_index_in_dim(kept_scaled, clipped, 0, keepdims=False)
+        inverse = lax.dynamic_index_in_dim(saved_inverse, clipped, 0, keepdims=False)
+        dhidden, scaled, dmixed = layer_backward(
+            hidden, upstream, layer_weights, gain, mixed, scaled, inverse
+        )
         saved_scaled = keep_where(saved_scaled, scaled, clipped, in_range)
         saved_dmixed = keep_where(saved_dmixed, dmixed, clipped, in_range)
     scaled_all = saved_scaled.reshape(sample_rows, width)

time: 305 us -> 307 us (level)
  no operation moved by 1% of the time
where the time goes in v5:
time: 307 us
  blocking collectives  193 us (63%)
  matrix products  43.3 us (14%)
  waiting for transfers between devices  43.1 us (14%)
  starting transfers between devices  14.2 us (5%)
  other arithmetic  8.41 us (3%)
  local copies, waits for them, and re-layouts  4.53 us (1%)
    all_to_all x1, blocking collectives, local(): landed = lax.all_to_all(pieces, 'blk', 0, 0, tiled=True)  99.8 us
    all_to_all x1, blocking collectives, gather_rows(): got = lax.all_to_all(spread, axis, 0, 0, tiled=True)  92.7 us
    ppermute x6, waiting for transfers between devices, shift_pairs(): return lambda value: lax.ppermute(value, axis, pairs)  35.9 us
    dot_general x3, matrix products, layer_parts(): mixed = jnp.dot(scaled, weight, preferred_element_type=jnp.float32)  14.6 us
    dot_general x2, matrix products, layer_backward(): lax.dot_general(dmixed, weight, (((1,), (1,)), ((), ())), preferred_eleme...  10.2 us
    all_to_all x1, starting transfers between devices, gather_rows(): got = lax.all_to_all(spread, axis, 0, 0, tiled=True)  7.35 us
    all_to_all x1, waiting for transfers between devices, gather_rows(): got = lax.all_to_all(spread, axis, 0, 0, tiled=True)  7.18 us
    ppermute x6, starting transfers between devices, shift_pairs(): return lambda value: lax.ppermute(value, axis, pairs)  6.83 us
  transfers between devices with their start and end apart: 7, of which 3 were waited for; matrix products, arithmetic and copies ran while one was open for 0% of the time, Pallas kernels for 0%

profile of v5, /device:TPU:8, one launch (start us, length us, event | category | flops | bytes accessed | tf_op | source)
XLA Modules:
  0.0 306.6 jit_solution(10626805894761810536)
XLA Ops:
  0.0 1.1 add_select_fusion.1
  1.1 1.3 fusion.9
  2.8 2.1 fusion.16
  4.9 5.5 %fusion.19 = (bf16[160,2048]{1,0:T(8,128)(2,1)S(1)}, f32[160,2048]{1,0:T(8,128)S(1)}) fusion(bf16[160,2048]{1,0:T(8,128)(2,1)S(1)} %get-tuple-element.16, pred[]{:T(512)S(6)} %or.3, bf16[2048,2048]{1,0:T(8,128)(2,1)} %param.12, f32[2048]{0:T(1024)S(1)} %bitcast.23, f32[160]{0:T(256)S(1)} %add_rsqrt_fusion.3), kind=kOutput, calls=%fused_computation.44 | convolution fusion | flops 1346437120 | bytes 11018881 | tf_op jit(solution)/shard_map/dot_general | solution.py:31
  10.4 1.8 collective-permute-start
  12.2 1.7 collective-permute-done
  14.3 2.8 fusion.23
  17.0 1.5 collective-permute-start.1
  19.5 6.3 %select_select_fusion = (f32[160,2048]{1,0:T(8,128)}, f32[160,2048]{1,0:T(8,128)S(1)}) fusion(f32[160,2048]{1,0:T(8,128)S(1)} %get-tuple-element.20, f32[160,2048]{1,0:T(8,128)S(1)} %get-tuple-element.18, pred[]{:T(512)S(6)} %and.34, pred[]{:T(512)S(6)} %and.33, pred[]{:T(512)S(6)} %and.30, bf16[2048,2048]{1,0:T(8,128)(2,1)} %param.12, ...), kind=kOutput, calls=%fused_computation.59 | convolution fusion | flops 1344471040 | bytes 14295683 | tf_op jit(solution)/shard_map/dot_general | solution.py:31
  25.8 1.3 multiply_reduce_fusion.3
  27.2 0.7 collective-permute-start.2
  28.0 0.9 broadcast_in_dim.72
  28.8 92.7 %all_to_all.15 = bf16[32,160,768]{2,1,0:T(8,128)(2,1)S(1)} all-to-all(bf16[32,160,768]{2,1,0:T(8,128)(2,1)S(1)} %broadcast_in_dim.72), channel_id=1, replica_groups=mesh['section'=4,'blk'=32] {'blk'}, dimensions={0} | all-to-all | bytes 15728640 | tf_op jit(solution)/shard_map/all_to_all | solution.py:22
  121.5 2.8 fusion.77
  124.6 0.6 exponential_reduce_fusion
  125.8 0.6 collective-permute-start.3
  126.5 0.6 broadcast_in_dim.75
  127.1 7.3 %all-to-all-start.1 = ((f32[32,160,1]{1,2,0:T(1,128)}), f32[32,160,1]{1,2,0:T(1,128)S(1)}, u32[]{:S(2)}, u32[]{:S(2)}) async-start(f32[32,160,1]{1,2,0:T(1,128)} %broadcast_in_dim.75), calls=%async_computation.1 | async-start | bytes 65536 | tf_op jit(solution)/shard_map/all_to_all | solution.py:22
  134.5 7.2 %all-to-all-done.1 = f32[32,160,1]{1,2,0:T(1,128)S(1)} async-done(((f32[32,160,1]{1,2,0:T(1,128)}), f32[32,160,1]{1,2,0:T(1,128)S(1)}, u32[]{:S(2)}, u32[]{:S(2)}) %all-to-all-start.1) | async-done | bytes 20512 | tf_op jit(solution)/shard_map/all_to_all | solution.py:22
  141.6 0.7 reduce
  142.3 0.8 broadcast_in_dim.76
  143.2 5.1 %multiply_reduce_fusion.2 = (f32[160]{0:T(256)S(1)}, f32[160,768]{1,0:T(8,128)S(1)}) fusion(f32[160,768]{1,0:T(8,128)} %copy-done.9, f32[160]{0:T(256)} %copy-done.16, bf16[160,768]{1,0:T(8,128)(2,1)S(1)} %collective-permute-done.2, bf16[5120,768]{1,0:T(8,128)(2,1)} %bitcast.16, f32[160,5120]{1,0:T(8,128)S(1)} %get-tuple-element.26, ...), kind=kOutput, calls=%fused_computation.92 | convolution fusion | flops 1261485952 | bytes 12392321 | tf_op jit(solution)/shard_map/dot_general | solution.py:141
  148.6 1.2 convolution_convert_fusion.1
  150.4 7.0 %multiply_reduce_fusion.1 = (f32[160]{0:T(256)S(1)}, bf16[160,2048]{1,0:T(8,128)(2,1)S(1)}, f32[160,2048]{1,0:T(8,128)S(1)}) fusion(f32[160]{0:T(256)S(1)} %copy-done.13, bf16[160,2048]{1,0:T(8,128)(2,1)S(1)} %copy-done.2, bf16[160,2048]{1,0:T(8,128)(2,1)S(1)} %copy-done.7, bf16[160,2048]{1,0:T(8,128)(2,1)S(1)} %copy-done.4, pred[]{:T(512)S(6)} %or.3, ...), kind=kOutput, calls=%fused_computation.55 | convolution fusion | flops 1348730752 | bytes 14296325 | tf_op jit(solution)/shard_map/dot_general | solution.py:46
  157.9 0.7 collective-permute-start.4
  158.6 3.2 %multiply_reduce_fusion = (f32[160]{0:T(256)S(1)}, f32[160,2048]{1,0:T(8,128)S(1)}) fusion(bf16[160,2048]{1,0:T(8,128)(2,1)S(1)} %get-tuple-element.6, f32[160]{0:T(256)S(1)} %copy-done.13, f32[2048]{0:T(1024)S(1)} %bitcast.27, bf16[2048,2048]{1,0:T(8,128)(2,1)S(1)} %bitcast.20, f32[160,2048]{1,0:T(8,128)S(1)} %copy-done.5, ...), kind=kOutput, calls=%fused_computation.54 | convolution fusion | flops 1347420032 | bytes 12985601 | tf_op jit(solution)/shard_map/dot_general | solution.py:46
  161.9 1.4 fusion.15
  163.3 1.5 collective-permute-start.5
  164.8 34.2 %collective-permute-done.5 = bf16[160,2048]{1,0:T(8,128)(2,1)} collective-permute-done((bf16[160,2048]{1,0:T(8,128)(2,1)}, bf16[160,2048]{1,0:T(8,128)(2,1)}, u32[]{:S(2)}, u32[]{:S(2)}) %collective-permute-start.5) | collective-permute-done | bytes 655392 | tf_op jit(solution)/shard_map/ppermute | solution.py:16
  199.0 4.8 %convolution_convert_fusion = bf16[2048,2048]{1,0:T(8,128)(2,1)S(1)} fusion(f32[160,2048]{1,0:T(8,128)S(1)} %copy-done.5, bf16[160,2048]{1,0:T(8,128)(2,1)S(1)} %convolution_convert_fusion.1, bf16[160,2048]{1,0:T(8,128)(2,1)} %collective-permute-done.5, pred[]{:T(512)S(6)} %ge.21, pred[]{:T(512)S(6)} %and.36, pred[]{:T(512)S(6)} %and.35, pred[]{:T(512)S(6)} %and.34, ...), kind=kOutput, calls=%fused_computation.1 | convolution fusion | flops 1360461824 | bytes 13641608 | tf_op jit(solution)/shard_map/dot_general | solution.py:172
  203.8 99.8 %all_to_all.16 = bf16[32,64,2048]{2,1,0:T(8,128)(2,1)S(1)} all-to-all(bf16[32,64,2048]{2,1,0:T(8,128)(2,1)S(1)} %bitcast.21), channel_id=1, replica_groups=mesh['section'=4,'blk'=32] {'blk'}, dimensions={0} | all-to-all | bytes 16777216 | tf_op jit(solution)/shard_map/all_to_all | solution.py:177
  303.7 3.0 convert_reduce_fusion
  (84 shorter events, 4.0 us)
Async XLA Ops:
  2.8 2.2 copy-start.11
  4.9 13.7 %copy-start.3 = (bf16[160,2048]{1,0:T(8,128)(2,1)}, bf16[160,2048]{1,0:T(8,128)(2,1)S(1)}, u32[]{:S(2)}) copy-start(bf16[160,2048]{1,0:T(8,128)(2,1)S(1)} %get-tuple-element.16) | copy-start | bytes 1966084
  4.9 5.5 %copy-start.19 = (f32[160]{0:T(256)}, f32[160]{0:T(256)S(1)}, u32[]{:S(2)}) copy-start(f32[160]{0:T(256)S(1)} %add_rsqrt_fusion.3) | copy-start | bytes 1924
  4.9 9.3 %slice-start = ((s8[8388608]{0:T(1024)(128)(4,1)}), s8[4194304]{0:T(1024)(128)(4,1)S(1)}, s32[]{:S(2)}) async-start(s8[8388608]{0:T(1024)(128)(4,1)} %bitcast.17), calls=%async_computation.3 | async-start | bytes 8388608
  4.9 9.3 %slice-start.1 = ((s8[8388608]{0:T(1024)(128)(4,1)}), s8[4194304]{0:T(1024)(128)(4,1)S(1)}, s32[]{:S(2)}) async-start(s8[8388608]{0:T(1024)(128)(4,1)} %bitcast.17), calls=%async_computation.4 | async-start | bytes 8388608
  10.4 3.8 %copy-start.27 = (bf16[160,2048]{1,0:T(8,128)(2,1)}, bf16[160,2048]{1,0:T(8,128)(2,1)S(1)}, u32[]{:S(2)}) copy-start(bf16[160,2048]{1,0:T(8,128)(2,1)S(1)} %get-tuple-element.17) | copy-start | bytes 1966084
  10.4 3.5 %collective-permute-start = (bf16[160,2048]{1,0:T(8,128)(2,1)S(1)}, bf16[160,2048]{1,0:T(8,128)(2,1)S(1)}, u32[]{:S(2)}, u32[]{:S(2)}) collective-permute-start(bf16[160,2048]{1,0:T(8,128)(2,1)S(1)} %get-tuple-element.17), channel_id=1, source_target_pairs={{0,32},{1,33},{2,34},{3,35},{4,36},{5,37},{6,38},{7,39},{8,40},{9,... | collective-permute-start | bytes 1966088 | tf_op jit(solution)/shard_map/ppermute | solution.py:16
  14.2 2.8 copy-start.6
  14.2 2.8 copy-start.21
  17.0 1.5 collective-permute-start.1
  18.9 6.9 %copy-start.1 = (bf16[160,2048]{1,0:T(8,128)(2,1)}, bf16[160,2048]{1,0:T(8,128)(2,1)S(1)}, u32[]{:S(2)}) copy-start(bf16[160,2048]{1,0:T(8,128)(2,1)S(1)} %get-tuple-element.8) | copy-start | bytes 1966084
  19.5 6.3 %copy-start.14 = (f32[160]{0:T(256)}, f32[160]{0:T(256)S(1)}, u32[]{:S(2)}) copy-start(f32[160]{0:T(256)S(1)} %get-tuple-element.14) | copy-start | bytes 1924
  19.5 6.3 %copy-start.23 = (bf16[2048,768]{1,0:T(8,128)(2,1)S(1)}, bf16[2048,768]{1,0:T(8,128)(2,1)}, u32[]{:S(2)}) copy-start(bf16[2048,768]{1,0:T(8,128)(2,1)} %param.15) | copy-start | bytes 9437188
  19.5 6.3 %copy-start.25 = (bf16[2048,768]{1,0:T(8,128)(2,1)S(1)}, bf16[2048,768]{1,0:T(8,128)(2,1)}, u32[]{:S(2)}) copy-start(bf16[2048,768]{1,0:T(8,128)(2,1)} %param.14) | copy-start | bytes 9437188
  19.5 6.4 %copy-start.28 = (bf16[160,2048]{1,0:T(8,128)(2,1)S(1)}, bf16[160,2048]{1,0:T(8,128)(2,1)}, u32[]{:S(2)}) copy-start(bf16[160,2048]{1,0:T(8,128)(2,1)} %copy-done.27) | copy-start | bytes 1966084
  27.2 0.7 collective-permute-start.2
  121.5 3.1 copy-start
  125.8 0.7 collective-permute-start.3
  127.1 14.5 %all-to-all-start.1 = ((f32[32,160,1]{1,2,0:T(1,128)}), f32[32,160,1]{1,2,0:T(1,128)S(1)}, u32[]{:S(2)}, u32[]{:S(2)}) async-start(f32[32,160,1]{1,2,0:T(1,128)} %broadcast_in_dim.75), calls=%async_computation.1 | async-start | bytes 65536 | tf_op jit(solution)/shard_map/all_to_all | solution.py:22
  143.2 5.2 %copy-start.10 = (f32[160,768]{1,0:T(8,128)S(1)}, f32[160,768]{1,0:T(8,128)}, u32[]{:S(2)}) copy-start(f32[160,768]{1,0:T(8,128)} %copy-done.9) | copy-start | bytes 1474564
  143.2 5.2 %copy-start.17 = (f32[160]{0:T(256)S(1)}, f32[160]{0:T(256)}, u32[]{:S(2)}) copy-start(f32[160]{0:T(256)} %copy-done.16) | copy-start | bytes 1924
  143.2 5.2 %copy-start.24 = (bf16[2048,768]{1,0:T(8,128)(2,1)S(1)}, bf16[2048,768]{1,0:T(8,128)(2,1)}, u32[]{:S(2)}) copy-start(bf16[2048,768]{1,0:T(8,128)(2,1)} %param.15) | copy-start | bytes 9437188
  143.2 5.4 %copy-start.26 = (bf16[2048,768]{1,0:T(8,128)(2,1)S(1)}, bf16[2048,768]{1,0:T(8,128)(2,1)}, u32[]{:S(2)}) copy-start(bf16[2048,768]{1,0:T(8,128)(2,1)} %param.14) | copy-start | bytes 9437188
  148.6 1.9 copy-start.7
  148.6 10.0 %slice-start.2 = ((s8[8388608]{0:T(1024)(128)(4,1)}), s8[4194304]{0:T(1024)(128)(4,1)S(1)}, s32[]{:S(2)}) async-start(s8[8388608]{0:T(1024)(128)(4,1)} %bitcast.19), calls=%async_computation.5 | async-start | bytes 8388608
  150.4 8.2 %slice-start.3 = ((s8[8388608]{0:T(1024)(128)(4,1)}), s8[4194304]{0:T(1024)(128)(4,1)S(1)}, s32[]{:S(2)}) async-start(s8[8388608]{0:T(1024)(128)(4,1)} %bitcast.19), calls=%async_computation.6 | async-start | bytes 8388608
  157.9 0.7 collective-permute-start.4
  158.6 3.2 %copy-start.8 = (bf16[160,2048]{1,0:T(8,128)(2,1)}, bf16[160,2048]{1,0:T(8,128)(2,1)S(1)}, u32[]{:S(2)}) copy-start(bf16[160,2048]{1,0:T(8,128)(2,1)S(1)} %collective-permute-done.4) | copy-start | bytes 1966084
  161.9 37.2 %copy-start.15 = (f32[160]{0:T(256)S(1)}, f32[160]{0:T(256)}, u32[]{:S(2)}) copy-start(f32[160]{0:T(256)} %copy-done.14) | copy-start | bytes 1924
  161.9 37.1 %copy-start.20 = (f32[160]{0:T(256)S(1)}, f32[160]{0:T(256)}, u32[]{:S(2)}) copy-start(f32[160]{0:T(256)} %copy-done.19) | copy-start | bytes 1924
  161.9 37.1 %copy-start.22 = (f32[160]{0:T(256)S(1)}, f32[160]{0:T(256)}, u32[]{:S(2)}) copy-start(f32[160]{0:T(256)} %copy-done.21) | copy-start | bytes 1924
  163.3 35.8 %collective-permute-start.5 = (bf16[160,2048]{1,0:T(8,128)(2,1)}, bf16[160,2048]{1,0:T(8,128)(2,1)}, u32[]{:S(2)}, u32[]{:S(2)}) collective-permute-start(bf16[160,2048]{1,0:T(8,128)(2,1)} %fusion.15), channel_id=1, source_target_pairs={{32,0},{33,1},{34,2},{35,3},{36,4},{37,5},{38,6},{39,7},{40,8},{41... | collective-permute-start | bytes 1966088 | tf_op jit(solution)/shard_map/ppermute | solution.py:16
  (8 other events, 10.3 us)

commit v6 on v3

--- a/solution.py
+++ b/solution.py
@@ -14,6 +14,16 @@
 
 def shift_pairs(axis, pairs):
     return lambda value: lax.ppermute(value, axis, pairs)
+
+
+def hop(value, source, target, relay):
+    if relay is None:
+        return lax.ppermute(value, "section", [(source, target)])
+    half = value.shape[0] // 2
+    direct = lax.ppermute(value[:half], "section", [(source, target)])
+    first = lax.ppermute(value[half:], "section", [(source, relay)])
+    second = lax.ppermute(first, "section", [(relay, target)])
+    return jnp.concatenate([direct, second], axis=0)
 
 
 def gather_rows(value, axis):
@@ -120,7 +130,9 @@
         tops = keep_where(tops, output, clipped, in_range)
         saved_mixed = keep_where(saved_mixed, mixed, clipped, in_range)
         senders = [s for s in range(top_section) if 0 <= moment - s < MICRO]
-        if senders:
+        if senders == [top_section - 1]:
+            received = hop(output, top_section - 1, top_section, last_section)
+        elif senders:
             received = shift_pairs("section", [(s, s + 1) for s in senders])(output)
     proj = jnp.where(spec_section, spec_proj, prog_proj)
     unit, inverse, key = embed_rows(tops.reshape(sample_rows, width), proj)
@@ -149,7 +161,9 @@
     for moment in range(MICRO + top_section):
         done = moment - 1
         senders = [s for s in range(1, top_section + 1) if 0 <= done - (top_section - s) < MICRO]
-        if senders:
+        if senders == [top_section]:
+            incoming = hop(dhidden, top_section, top_section - 1, last_section)
+        elif senders:
             incoming = shift_pairs("section", [(s, s - 1) for s in senders])(dhidden)
         micro_index = moment - backward_offset
         in_range = (micro_index >= 0) & (micro_index < MICRO)

time: 305 us -> 308 us (level)
  waiting for transfers between devices: 41.4 us -> 33.5 us
  blocking collectives: 192 us -> 197 us
  starting transfers between devices: 13.5 us -> 18.2 us
    ppermute x6 -> x4, waiting for transfers between devices: 35.5 us -> 27.6 us  [shift_pairs(): return lambda value: lax.ppermute(value, axis, pairs)]
    ppermute x0 -> x6, starting transfers between devices: none -> 6.22 us  [the longest x2 2.08 us: hop(): first = lax.ppermute(value[half:], 'section', [(source, relay)])]
    all_to_all x1, blocking collectives: 92.6 us -> 96.7 us  [gather_rows(): got = lax.all_to_all(spread, axis, 0, 0, tiled=True)]
  transfers between devices with their start and end apart: 7 -> 11, of which waited for: 3 -> 3; matrix products, arithmetic and copies ran while one was open for 0% -> 0% of each run, Pallas kernels for 0% -> 0%
where the time goes in v6:
time: 308 us; the launch traced here: 307 us
  blocking collectives  197 us (64%)
  matrix products  42.4 us (14%)
  waiting for transfers between devices  33.5 us (11%)
  starting transfers between devices  18.2 us (6%)
  other arithmetic  11.2 us (4%)
  local copies, waits for them, and re-layouts  4.39 us (1%)
    all_to_all x1, blocking collectives, local(): landed = lax.all_to_all(pieces, 'blk', 0, 0, tiled=True)  99.8 us
    all_to_all x1, blocking collectives, gather_rows(): got = lax.all_to_all(spread, axis, 0, 0, tiled=True)  96.7 us
    ppermute x4, waiting for transfers between devices, shift_pairs(): return lambda value: lax.ppermute(value, axis, pairs)  27.6 us
    dot_general x3, matrix products, layer_parts(): mixed = jnp.dot(scaled, weight, preferred_element_type=jnp.float32)  14.7 us
    dot_general x2, matrix products, layer_backward(): lax.dot_general(dmixed, weight, (((1,), (1,)), ((), ())), preferred_eleme...  9.95 us
    all_to_all x1, starting transfers between devices, gather_rows(): got = lax.all_to_all(spread, axis, 0, 0, tiled=True)  7.31 us
  transfers between devices with their start and end apart: 11, of which 3 were waited for; matrix products, arithmetic and copies ran while one was open for 0% of the time, Pallas kernels for 0%

profile of v6, /device:TPU:8, one launch (start us, length us, event | category | flops | bytes accessed | tf_op | source)
XLA Modules:
  0.0 306.8 jit_solution(17253552561482277208)
XLA Ops:
  0.0 1.1 add_select_fusion.1
  1.1 1.3 fusion.14
  2.8 2.1 fusion.29
  4.9 5.4 %fusion.32 = (bf16[160,2048]{1,0:T(8,128)(2,1)S(1)}, f32[160,2048]{1,0:T(8,128)S(1)}) fusion(bf16[160,2048]{1,0:T(8,128)(2,1)S(1)} %get-tuple-element.17, pred[]{:T(512)S(6)} %or.3, bf16[2048,2048]{1,0:T(8,128)(2,1)} %param.12, f32[2048]{0:T(1024)S(1)} %bitcast.23, f32[160]{0:T(256)S(1)} %add_rsqrt_fusion.4), kind=kOutput, calls=%fused_computation.59 | convolution fusion | flops 1346437120 | bytes 11018881 | tf_op jit(solution)/shard_map/dot_general | solution.py:41
  10.3 1.8 collective-permute-start
  12.1 1.7 collective-permute-done
  14.1 3.0 fusion.36
  17.1 0.8 fusion.92
  17.9 1.4 collective-permute-start.2
  19.3 1.4 collective-permute-start.1
  20.6 1.4 collective-permute-start.3
  22.0 3.1 %fusion.22 = (f32[160]{0:T(256)}, bf16[160,2048]{1,0:T(8,128)(2,1)}, bf16[160,2048]{1,0:T(8,128)(2,1)S(1)}) fusion(bf16[160,2048]{1,0:T(8,128)(2,1)S(1)} %get-tuple-element.9, bf16[160,2048]{1,0:T(8,128)(2,1)S(1)} %get-tuple-element.17, pred[]{:T(512)S(6)} %or.3, pred[]{:T(512)S(6)} %and.34, pred[]{:T(512)S(6)} %and.33, pred[]{:T(512)S(6)} %and.30, ...), kind=kLoop, calls=%fused_computation.49 | loop fusion | flops 3932000 | bytes 3277444 | tf_op jit(solution)/shard_map/reduce_sum | solution.py:52
  25.4 6.3 %select_select_fusion = (f32[160,2048]{1,0:T(8,128)}, f32[160,2048]{1,0:T(8,128)S(1)}) fusion(f32[160,2048]{1,0:T(8,128)S(1)} %copy-done.3, f32[160,2048]{1,0:T(8,128)S(1)} %get-tuple-element.19, pred[]{:T(512)S(6)} %and.34, pred[]{:T(512)S(6)} %and.33, pred[]{:T(512)S(6)} %and.30, bf16[2048,2048]{1,0:T(8,128)(2,1)} %param.12, ...), kind=kOutput, calls=%fused_computation.71 | convolution fusion | flops 1344471040 | bytes 14295683 | tf_op jit(solution)/shard_map/dot_general | solution.py:41
  31.8 1.2 multiply_reduce_fusion.1
  33.9 0.9 broadcast_in_dim.41
  34.8 96.7 %all_to_all.15 = bf16[32,160,768]{2,1,0:T(8,128)(2,1)S(1)} all-to-all(bf16[32,160,768]{2,1,0:T(8,128)(2,1)S(1)} %broadcast_in_dim.41), channel_id=1, replica_groups=mesh['section'=4,'blk'=32] {'blk'}, dimensions={0} | all-to-all | bytes 15728640 | tf_op jit(solution)/shard_map/all_to_all | solution.py:32
  131.5 2.8 fusion.93
  136.5 7.3 %all-to-all-start.1 = ((f32[32,160,1]{1,2,0:T(1,128)}), f32[32,160,1]{1,2,0:T(1,128)S(1)}, u32[]{:S(2)}, u32[]{:S(2)}) async-start(f32[32,160,1]{1,2,0:T(1,128)} %broadcast_in_dim.70), calls=%async_computation.1 | async-start | bytes 65536 | tf_op jit(solution)/shard_map/all_to_all | solution.py:32
  143.8 1.3 add_rsqrt_fusion.2
  145.0 5.9 %all-to-all-done.1 = f32[32,160,1]{1,2,0:T(1,128)S(1)} async-done(((f32[32,160,1]{1,2,0:T(1,128)}), f32[32,160,1]{1,2,0:T(1,128)S(1)}, u32[]{:S(2)}, u32[]{:S(2)}) %all-to-all-start.1) | async-done | bytes 20512 | tf_op jit(solution)/shard_map/all_to_all | solution.py:32
  151.0 0.7 reduce
  151.7 0.8 broadcast_in_dim.71
  152.5 5.1 %multiply_reduce_fusion = (f32[160]{0:T(256)S(1)}, f32[160,768]{1,0:T(8,128)S(1)}) fusion(f32[160,768]{1,0:T(8,128)} %copy-done.4, f32[160]{0:T(256)} %copy-done.11, bf16[160,768]{1,0:T(8,128)(2,1)S(1)} %collective-permute-done.4, bf16[5120,768]{1,0:T(8,128)(2,1)} %bitcast.16, f32[160,5120]{1,0:T(8,128)S(1)} %get-tuple-element.27, ...), kind=kOutput, calls=%fused_computation.109 | convolution fusion | flops 1261485952 | bytes 12392321 | tf_op jit(solution)/shard_map/dot_general | solution.py:152
  157.9 1.3 convolution_convert_fusion.1
  159.4 6.8 %fusion.16 = (f32[160]{0:T(256)S(1)}, f32[160,2048]{1,0:T(8,128)S(1)}) fusion(bf16[160,2048]{1,0:T(8,128)(2,1)S(1)} %copy-done.1, f32[160]{0:T(256)S(1)} %copy-done.10, f32[2048]{0:T(1024)S(1)} %bitcast.26, bf16[2048,2048]{1,0:T(8,128)(2,1)} %param.12, f32[160,2048]{1,0:T(8,128)S(1)} %copy-done.2, bf16[160,2048]{1,0:T(8,128)(2,1)S(1)} %convolution_convert_fusion.1, ...), kind=kOutput, calls=%fused_computation.43 | convolution fusion | flops 1347420032 | bytes 12330241 | tf_op jit(solution)/shard_map/dot_general | solution.py:59
  166.8 0.7 collective-permute-start.7
  168.9 3.1 %fusion.19 = (f32[160]{0:T(256)S(1)}, f32[160,2048]{1,0:T(8,128)S(1)}) fusion(bf16[160,2048]{1,0:T(8,128)(2,1)S(1)} %copy-done.1, f32[160]{0:T(256)S(1)} %copy-done.10, f32[2048]{0:T(1024)S(1)} %bitcast.27, bf16[2048,2048]{1,0:T(8,128)(2,1)S(1)} %bitcast.20, f32[160,2048]{1,0:T(8,128)S(1)} %copy-done.2, ...), kind=kOutput, calls=%fused_computation.46 | convolution fusion | flops 1348730752 | bytes 12985601 | tf_op jit(solution)/shard_map/dot_general | solution.py:59
  172.5 1.5 collective-permute-start.9
  174.0 25.9 %collective-permute-done.9 = bf16[160,2048]{1,0:T(8,128)(2,1)} collective-permute-done((bf16[160,2048]{1,0:T(8,128)(2,1)S(1)}, bf16[160,2048]{1,0:T(8,128)(2,1)}, u32[]{:S(2)}, u32[]{:S(2)}) %collective-permute-start.9) | collective-permute-done | bytes 655392 | tf_op jit(solution)/shard_map/ppermute | solution.py:16
  199.9 4.0 %convolution_convert_fusion = bf16[2048,2048]{1,0:T(8,128)(2,1)S(1)} fusion(bf16[160,2048]{1,0:T(8,128)(2,1)S(1)} %copy-done.1, f32[160,2048]{1,0:T(8,128)S(1)} %copy-done.2, bf16[160,2048]{1,0:T(8,128)(2,1)S(1)} %convolution_convert_fusion.1, bf16[160,2048]{1,0:T(8,128)(2,1)} %collective-permute-done.9, f32[160]{0:T(256)S(1)} %copy-done.10, ...), kind=kOutput, calls=%fused_computation.1 | convolution fusion | flops 1357840384 | bytes 12329604 | tf_op jit(solution)/shard_map/dot_general | solution.py:181
  204.0 99.8 %all_to_all.16 = bf16[32,64,2048]{2,1,0:T(8,128)(2,1)S(1)} all-to-all(bf16[32,64,2048]{2,1,0:T(8,128)(2,1)S(1)} %bitcast.21), channel_id=1, replica_groups=mesh['section'=4,'blk'=32] {'blk'}, dimensions={0} | all-to-all | bytes 16777216 | tf_op jit(solution)/shard_map/all_to_all | solution.py:186
  303.8 2.9 convert_reduce_fusion
  (78 shorter events, 6.7 us)
Async XLA Ops:
  2.8 2.1 copy-start.8
  4.9 9.2 %slice-start = ((s8[8388608]{0:T(1024)(128)(4,1)}), s8[4194304]{0:T(1024)(128)(4,1)S(1)}, s32[]{:S(2)}) async-start(s8[8388608]{0:T(1024)(128)(4,1)} %bitcast.17), calls=%async_computation.3 | async-start | bytes 8388608
  4.9 9.2 %slice-start.1 = ((s8[8388608]{0:T(1024)(128)(4,1)}), s8[4194304]{0:T(1024)(128)(4,1)S(1)}, s32[]{:S(2)}) async-start(s8[8388608]{0:T(1024)(128)(4,1)} %bitcast.17), calls=%async_computation.4 | async-start | bytes 8388608
  10.3 1.8 copy-start.18
  10.3 3.5 %collective-permute-start = (bf16[160,2048]{1,0:T(8,128)(2,1)S(1)}, bf16[160,2048]{1,0:T(8,128)(2,1)S(1)}, u32[]{:S(2)}, u32[]{:S(2)}) collective-permute-start(bf16[160,2048]{1,0:T(8,128)(2,1)S(1)} %get-tuple-element.18), channel_id=1, source_target_pairs={{0,32},{1,33},{2,34},{3,35},{4,36},{5,37},{6,38},{7,39},{8,40},{9,... | collective-permute-start | bytes 1966088 | tf_op jit(solution)/shard_map/ppermute | solution.py:16
  17.9 2.8 collective-permute-start.2
  19.3 2.8 collective-permute-start.1
  20.6 1.4 collective-permute-start.3
  22.0 3.4 %copy-start.3 = (f32[160,2048]{1,0:T(8,128)S(1)}, f32[160,2048]{1,0:T(8,128)}, u32[]{:S(2)}) copy-start(f32[160,2048]{1,0:T(8,128)} %get-tuple-element.21) | copy-start | bytes 3932164
  25.4 6.4 %copy-start.14 = (bf16[2048,768]{1,0:T(8,128)(2,1)S(1)}, bf16[2048,768]{1,0:T(8,128)(2,1)}, u32[]{:S(2)}) copy-start(bf16[2048,768]{1,0:T(8,128)(2,1)} %param.15) | copy-start | bytes 9437188
  25.4 6.4 %copy-start.16 = (bf16[2048,768]{1,0:T(8,128)(2,1)S(1)}, bf16[2048,768]{1,0:T(8,128)(2,1)}, u32[]{:S(2)}) copy-start(bf16[2048,768]{1,0:T(8,128)(2,1)} %param.14) | copy-start | bytes 9437188
  25.4 6.3 %copy-start.19 = (bf16[160,2048]{1,0:T(8,128)(2,1)S(1)}, bf16[160,2048]{1,0:T(8,128)(2,1)}, u32[]{:S(2)}) copy-start(bf16[160,2048]{1,0:T(8,128)(2,1)} %copy-done.18) | copy-start | bytes 1966084
  33.2 0.7 collective-permute-start.4
  131.5 3.0 copy-start
  135.1 1.3 copy-start.13
  135.1 0.7 collective-permute-start.5
  136.5 14.5 %all-to-all-start.1 = ((f32[32,160,1]{1,2,0:T(1,128)}), f32[32,160,1]{1,2,0:T(1,128)S(1)}, u32[]{:S(2)}, u32[]{:S(2)}) async-start(f32[32,160,1]{1,2,0:T(1,128)} %broadcast_in_dim.70), calls=%async_computation.1 | async-start | bytes 65536 | tf_op jit(solution)/shard_map/all_to_all | solution.py:32
  152.5 5.2 %copy-start.5 = (f32[160,768]{1,0:T(8,128)S(1)}, f32[160,768]{1,0:T(8,128)}, u32[]{:S(2)}) copy-start(f32[160,768]{1,0:T(8,128)} %copy-done.4) | copy-start | bytes 1474564
  152.5 5.2 %copy-start.12 = (f32[160]{0:T(256)S(1)}, f32[160]{0:T(256)}, u32[]{:S(2)}) copy-start(f32[160]{0:T(256)} %copy-done.11) | copy-start | bytes 1924
  152.5 5.2 %copy-start.15 = (bf16[2048,768]{1,0:T(8,128)(2,1)S(1)}, bf16[2048,768]{1,0:T(8,128)(2,1)}, u32[]{:S(2)}) copy-start(bf16[2048,768]{1,0:T(8,128)(2,1)} %param.15) | copy-start | bytes 9437188
  152.5 5.4 %copy-start.17 = (bf16[2048,768]{1,0:T(8,128)(2,1)S(1)}, bf16[2048,768]{1,0:T(8,128)(2,1)}, u32[]{:S(2)}) copy-start(bf16[2048,768]{1,0:T(8,128)(2,1)} %param.14) | copy-start | bytes 9437188
  157.9 1.5 copy-start.2
  157.9 1.5 copy-start.9
  157.9 1.5 copy-start.10
  157.9 11.0 %slice-start.2 = ((s8[8388608]{0:T(1024)(128)(4,1)}), s8[4194304]{0:T(1024)(128)(4,1)S(1)}, s32[]{:S(2)}) async-start(s8[8388608]{0:T(1024)(128)(4,1)} %bitcast.19), calls=%async_computation.5 | async-start | bytes 8388608
  159.4 9.5 %slice-start.3 = ((s8[8388608]{0:T(1024)(128)(4,1)}), s8[4194304]{0:T(1024)(128)(4,1)S(1)}, s32[]{:S(2)}) async-start(s8[8388608]{0:T(1024)(128)(4,1)} %bitcast.19), calls=%async_computation.6 | async-start | bytes 8388608
  166.8 1.4 collective-permute-start.7
  167.5 1.4 collective-permute-start.6
  168.2 0.7 collective-permute-start.8
  168.9 3.2 %copy-start.6 = (bf16[80,2048]{1,0:T(8,128)(2,1)}, bf16[80,2048]{1,0:T(8,128)(2,1)S(1)}, u32[]{:S(2)}) copy-start(bf16[80,2048]{1,0:T(8,128)(2,1)S(1)} %collective-permute-done.6) | copy-start | bytes 983044
  168.9 3.1 %copy-start.7 = (bf16[80,2048]{1,0:T(8,128)(2,1)}, bf16[80,2048]{1,0:T(8,128)(2,1)S(1)}, u32[]{:S(2)}) copy-start(bf16[80,2048]{1,0:T(8,128)(2,1)S(1)} %collective-permute-done.8) | copy-start | bytes 983044
  172.5 27.4 %collective-permute-start.9 = (bf16[160,2048]{1,0:T(8,128)(2,1)S(1)}, bf16[160,2048]{1,0:T(8,128)(2,1)}, u32[]{:S(2)}, u32[]{:S(2)}) collective-permute-start(bf16[160,2048]{1,0:T(8,128)(2,1)S(1)} %fusion.28), channel_id=1, source_target_pairs={{32,0},{33,1},{34,2},{35,3},{36,4},{37,5},{38,6},{39,7},{40,8},{41... | collective-permute-start | bytes 1966088 | tf_op jit(solution)/shard_map/ppermute | solution.py:16
  (3 other events, 2.9 us)

commit v7 on v3

--- a/solution.py
+++ b/solution.py
@@ -105,7 +105,7 @@
     blank = jnp.zeros((MICRO, micro_rows, width), jnp.bfloat16)
     saved_inputs = blank
     tops = blank
-    saved_mixed = jnp.zeros((MICRO, micro_rows, width), jnp.float32)
+    mixed_steps = []
     received = jnp.zeros((micro_rows, width), jnp.bfloat16)
     forward_offset = jnp.where(spec_section, 0, section_index)
     takes_bag = spec_section | (section_index == 0)
@@ -118,7 +118,7 @@
         saved_inputs = keep_where(saved_inputs, current, clipped, in_range)
         output, mixed = layer_forward(current, layer_weights, gain)
         tops = keep_where(tops, output, clipped, in_range)
-        saved_mixed = keep_where(saved_mixed, mixed, clipped, in_range)
+        mixed_steps.append((in_range, clipped, mixed))
         senders = [s for s in range(top_section) if 0 <= moment - s < MICRO]
         if senders:
             received = shift_pairs("section", [(s, s + 1) for s in senders])(output)
@@ -158,7 +158,9 @@
             starts_grad, lax.dynamic_index_in_dim(top_grad, clipped, 0, keepdims=False), incoming
         )
         hidden = lax.dynamic_index_in_dim(saved_inputs, clipped, 0, keepdims=False)
-        mixed = lax.dynamic_index_in_dim(saved_mixed, clipped, 0, keepdims=False)
+        mixed = jnp.zeros((micro_rows, width), jnp.float32)
+        for kept, step_index, step_mixed in mixed_steps:
+            mixed = jnp.where(kept & (step_index == clipped), step_mixed, mixed)
         dhidden, scaled, dmixed = layer_backward(hidden, upstream, layer_weights, gain, mixed)
         saved_scaled = keep_where(saved_scaled, scaled, clipped, in_range)
         saved_dmixed = keep_where(saved_dmixed, dmixed, clipped, in_range)

time: 305 us -> 353 us (1.16)
  waiting for transfers between devices: 41.4 us -> 158 us
  blocking collectives: 192 us -> 99.9 us
  starting transfers between devices: 13.5 us -> 23.7 us
  matrix products: 42.4 us -> 50.7 us
  local copies, waits for them, and re-layouts: 3.58 us -> 8.76 us
    all_to_all x1 -> x2, waiting for transfers between devices: 5.96 us -> 111 us  [gather_rows(): got = lax.all_to_all(spread, axis, 0, 0, tiled=True)]
    all_to_all x1 -> x0, blocking collectives: 92.6 us -> none  [gather_rows(): got = lax.all_to_all(spread, axis, 0, 0, tiled=True)]
    ppermute x6, waiting for transfers between devices: 35.5 us -> 47.9 us  [shift_pairs(): return lambda value: lax.ppermute(value, axis, pairs)]
    all_to_all x1 -> x2, starting transfers between devices: 7.48 us -> 17.7 us  [gather_rows(): got = lax.all_to_all(spread, axis, 0, 0, tiled=True)]
    dot_general x2, matrix products: 9.95 us -> 13.6 us  [layer_backward(): lax.dot_general(dmixed, weight, (((1,), (1,)), ((), ())), preferred_eleme...]
  transfers between devices with their start and end apart: 7 -> 8, of which waited for: 3 -> 4; matrix products, arithmetic and copies ran while one was open for 0% -> 0% of each run, Pallas kernels for 0% -> 0%
where the time goes in v7:
time: 353 us; the launch traced here: 352 us
  waiting for transfers between devices  158 us (45%)
  blocking collectives  99.9 us (28%)
  matrix products  50.7 us (14%)
  starting transfers between devices  23.7 us (7%)
  other arithmetic  10 us (3%)
  local copies, waits for them, and re-layouts  8.76 us (2%)
    all_to_all x2, waiting for transfers between devices, gather_rows(): got = lax.all_to_all(spread, axis, 0, 0, tiled=True)  111 us
    all_to_all x1, blocking collectives, local(): landed = lax.all_to_all(pieces, 'blk', 0, 0, tiled=True)  99.9 us
    ppermute x6, waiting for transfers between devices, shift_pairs(): return lambda value: lax.ppermute(value, axis, pairs)  47.9 us
    all_to_all x2, starting transfers between devices, gather_rows(): got = lax.all_to_all(spread, axis, 0, 0, tiled=True)  17.7 us
    dot_general x3, matrix products, layer_parts(): mixed = jnp.dot(scaled, weight, preferred_element_type=jnp.float32)  14.5 us
    dot_general x2, matrix products, layer_backward(): lax.dot_general(dmixed, weight, (((1,), (1,)), ((), ())), preferred_eleme...  13.6 us
  transfers between devices with their start and end apart: 8, of which 4 were waited for; matrix products, arithmetic and copies ran while one was open for 0% of the time, Pallas kernels for 0%

profile of v7, /device:TPU:8, one launch (start us, length us, event | category | flops | bytes accessed | tf_op | source)
XLA Modules:
  0.0 352.1 jit_solution(11227051663569943301)
XLA Ops:
  0.0 1.1 add_select_fusion.1
  1.1 1.3 fusion.14
  2.8 2.1 fusion.29
  4.9 6.4 %fusion.32 = (bf16[160,2048]{1,0:T(8,128)(2,1)S(1)}, f32[160,2048]{1,0:T(8,128)}) fusion(bf16[160,2048]{1,0:T(8,128)(2,1)S(1)} %get-tuple-element.13, pred[]{:T(512)S(6)} %or.3, bf16[2048,2048]{1,0:T(8,128)(2,1)} %param.12, f32[2048]{0:T(1024)S(1)} %bitcast.21, f32[160]{0:T(256)S(1)} %add_rsqrt_fusion.4), kind=kOutput, calls=%fused_computation.59 | convolution fusion | flops 1346437120 | bytes 11018881 | tf_op jit(solution)/shard_map/dot_general | solution.py:31
  11.3 1.8 collective-permute-start
  13.1 1.7 collective-permute-done
  15.1 3.0 fusion.36
  18.1 0.7 collective-permute-start.1
  18.8 2.0 fusion.22
  21.0 5.1 %fusion.45 = f32[160,2048]{1,0:T(8,128)S(1)} fusion(bf16[2048,2048]{1,0:T(8,128)(2,1)} %param.12, bf16[160,2048]{1,0:T(8,128)(2,1)S(1)} %get-tuple-element.7, f32[160]{0:T(256)S(1)} %add_rsqrt_fusion.1, f32[2048]{0:T(1024)S(1)} %bitcast.23), kind=kOutput, calls=%fused_computation.74 | convolution fusion | flops 1343488000 | bytes 10363520 | tf_op jit(solution)/shard_map/dot_general | solution.py:31
  26.3 1.3 multiply_reduce_fusion.1
  27.6 0.7 copy-done.1
  29.2 0.7 copy-done.3
  29.9 4.0 %broadcast_in_dim.37 = bf16[32,160,768]{2,1,0:T(8,128)(2,1)} broadcast(bf16[160,768]{1,0:T(8,128)(2,1)S(1)} %collective-permute-done.2), dimensions={1,2} | broadcast | bytes 8110080 | tf_op jit(solution)/shard_map/broadcast_in_dim | solution.py:21
  33.9 9.6 %all-to-all-start = ((bf16[32,160,768]{2,1,0:T(8,128)(2,1)}), bf16[32,160,768]{2,1,0:T(8,128)(2,1)}, u32[]{:S(2)}, u32[]{:S(2)}) async-start(bf16[32,160,768]{2,1,0:T(8,128)(2,1)} %broadcast_in_dim.37), calls=%async_computation | async-start | bytes 15728640 | tf_op jit(solution)/shard_map/all_to_all | solution.py:22
  43.5 104.6 %all-to-all-done = bf16[32,160,768]{2,1,0:T(8,128)(2,1)} async-done(((bf16[32,160,768]{2,1,0:T(8,128)(2,1)}), bf16[32,160,768]{2,1,0:T(8,128)(2,1)}, u32[]{:S(2)}, u32[]{:S(2)}) %all-to-all-start) | async-done | bytes 7864352 | tf_op jit(solution)/shard_map/all_to_all | solution.py:22
  148.0 6.0 %fusion.96 = (f32[160]{0:T(256)S(1)}, f32[160,5120]{1,0:T(8,128)S(1)}) fusion(bf16[160,768]{1,0:T(8,128)(2,1)S(1)} %multiply_convert_fusion.3, bf16[5120,768]{1,0:T(8,128)(2,1)} %bitcast.2), kind=kOutput, calls=%fused_computation.141 | convolution fusion | flops 1259929472 | bytes 11387520 | tf_op jit(solution)/shard_map/dot_general | solution.py:130
  156.1 8.1 %all-to-all-start.1 = ((f32[32,160,1]{1,2,0:T(1,128)}), f32[32,160,1]{1,2,0:T(1,128)S(1)}, u32[]{:S(2)}, u32[]{:S(2)}) async-start(f32[32,160,1]{1,2,0:T(1,128)} %broadcast_in_dim.65), calls=%async_computation.1 | async-start | bytes 65536 | tf_op jit(solution)/shard_map/all_to_all | solution.py:22
  164.2 1.2 add_rsqrt_fusion.2
  165.4 6.0 %all-to-all-done.1 = f32[32,160,1]{1,2,0:T(1,128)S(1)} async-done(((f32[32,160,1]{1,2,0:T(1,128)}), f32[32,160,1]{1,2,0:T(1,128)S(1)}, u32[]{:S(2)}, u32[]{:S(2)}) %all-to-all-start.1) | async-done | bytes 20512 | tf_op jit(solution)/shard_map/all_to_all | solution.py:22
  171.4 0.7 reduce
  172.1 0.8 broadcast_in_dim.66
  173.0 5.1 %multiply_reduce_fusion = (f32[160]{0:T(256)S(1)}, f32[160,768]{1,0:T(8,128)S(1)}) fusion(f32[160,768]{1,0:T(8,128)} %copy-done.1, f32[160]{0:T(256)} %copy-done.6, bf16[160,768]{1,0:T(8,128)(2,1)S(1)} %copy-done.4, bf16[5120,768]{1,0:T(8,128)(2,1)} %bitcast.2, f32[160,5120]{1,0:T(8,128)S(1)} %get-tuple-element.21, f32[5120]{0:T(1024)S(1)} %broadcast_in_dim.66, ...), kind=kOutput, calls=%fused_computation.110 | convolution fusion | flops 1261485952 | bytes 12392321 | tf_op jit(solution)/shard_map/dot_general | solution.py:140
  178.4 1.3 convolution_convert_fusion.1
  180.7 6.6 %fusion.16 = (f32[160]{0:T(256)S(1)}, f32[160,2048]{1,0:T(8,128)S(1)}) fusion(bf16[160,2048]{1,0:T(8,128)(2,1)S(1)} %copy-done, f32[160]{0:T(256)S(1)} %copy-done.5, f32[2048]{0:T(1024)S(1)} %bitcast.24, bf16[2048,2048]{1,0:T(8,128)(2,1)} %param.12, f32[160,2048]{1,0:T(8,128)S(1)} %copy-done.17, f32[160,2048]{1,0:T(8,128)S(1)} %copy-done.19, ...), kind=kOutput, calls=%fused_computation.43 | convolution fusion | flops 1348403072 | bytes 14951684 | tf_op jit(solution)/shard_map/dot_general | solution.py:49
  187.7 0.7 collective-permute-start.4
  188.5 7.0 %fusion.19 = (f32[160]{0:T(256)S(1)}, f32[160,2048]{1,0:T(8,128)S(1)}) fusion(bf16[160,2048]{1,0:T(8,128)(2,1)S(1)} %copy-done, f32[160]{0:T(256)S(1)} %copy-done.5, f32[2048]{0:T(1024)S(1)} %bitcast.25, bf16[2048,2048]{1,0:T(8,128)(2,1)} %param.12, f32[160,2048]{1,0:T(8,128)} %copy-done.16, f32[160,2048]{1,0:T(8,128)} %get-tuple-element.17, ...), kind=kOutput, calls=%fused_computation.46 | convolution fusion | flops 1348403072 | bytes 15607044 | tf_op jit(solution)/shard_map/dot_general | solution.py:49
  195.9 1.5 collective-permute-start.5
  197.5 46.2 %collective-permute-done.5 = bf16[160,2048]{1,0:T(8,128)(2,1)S(1)} collective-permute-done((bf16[160,2048]{1,0:T(8,128)(2,1)S(1)}, bf16[160,2048]{1,0:T(8,128)(2,1)S(1)}, u32[]{:S(2)}, u32[]{:S(2)}) %collective-permute-start.5) | collective-permute-done | bytes 655392 | tf_op jit(solution)/shard_map/ppermute | solution.py:16
  243.7 5.6 %convolution_convert_fusion = bf16[2048,2048]{1,0:T(8,128)(2,1)S(1)} fusion(bf16[160,2048]{1,0:T(8,128)(2,1)S(1)} %copy-done, f32[160,2048]{1,0:T(8,128)} %copy-done.16, f32[160,2048]{1,0:T(8,128)} %get-tuple-element.17, f32[160,2048]{1,0:T(8,128)} %get-tuple-element.15, bf16[160,2048]{1,0:T(8,128)(2,1)S(1)} %convolution_convert_fusion.1, ...), kind=kOutput, calls=%fused_computation.1 | convolution fusion | flops 1363410944 | bytes 14951053 | tf_op jit(solution)/shard_map/dot_general | solution.py:169
  249.3 99.9 %all_to_all.15 = bf16[32,64,2048]{2,1,0:T(8,128)(2,1)S(1)} all-to-all(bf16[32,64,2048]{2,1,0:T(8,128)(2,1)S(1)} %bitcast.15), channel_id=1, replica_groups=mesh['section'=4,'blk'=32] {'blk'}, dimensions={0} | all-to-all | bytes 16777216 | tf_op jit(solution)/shard_map/all_to_all | solution.py:174
  349.1 3.0 convert_reduce_fusion
  (64 shorter events, 5.9 us)
Async XLA Ops:
  1.1 1.7 copy-start.13
  2.8 2.1 copy-start.14
  4.9 10.2 %slice-start = ((s8[8388608]{0:T(1024)(128)(4,1)}), s8[4194304]{0:T(1024)(128)(4,1)S(1)}, s32[]{:S(2)}) async-start(s8[8388608]{0:T(1024)(128)(4,1)} %bitcast.19), calls=%async_computation.3 | async-start | bytes 8388608
  4.9 10.2 %slice-start.1 = ((s8[8388608]{0:T(1024)(128)(4,1)}), s8[4194304]{0:T(1024)(128)(4,1)S(1)}, s32[]{:S(2)}) async-start(s8[8388608]{0:T(1024)(128)(4,1)} %bitcast.19), calls=%async_computation.4 | async-start | bytes 8388608
  11.3 3.4 collective-permute-start
  18.1 0.7 collective-permute-start.1
  21.0 5.2 %copy-start.9 = (bf16[2048,768]{1,0:T(8,128)(2,1)S(1)}, bf16[2048,768]{1,0:T(8,128)(2,1)}, u32[]{:S(2)}) copy-start(bf16[2048,768]{1,0:T(8,128)(2,1)} %param.15) | copy-start | bytes 9437188
  21.0 5.2 %copy-start.11 = (bf16[2048,768]{1,0:T(8,128)(2,1)S(1)}, bf16[2048,768]{1,0:T(8,128)(2,1)}, u32[]{:S(2)}) copy-start(bf16[2048,768]{1,0:T(8,128)(2,1)} %param.14) | copy-start | bytes 9437188
  26.3 1.3 copy-start.16
  27.6 0.8 copy-start.1
  27.6 0.9 copy-start.6
  28.5 0.7 collective-permute-start.2
  29.2 0.7 copy-start.3
  33.9 114.1 %all-to-all-start = ((bf16[32,160,768]{2,1,0:T(8,128)(2,1)}), bf16[32,160,768]{2,1,0:T(8,128)(2,1)}, u32[]{:S(2)}, u32[]{:S(2)}) async-start(bf16[32,160,768]{2,1,0:T(8,128)(2,1)} %broadcast_in_dim.37), calls=%async_computation | async-start | bytes 15728640 | tf_op jit(solution)/shard_map/all_to_all | solution.py:22
  154.1 18.8 %copy-start.4 = (bf16[160,768]{1,0:T(8,128)(2,1)S(1)}, bf16[160,768]{1,0:T(8,128)(2,1)}, u32[]{:S(2)}) copy-start(bf16[160,768]{1,0:T(8,128)(2,1)} %copy-done.3) | copy-start | bytes 737284
  154.7 1.4 copy-start.8
  154.7 0.7 collective-permute-start.3
  156.1 15.3 %all-to-all-start.1 = ((f32[32,160,1]{1,2,0:T(1,128)}), f32[32,160,1]{1,2,0:T(1,128)S(1)}, u32[]{:S(2)}, u32[]{:S(2)}) async-start(f32[32,160,1]{1,2,0:T(1,128)} %broadcast_in_dim.65), calls=%async_computation.1 | async-start | bytes 65536 | tf_op jit(solution)/shard_map/all_to_all | solution.py:22
  172.9 5.2 %copy-start.2 = (f32[160,768]{1,0:T(8,128)S(1)}, f32[160,768]{1,0:T(8,128)}, u32[]{:S(2)}) copy-start(f32[160,768]{1,0:T(8,128)} %copy-done.1) | copy-start | bytes 1474564
  172.9 5.2 %copy-start.7 = (f32[160]{0:T(256)S(1)}, f32[160]{0:T(256)}, u32[]{:S(2)}) copy-start(f32[160]{0:T(256)} %copy-done.6) | copy-start | bytes 1924
  173.0 5.2 %copy-start.10 = (bf16[2048,768]{1,0:T(8,128)(2,1)S(1)}, bf16[2048,768]{1,0:T(8,128)(2,1)}, u32[]{:S(2)}) copy-start(bf16[2048,768]{1,0:T(8,128)(2,1)} %param.15) | copy-start | bytes 9437188
  173.0 5.4 %copy-start.12 = (bf16[2048,768]{1,0:T(8,128)(2,1)S(1)}, bf16[2048,768]{1,0:T(8,128)(2,1)}, u32[]{:S(2)}) copy-start(bf16[2048,768]{1,0:T(8,128)(2,1)} %param.14) | copy-start | bytes 9437188
  178.3 1.3 copy-start
  178.3 1.3 copy-start.5
  178.3 1.3 copy-start.15
  178.3 1.5 copy-start.17
  178.3 1.9 copy-start.18
  178.4 2.3 copy-start.19
  187.7 0.7 collective-permute-start.4
  195.9 47.8 %collective-permute-start.5 = (bf16[160,2048]{1,0:T(8,128)(2,1)S(1)}, bf16[160,2048]{1,0:T(8,128)(2,1)S(1)}, u32[]{:S(2)}, u32[]{:S(2)}) collective-permute-start(bf16[160,2048]{1,0:T(8,128)(2,1)S(1)} %fusion.28), channel_id=1, source_target_pairs={{32,0},{33,1},{34,2},{35,3},{36,4},{37,5},{38,6},{39,7},{40,8},{41... | collective-permute-start | bytes 1966088 | tf_op jit(solution)/shard_map/ppermute | solution.py:16

commit v8 on v3

--- a/solution.py
+++ b/solution.py
@@ -133,6 +133,7 @@
     row_max = jnp.max(scores, axis=1, keepdims=True)
     lse = row_max + jnp.log(jnp.sum(jnp.exp(scores - row_max), axis=1, keepdims=True))
     lse_down = shift_pairs("section", [(last_section, top_section)])(lse)
+    lse_down, unit, inverse = lax.optimization_barrier((lse_down, unit, inverse))
     lse_all = gather_rows(lse_down, "blk").reshape(1, -1)
     shift = jnp.where(spec_section, lse, lse_all)
     probs = jnp.exp(scores - shift).astype(jnp.bfloat16)

time: 305 us -> 306 us (level)
  no operation moved by 1% of the time
where the time goes in v8:
time: 306 us
  blocking collectives  192 us (63%)
  matrix products  42.4 us (14%)
  waiting for transfers between devices  41.4 us (14%)
  starting transfers between devices  13.5 us (4%)
  other arithmetic  11.7 us (4%)
  local copies, waits for them, and re-layouts  3.6 us (1%)
    all_to_all x1, blocking collectives, local(): landed = lax.all_to_all(pieces, 'blk', 0, 0, tiled=True)  99.8 us
    all_to_all x1, blocking collectives, gather_rows(): got = lax.all_to_all(spread, axis, 0, 0, tiled=True)  92.6 us
    ppermute x6, waiting for transfers between devices, shift_pairs(): return lambda value: lax.ppermute(value, axis, pairs)  35.5 us
    dot_general x3, matrix products, layer_parts(): mixed = jnp.dot(scaled, weight, preferred_element_type=jnp.float32)  14.8 us
    dot_general x2, matrix products, layer_backward(): lax.dot_general(dmixed, weight, (((1,), (1,)), ((), ())), preferred_eleme...  9.94 us
    all_to_all x1, starting transfers between devices, gather_rows(): got = lax.all_to_all(spread, axis, 0, 0, tiled=True)  7.48 us
  transfers between devices with their start and end apart: 7, of which 3 were waited for; matrix products, arithmetic and copies ran while one was open for 0% of the time, Pallas kernels for 0%

profile of v8, /device:TPU:8, one launch (start us, length us, event | category | flops | bytes accessed | tf_op | source)
XLA Modules:
  0.0 305.5 jit_solution(11002393586333730645)
XLA Ops:
  0.0 1.1 add_select_fusion.1
  1.1 1.3 fusion.14
  2.8 2.1 fusion.29
  4.9 5.4 %fusion.32 = (bf16[160,2048]{1,0:T(8,128)(2,1)S(1)}, f32[160,2048]{1,0:T(8,128)S(1)}) fusion(bf16[160,2048]{1,0:T(8,128)(2,1)S(1)} %get-tuple-element.21, pred[]{:T(512)S(6)} %or.3, bf16[2048,2048]{1,0:T(8,128)(2,1)} %param.12, f32[2048]{0:T(1024)S(1)} %bitcast.25, f32[160]{0:T(256)S(1)} %add_rsqrt_fusion.4), kind=kOutput, calls=%fused_computation.59 | convolution fusion | flops 1346437120 | bytes 11018881 | tf_op jit(solution)/shard_map/dot_general | solution.py:31
  10.3 1.8 collective-permute-start
  12.1 1.7 collective-permute-done
  14.1 3.2 %fusion.36 = (bf16[160,2048]{1,0:T(8,128)(2,1)}, f32[160,2048]{1,0:T(8,128)}) fusion(bf16[160,2048]{1,0:T(8,128)(2,1)S(1)} %get-tuple-element.17, bf16[2048,2048]{1,0:T(8,128)(2,1)S(1)} %bitcast.20, f32[160]{0:T(256)S(1)} %add_rsqrt_fusion.3, f32[2048]{0:T(1024)S(1)} %bitcast.26), kind=kOutput, calls=%fused_computation.63 | convolution fusion | flops 1345781760 | bytes 11018880 | tf_op jit(solution)/shard_map/dot_general | solution.py:31
  17.3 0.7 collective-permute-start.1
  18.0 2.0 fusion.22
  20.3 6.3 %select_select_fusion = (f32[160,2048]{1,0:T(8,128)}, f32[160,2048]{1,0:T(8,128)S(1)}) fusion(f32[160,2048]{1,0:T(8,128)S(1)} %copy-done.4, f32[160,2048]{1,0:T(8,128)S(1)} %get-tuple-element.23, pred[]{:T(512)S(6)} %and.34, pred[]{:T(512)S(6)} %and.33, pred[]{:T(512)S(6)} %and.30, bf16[2048,2048]{1,0:T(8,128)(2,1)} %param.12, ...), kind=kOutput, calls=%fused_computation.71 | convolution fusion | flops 1344471040 | bytes 14295683 | tf_op jit(solution)/shard_map/dot_general | solution.py:31
  26.6 1.3 multiply_reduce_fusion.1
  27.9 0.9 fusion.91
  28.8 0.7 collective-permute-start.2
  29.5 0.9 broadcast_in_dim.41
  30.4 92.6 %all_to_all.15 = bf16[32,160,768]{2,1,0:T(8,128)(2,1)S(1)} all-to-all(bf16[32,160,768]{2,1,0:T(8,128)(2,1)S(1)} %broadcast_in_dim.41), channel_id=1, replica_groups=mesh['section'=4,'blk'=32] {'blk'}, dimensions={0} | all-to-all | bytes 15728640 | tf_op jit(solution)/shard_map/all_to_all | solution.py:22
  123.0 2.8 fusion.92
  127.9 7.5 %all-to-all-start.1 = ((f32[32,160,1]{1,2,0:T(1,128)}), f32[32,160,1]{1,2,0:T(1,128)S(1)}, u32[]{:S(2)}, u32[]{:S(2)}) async-start(f32[32,160,1]{1,2,0:T(1,128)} %broadcast_in_dim.70), calls=%async_computation.1 | async-start | bytes 65536 | tf_op jit(solution)/shard_map/all_to_all | solution.py:22
  135.4 1.2 add_rsqrt_fusion.2
  136.7 6.0 %all-to-all-done.1 = f32[32,160,1]{1,2,0:T(1,128)S(1)} async-done(((f32[32,160,1]{1,2,0:T(1,128)}), f32[32,160,1]{1,2,0:T(1,128)S(1)}, u32[]{:S(2)}, u32[]{:S(2)}) %all-to-all-start.1) | async-done | bytes 20512 | tf_op jit(solution)/shard_map/all_to_all | solution.py:22
  142.6 0.7 reduce
  143.3 0.8 broadcast_in_dim.71
  144.2 5.1 %multiply_reduce_fusion = (f32[160]{0:T(256)S(1)}, f32[160,768]{1,0:T(8,128)S(1)}) fusion(f32[160,768]{1,0:T(8,128)} %get-tuple-element.10, bf16[160,768]{1,0:T(8,128)(2,1)S(1)} %collective-permute-done.2, bf16[5120,768]{1,0:T(8,128)(2,1)} %bitcast.18, f32[160,5120]{1,0:T(8,128)S(1)} %get-tuple-element.31, f32[5120]{0:T(1024)S(1)} %broadcast_in_dim.71, ...), kind=kOutput, calls=%fused_computation.109 | convolution fusion | flops 1261363072 | bytes 12391681 | tf_op jit(solution)/shard_map/dot_general | solution.py:141
  149.6 1.2 convolution_convert_fusion.1
  151.1 6.8 %fusion.16 = (f32[160]{0:T(256)S(1)}, f32[160,2048]{1,0:T(8,128)S(1)}) fusion(bf16[160,2048]{1,0:T(8,128)(2,1)S(1)} %copy-done.1, f32[160]{0:T(256)S(1)} %copy-done.7, f32[2048]{0:T(1024)S(1)} %bitcast.28, bf16[2048,2048]{1,0:T(8,128)(2,1)} %param.12, f32[160,2048]{1,0:T(8,128)S(1)} %copy-done.3, bf16[160,2048]{1,0:T(8,128)(2,1)S(1)} %convolution_convert_fusion.1, ...), kind=kOutput, calls=%fused_computation.43 | convolution fusion | flops 1347420032 | bytes 12330241 | tf_op jit(solution)/shard_map/dot_general | solution.py:49
  158.3 0.7 collective-permute-start.4
  159.1 3.1 %fusion.19 = (f32[160]{0:T(256)S(1)}, f32[160,2048]{1,0:T(8,128)S(1)}) fusion(bf16[160,2048]{1,0:T(8,128)(2,1)S(1)} %copy-done.1, f32[160]{0:T(256)S(1)} %copy-done.7, f32[2048]{0:T(1024)S(1)} %bitcast.29, bf16[2048,2048]{1,0:T(8,128)(2,1)S(1)} %bitcast.22, f32[160,2048]{1,0:T(8,128)S(1)} %copy-done.3, bf16[160,2048]{1,0:T(8,128)(2,1)S(1)} %convolution_convert_fusion.1, ...), kind=kOutput, calls=%fused_computation.46 | convolution fusion | flops 1347420032 | bytes 12985601 | tf_op jit(solution)/shard_map/dot_general | solution.py:49
  162.2 1.3 fusion.28
  163.5 1.5 collective-permute-start.5
  165.1 33.8 %collective-permute-done.5 = bf16[160,2048]{1,0:T(8,128)(2,1)} collective-permute-done((bf16[160,2048]{1,0:T(8,128)(2,1)}, bf16[160,2048]{1,0:T(8,128)(2,1)}, u32[]{:S(2)}, u32[]{:S(2)}) %collective-permute-start.5) | collective-permute-done | bytes 655392 | tf_op jit(solution)/shard_map/ppermute | solution.py:16
  198.9 3.9 %convolution_convert_fusion = bf16[2048,2048]{1,0:T(8,128)(2,1)S(1)} fusion(bf16[160,2048]{1,0:T(8,128)(2,1)S(1)} %copy-done.1, f32[160,2048]{1,0:T(8,128)S(1)} %copy-done.3, bf16[160,2048]{1,0:T(8,128)(2,1)S(1)} %convolution_convert_fusion.1, bf16[160,2048]{1,0:T(8,128)(2,1)} %collective-permute-done.5, f32[160]{0:T(256)S(1)} %copy-done.7, ...), kind=kOutput, calls=%fused_computation.1 | convolution fusion | flops 1356529664 | bytes 12329604 | tf_op jit(solution)/shard_map/dot_general | solution.py:168
  202.7 99.8 %all_to_all.16 = bf16[32,64,2048]{2,1,0:T(8,128)(2,1)S(1)} all-to-all(bf16[32,64,2048]{2,1,0:T(8,128)(2,1)S(1)} %bitcast.23), channel_id=1, replica_groups=mesh['section'=4,'blk'=32] {'blk'}, dimensions={0} | all-to-all | bytes 16777216 | tf_op jit(solution)/shard_map/all_to_all | solution.py:173
  302.6 2.9 convert_reduce_fusion
  (62 shorter events, 4.1 us)
Async XLA Ops:
  2.8 2.1 copy-start.5
  4.9 9.2 %slice-start = ((s8[8388608]{0:T(1024)(128)(4,1)}), s8[4194304]{0:T(1024)(128)(4,1)S(1)}, s32[]{:S(2)}) async-start(s8[8388608]{0:T(1024)(128)(4,1)} %bitcast.19), calls=%async_computation.3 | async-start | bytes 8388608
  4.9 9.2 %slice-start.1 = ((s8[8388608]{0:T(1024)(128)(4,1)}), s8[4194304]{0:T(1024)(128)(4,1)S(1)}, s32[]{:S(2)}) async-start(s8[8388608]{0:T(1024)(128)(4,1)} %bitcast.19), calls=%async_computation.4 | async-start | bytes 8388608
  10.3 1.8 copy-start.15
  10.3 3.5 %collective-permute-start = (bf16[160,2048]{1,0:T(8,128)(2,1)S(1)}, bf16[160,2048]{1,0:T(8,128)(2,1)S(1)}, u32[]{:S(2)}, u32[]{:S(2)}) collective-permute-start(bf16[160,2048]{1,0:T(8,128)(2,1)S(1)} %get-tuple-element.22), channel_id=1, source_target_pairs={{0,32},{1,33},{2,34},{3,35},{4,36},{5,37},{6,38},{7,39},{8,40},{9,... | collective-permute-start | bytes 1966088 | tf_op jit(solution)/shard_map/ppermute | solution.py:16
  17.3 0.7 collective-permute-start.1
  18.0 2.2 copy-start.4
  20.2 6.3 %copy-start.11 = (bf16[2048,768]{1,0:T(8,128)(2,1)S(1)}, bf16[2048,768]{1,0:T(8,128)(2,1)}, u32[]{:S(2)}) copy-start(bf16[2048,768]{1,0:T(8,128)(2,1)} %param.15) | copy-start | bytes 9437188
  20.2 6.3 %copy-start.13 = (bf16[2048,768]{1,0:T(8,128)(2,1)S(1)}, bf16[2048,768]{1,0:T(8,128)(2,1)}, u32[]{:S(2)}) copy-start(bf16[2048,768]{1,0:T(8,128)(2,1)} %param.14) | copy-start | bytes 9437188
  20.2 6.3 %copy-start.16 = (bf16[160,2048]{1,0:T(8,128)(2,1)S(1)}, bf16[160,2048]{1,0:T(8,128)(2,1)}, u32[]{:S(2)}) copy-start(bf16[160,2048]{1,0:T(8,128)(2,1)} %copy-done.15) | copy-start | bytes 1966084
  27.9 2.5 copy-start.9
  28.8 0.7 collective-permute-start.2
  123.0 3.1 %copy-start = (bf16[32,160,768]{2,1,0:T(8,128)(2,1)}, bf16[32,160,768]{2,1,0:T(8,128)(2,1)S(1)}, u32[]{:S(2)}) copy-start(bf16[32,160,768]{2,1,0:T(8,128)(2,1)S(1)} %all_to_all.15) | copy-start | bytes 23592964
  126.6 1.3 copy-start.8
  126.6 0.7 collective-permute-start.3
  127.9 14.7 %all-to-all-start.1 = ((f32[32,160,1]{1,2,0:T(1,128)}), f32[32,160,1]{1,2,0:T(1,128)S(1)}, u32[]{:S(2)}, u32[]{:S(2)}) async-start(f32[32,160,1]{1,2,0:T(1,128)} %broadcast_in_dim.70), calls=%async_computation.1 | async-start | bytes 65536 | tf_op jit(solution)/shard_map/all_to_all | solution.py:22
  144.1 5.2 %copy-start.2 = (f32[160,768]{1,0:T(8,128)S(1)}, f32[160,768]{1,0:T(8,128)}, u32[]{:S(2)}) copy-start(f32[160,768]{1,0:T(8,128)} %get-tuple-element.10) | copy-start | bytes 1474564
  144.2 5.2 %copy-start.10 = (f32[160]{0:T(256)S(1)}, f32[160]{0:T(256)}, u32[]{:S(2)}) copy-start(f32[160]{0:T(256)} %copy-done.9) | copy-start | bytes 1924
  144.2 5.2 %copy-start.12 = (bf16[2048,768]{1,0:T(8,128)(2,1)S(1)}, bf16[2048,768]{1,0:T(8,128)(2,1)}, u32[]{:S(2)}) copy-start(bf16[2048,768]{1,0:T(8,128)(2,1)} %param.15) | copy-start | bytes 9437188
  144.2 5.4 %copy-start.14 = (bf16[2048,768]{1,0:T(8,128)(2,1)S(1)}, bf16[2048,768]{1,0:T(8,128)(2,1)}, u32[]{:S(2)}) copy-start(bf16[2048,768]{1,0:T(8,128)(2,1)} %param.14) | copy-start | bytes 9437188
  149.5 1.3 copy-start.1
  149.5 1.5 copy-start.3
  149.6 1.5 copy-start.6
  149.6 1.5 copy-start.7
  149.6 9.5 %slice-start.2 = ((s8[8388608]{0:T(1024)(128)(4,1)}), s8[4194304]{0:T(1024)(128)(4,1)S(1)}, s32[]{:S(2)}) async-start(s8[8388608]{0:T(1024)(128)(4,1)} %bitcast.21), calls=%async_computation.5 | async-start | bytes 8388608
  151.1 8.0 %slice-start.3 = ((s8[8388608]{0:T(1024)(128)(4,1)}), s8[4194304]{0:T(1024)(128)(4,1)S(1)}, s32[]{:S(2)}) async-start(s8[8388608]{0:T(1024)(128)(4,1)} %bitcast.21), calls=%async_computation.6 | async-start | bytes 8388608
  158.3 0.7 collective-permute-start.4
  163.5 35.3 %collective-permute-start.5 = (bf16[160,2048]{1,0:T(8,128)(2,1)}, bf16[160,2048]{1,0:T(8,128)(2,1)}, u32[]{:S(2)}, u32[]{:S(2)}) collective-permute-start(bf16[160,2048]{1,0:T(8,128)(2,1)} %fusion.28), channel_id=1, source_target_pairs={{32,0},{33,1},{34,2},{35,3},{36,4},{37,5},{38,6},{39,7},{40,8},{41... | collective-permute-start | bytes 1966088 | tf_op jit(solution)/shard_map/ppermute | solution.py:16

commit v9 on v3

--- a/solution.py
+++ b/solution.py
@@ -83,8 +83,11 @@
     last_section = lax.axis_size("section") - 1
     top_section = last_section - 1
     spec_section = section_index == last_section
-    token_ids = jnp.where(spec_section, spec_ids, prog_ids)
-    table = jnp.where(spec_section, spec_table, prog_table)
+    token_ids, table = lax.cond(
+        spec_section,
+        lambda: (spec_ids, spec_table),
+        lambda: (prog_ids, prog_table),
+    )
     vocab = table.shape[0]
     high = (token_ids // DIGIT)[:, :, None] == jnp.arange(vocab // DIGIT, dtype=jnp.int32)
     low = (token_ids % DIGIT)[:, :, None] == jnp.arange(DIGIT, dtype=jnp.int32)

time: 305 us -> 304 us (level)
  no operation moved by 1% of the time
where the time goes in v9:
time: 304 us
  blocking collectives  192 us (63%)
  waiting for transfers between devices  41.4 us (14%)
  matrix products  41 us (13%)
  starting transfers between devices  13.5 us (4%)
  other arithmetic  9.92 us (3%)
  local copies, waits for them, and re-layouts  4.99 us (2%)
    all_to_all x1, blocking collectives, local(): landed = lax.all_to_all(pieces, 'blk', 0, 0, tiled=True)  99.8 us
    all_to_all x1, blocking collectives, gather_rows(): got = lax.all_to_all(spread, axis, 0, 0, tiled=True)  92.6 us
    ppermute x6, waiting for transfers between devices, shift_pairs(): return lambda value: lax.ppermute(value, axis, pairs)  35.5 us
    dot_general x3, matrix products, layer_parts(): mixed = jnp.dot(scaled, weight, preferred_element_type=jnp.float32)  14.9 us
    dot_general x2, matrix products, layer_backward(): lax.dot_general(dmixed, weight, (((1,), (1,)), ((), ())), preferred_eleme...  9.95 us
    all_to_all x1, starting transfers between devices, gather_rows(): got = lax.all_to_all(spread, axis, 0, 0, tiled=True)  7.48 us
  transfers between devices with their start and end apart: 7, of which 3 were waited for; matrix products, arithmetic and copies ran while one was open for 0% of the time, Pallas kernels for 0%

profile of v9, /device:TPU:8, one launch (start us, length us, event | category | flops | bytes accessed | tf_op | source)
XLA Modules:
  0.0 303.8 jit_solution(9731291685316109605)
XLA Ops:
  0.0 1.4 copy-done.2
  1.6 1.3 fusion.12
  3.3 0.7 fusion.27
  4.0 5.4 %fusion.30 = (bf16[160,2048]{1,0:T(8,128)(2,1)S(1)}, f32[160,2048]{1,0:T(8,128)S(1)}) fusion(bf16[160,2048]{1,0:T(8,128)(2,1)S(1)} %get-tuple-element.84, pred[]{:T(512)S(6)} %or.3, bf16[2048,2048]{1,0:T(8,128)(2,1)} %param.14, f32[2048]{0:T(1024)S(1)} %bitcast.24, f32[160]{0:T(256)S(1)} %add_rsqrt_fusion.4), kind=kOutput, calls=%fused_computation.57 | convolution fusion | flops 1346437120 | bytes 11018881 | tf_op jit(solution)/shard_map/dot_general | solution.py:31
  9.4 1.8 collective-permute-start
  11.2 1.7 collective-permute-done
  13.2 3.2 %fusion.34 = (bf16[160,2048]{1,0:T(8,128)(2,1)}, f32[160,2048]{1,0:T(8,128)}) fusion(bf16[160,2048]{1,0:T(8,128)(2,1)S(1)} %get-tuple-element.80, bf16[2048,2048]{1,0:T(8,128)(2,1)S(1)} %bitcast.19, f32[160]{0:T(256)S(1)} %add_rsqrt_fusion.3, f32[2048]{0:T(1024)S(1)} %bitcast.25), kind=kOutput, calls=%fused_computation.61 | convolution fusion | flops 1345781760 | bytes 11018880 | tf_op jit(solution)/shard_map/dot_general | solution.py:31
  16.4 0.7 collective-permute-start.1
  17.1 1.9 fusion.20
  19.3 6.3 %select_select_fusion = (f32[160,2048]{1,0:T(8,128)}, f32[160,2048]{1,0:T(8,128)S(1)}) fusion(f32[160,2048]{1,0:T(8,128)S(1)} %copy-done.4, f32[160,2048]{1,0:T(8,128)S(1)} %get-tuple-element.86, pred[]{:T(512)S(6)} %and.34, pred[]{:T(512)S(6)} %and.33, pred[]{:T(512)S(6)} %and.30, bf16[2048,2048]{1,0:T(8,128)(2,1)} %param.14, ...), kind=kOutput, calls=%fused_computation.69 | convolution fusion | flops 1344471040 | bytes 14295683 | tf_op jit(solution)/shard_map/dot_general | solution.py:31
  25.7 1.3 multiply_reduce_fusion.1
  27.0 0.7 collective-permute-start.2
  27.8 0.9 broadcast_in_dim.41
  28.6 92.6 %all_to_all.15 = bf16[32,160,768]{2,1,0:T(8,128)(2,1)S(1)} all-to-all(bf16[32,160,768]{2,1,0:T(8,128)(2,1)S(1)} %broadcast_in_dim.41), channel_id=1, replica_groups=mesh['section'=4,'blk'=32] {'blk'}, dimensions={0} | all-to-all | bytes 15728640 | tf_op jit(solution)/shard_map/all_to_all | solution.py:22
  121.3 2.8 fusion.89
  124.9 0.7 collective-permute-start.3
  126.2 7.5 %all-to-all-start.1 = ((f32[32,160,1]{1,2,0:T(1,128)}), f32[32,160,1]{1,2,0:T(1,128)S(1)}, u32[]{:S(2)}, u32[]{:S(2)}) async-start(f32[32,160,1]{1,2,0:T(1,128)} %broadcast_in_dim.70), calls=%async_computation.1 | async-start | bytes 65536 | tf_op jit(solution)/shard_map/all_to_all | solution.py:22
  133.7 1.2 add_rsqrt_fusion.2
  134.9 6.0 %all-to-all-done.1 = f32[32,160,1]{1,2,0:T(1,128)S(1)} async-done(((f32[32,160,1]{1,2,0:T(1,128)}), f32[32,160,1]{1,2,0:T(1,128)S(1)}, u32[]{:S(2)}, u32[]{:S(2)}) %all-to-all-start.1) | async-done | bytes 20512 | tf_op jit(solution)/shard_map/all_to_all | solution.py:22
  140.9 0.7 reduce
  141.6 0.8 broadcast_in_dim.71
  142.5 5.1 %multiply_reduce_fusion = (f32[160]{0:T(256)S(1)}, f32[160,768]{1,0:T(8,128)S(1)}) fusion(f32[160,768]{1,0:T(8,128)} %copy-done.6, f32[160]{0:T(256)} %copy-done.12, bf16[160,768]{1,0:T(8,128)(2,1)S(1)} %collective-permute-done.2, bf16[5120,768]{1,0:T(8,128)(2,1)} %bitcast.17, f32[160,5120]{1,0:T(8,128)S(1)} %get-tuple-element.94, ...), kind=kOutput, calls=%fused_computation.107 | convolution fusion | flops 1261485952 | bytes 12392321 | tf_op jit(solution)/shard_map/dot_general | solution.py:143
  147.8 1.3 convolution_convert_fusion.1
  149.4 6.8 %fusion.14 = (f32[160]{0:T(256)S(1)}, f32[160,2048]{1,0:T(8,128)S(1)}) fusion(bf16[160,2048]{1,0:T(8,128)(2,1)S(1)} %copy-done.1, f32[160]{0:T(256)S(1)} %copy-done.11, f32[2048]{0:T(1024)S(1)} %bitcast.27, bf16[2048,2048]{1,0:T(8,128)(2,1)} %param.14, f32[160,2048]{1,0:T(8,128)S(1)} %copy-done.3, bf16[160,2048]{1,0:T(8,128)(2,1)S(1)} %convolution_convert_fusion.1, ...), kind=kOutput, calls=%fused_computation.41 | convolution fusion | flops 1347420032 | bytes 12330241 | tf_op jit(solution)/shard_map/dot_general | solution.py:49
  156.6 0.7 collective-permute-start.4
  157.4 3.1 %fusion.17 = (f32[160]{0:T(256)S(1)}, f32[160,2048]{1,0:T(8,128)S(1)}) fusion(bf16[160,2048]{1,0:T(8,128)(2,1)S(1)} %copy-done.1, f32[160]{0:T(256)S(1)} %copy-done.11, f32[2048]{0:T(1024)S(1)} %bitcast.28, bf16[2048,2048]{1,0:T(8,128)(2,1)S(1)} %bitcast.21, f32[160,2048]{1,0:T(8,128)S(1)} %copy-done.3, ...), kind=kOutput, calls=%fused_computation.44 | convolution fusion | flops 1347420032 | bytes 12985601 | tf_op jit(solution)/shard_map/dot_general | solution.py:49
  160.5 1.3 fusion.26
  161.8 1.5 collective-permute-start.5
  163.4 33.8 %collective-permute-done.5 = bf16[160,2048]{1,0:T(8,128)(2,1)} collective-permute-done((bf16[160,2048]{1,0:T(8,128)(2,1)}, bf16[160,2048]{1,0:T(8,128)(2,1)}, u32[]{:S(2)}, u32[]{:S(2)}) %collective-permute-start.5) | collective-permute-done | bytes 655392 | tf_op jit(solution)/shard_map/ppermute | solution.py:16
  197.1 3.9 %convolution_convert_fusion = bf16[2048,2048]{1,0:T(8,128)(2,1)S(1)} fusion(bf16[160,2048]{1,0:T(8,128)(2,1)S(1)} %copy-done.1, f32[160,2048]{1,0:T(8,128)S(1)} %copy-done.3, bf16[160,2048]{1,0:T(8,128)(2,1)S(1)} %convolution_convert_fusion.1, bf16[160,2048]{1,0:T(8,128)(2,1)} %collective-permute-done.5, f32[160]{0:T(256)S(1)} %copy-done.11, ...), kind=kOutput, calls=%fused_computation.1 | convolution fusion | flops 1356529664 | bytes 12329604 | tf_op jit(solution)/shard_map/dot_general | solution.py:170
  201.0 99.8 %all_to_all.16 = bf16[32,64,2048]{2,1,0:T(8,128)(2,1)S(1)} all-to-all(bf16[32,64,2048]{2,1,0:T(8,128)(2,1)S(1)} %bitcast.22), channel_id=1, replica_groups=mesh['section'=4,'blk'=32] {'blk'}, dimensions={0} | all-to-all | bytes 16777216 | tf_op jit(solution)/shard_map/all_to_all | solution.py:175
  300.9 2.9 convert_reduce_fusion
  (71 shorter events, 3.7 us)
Async XLA Ops:
  0.0 1.4 copy-start.2
  0.0 1.4 copy-start.5
  0.0 1.4 copy-start.8
  3.3 0.7 copy-start.9
  4.0 9.2 %slice-start = ((s8[8388608]{0:T(1024)(128)(4,1)}), s8[4194304]{0:T(1024)(128)(4,1)S(1)}, s32[]{:S(2)}) async-start(s8[8388608]{0:T(1024)(128)(4,1)} %bitcast.18), calls=%async_computation.3 | async-start | bytes 8388608
  4.0 9.2 %slice-start.1 = ((s8[8388608]{0:T(1024)(128)(4,1)}), s8[4194304]{0:T(1024)(128)(4,1)S(1)}, s32[]{:S(2)}) async-start(s8[8388608]{0:T(1024)(128)(4,1)} %bitcast.18), calls=%async_computation.4 | async-start | bytes 8388608
  9.4 1.8 copy-start.19
  9.4 3.5 %collective-permute-start = (bf16[160,2048]{1,0:T(8,128)(2,1)S(1)}, bf16[160,2048]{1,0:T(8,128)(2,1)S(1)}, u32[]{:S(2)}, u32[]{:S(2)}) collective-permute-start(bf16[160,2048]{1,0:T(8,128)(2,1)S(1)} %get-tuple-element.85), channel_id=1, source_target_pairs={{0,32},{1,33},{2,34},{3,35},{4,36},{5,37},{6,38},{7,39},{8,40},{9,... | collective-permute-start | bytes 1966088 | tf_op jit(solution)/shard_map/ppermute | solution.py:16
  16.4 0.7 collective-permute-start.1
  17.1 2.2 copy-start.4
  19.3 6.4 %copy-start.15 = (bf16[2048,768]{1,0:T(8,128)(2,1)S(1)}, bf16[2048,768]{1,0:T(8,128)(2,1)}, u32[]{:S(2)}) copy-start(bf16[2048,768]{1,0:T(8,128)(2,1)} %param.17) | copy-start | bytes 9437188
  19.3 6.3 %copy-start.17 = (bf16[2048,768]{1,0:T(8,128)(2,1)S(1)}, bf16[2048,768]{1,0:T(8,128)(2,1)}, u32[]{:S(2)}) copy-start(bf16[2048,768]{1,0:T(8,128)(2,1)} %param.16) | copy-start | bytes 9437188
  19.3 6.3 %copy-start.20 = (bf16[160,2048]{1,0:T(8,128)(2,1)S(1)}, bf16[160,2048]{1,0:T(8,128)(2,1)}, u32[]{:S(2)}) copy-start(bf16[160,2048]{1,0:T(8,128)(2,1)} %copy-done.19) | copy-start | bytes 1966084
  26.9 0.8 copy-start.6
  26.9 0.8 copy-start.12
  27.0 0.7 collective-permute-start.2
  121.3 3.1 %copy-start = (bf16[32,160,768]{2,1,0:T(8,128)(2,1)}, bf16[32,160,768]{2,1,0:T(8,128)(2,1)S(1)}, u32[]{:S(2)}) copy-start(bf16[32,160,768]{2,1,0:T(8,128)(2,1)S(1)} %all_to_all.15) | copy-start | bytes 23592964
  124.9 1.3 copy-start.14
  124.9 0.7 collective-permute-start.3
  126.2 14.7 %all-to-all-start.1 = ((f32[32,160,1]{1,2,0:T(1,128)}), f32[32,160,1]{1,2,0:T(1,128)S(1)}, u32[]{:S(2)}, u32[]{:S(2)}) async-start(f32[32,160,1]{1,2,0:T(1,128)} %broadcast_in_dim.70), calls=%async_computation.1 | async-start | bytes 65536 | tf_op jit(solution)/shard_map/all_to_all | solution.py:22
  142.4 5.2 %copy-start.7 = (f32[160,768]{1,0:T(8,128)S(1)}, f32[160,768]{1,0:T(8,128)}, u32[]{:S(2)}) copy-start(f32[160,768]{1,0:T(8,128)} %copy-done.6) | copy-start | bytes 1474564
  142.4 5.2 %copy-start.13 = (f32[160]{0:T(256)S(1)}, f32[160]{0:T(256)}, u32[]{:S(2)}) copy-start(f32[160]{0:T(256)} %copy-done.12) | copy-start | bytes 1924
  142.4 5.2 %copy-start.16 = (bf16[2048,768]{1,0:T(8,128)(2,1)S(1)}, bf16[2048,768]{1,0:T(8,128)(2,1)}, u32[]{:S(2)}) copy-start(bf16[2048,768]{1,0:T(8,128)(2,1)} %param.17) | copy-start | bytes 9437188
  142.5 5.4 %copy-start.18 = (bf16[2048,768]{1,0:T(8,128)(2,1)S(1)}, bf16[2048,768]{1,0:T(8,128)(2,1)}, u32[]{:S(2)}) copy-start(bf16[2048,768]{1,0:T(8,128)(2,1)} %param.16) | copy-start | bytes 9437188
  147.8 1.3 copy-start.1
  147.8 1.5 copy-start.3
  147.8 1.5 copy-start.10
  147.8 1.5 copy-start.11
  147.8 9.5 %slice-start.2 = ((s8[8388608]{0:T(1024)(128)(4,1)}), s8[4194304]{0:T(1024)(128)(4,1)S(1)}, s32[]{:S(2)}) async-start(s8[8388608]{0:T(1024)(128)(4,1)} %bitcast.20), calls=%async_computation.5 | async-start | bytes 8388608
  149.3 8.0 %slice-start.3 = ((s8[8388608]{0:T(1024)(128)(4,1)}), s8[4194304]{0:T(1024)(128)(4,1)S(1)}, s32[]{:S(2)}) async-start(s8[8388608]{0:T(1024)(128)(4,1)} %bitcast.20), calls=%async_computation.6 | async-start | bytes 8388608
  156.6 0.7 collective-permute-start.4
  161.8 35.3 %collective-permute-start.5 = (bf16[160,2048]{1,0:T(8,128)(2,1)}, bf16[160,2048]{1,0:T(8,128)(2,1)}, u32[]{:S(2)}, u32[]{:S(2)}) collective-permute-start(bf16[160,2048]{1,0:T(8,128)(2,1)} %fusion.26), channel_id=1, source_target_pairs={{32,0},{33,1},{34,2},{35,3},{36,4},{37,5},{38,6},{39,7},{40,8},{41... | collective-permute-start | bytes 1966088 | tf_op jit(solution)/shard_map/ppermute | solution.py:16

commit v10 on v9

--- a/solution.py
+++ b/solution.py
@@ -125,7 +125,7 @@
         senders = [s for s in range(top_section) if 0 <= moment - s < MICRO]
         if senders:
             received = shift_pairs("section", [(s, s + 1) for s in senders])(output)
-    proj = jnp.where(spec_section, spec_proj, prog_proj)
+    proj = lax.cond(spec_section, lambda: spec_proj, lambda: prog_proj)
     unit, inverse, key = embed_rows(tops.reshape(sample_rows, width), proj)
     swap = shift_pairs("section", [(top_section, last_section), (last_section, top_section)])
     partner_key = swap(key)

time: 304 us -> 307 us (level)
  no operation moved by 1% of the time
where the time goes in v10:
time: 307 us; the launch traced here: 306 us
  blocking collectives  193 us (63%)
  matrix products  41.7 us (14%)
  waiting for transfers between devices  39.1 us (13%)
  starting transfers between devices  14.5 us (5%)
  other arithmetic  11.8 us (4%)
  local copies, waits for them, and re-layouts  5.03 us (2%)
    all_to_all x1, blocking collectives, local(): landed = lax.all_to_all(pieces, 'blk', 0, 0, tiled=True)  99.8 us
    all_to_all x1, blocking collectives, gather_rows(): got = lax.all_to_all(spread, axis, 0, 0, tiled=True)  93.5 us
    ppermute x6, waiting for transfers between devices, shift_pairs(): return lambda value: lax.ppermute(value, axis, pairs)  33.2 us
    dot_general x3, matrix products, layer_parts(): mixed = jnp.dot(scaled, weight, preferred_element_type=jnp.float32)  15.8 us
    dot_general x2, matrix products, layer_backward(): lax.dot_general(dmixed, weight, (((1,), (1,)), ((), ())), preferred_eleme...  9.8 us
    all_to_all x1, starting transfers between devices, gather_rows(): got = lax.all_to_all(spread, axis, 0, 0, tiled=True)  7.74 us
    ppermute x6, starting transfers between devices, shift_pairs(): return lambda value: lax.ppermute(value, axis, pairs)  6.8 us
  transfers between devices with their start and end apart: 7, of which 3 were waited for; matrix products, arithmetic and copies ran while one was open for 0% of the time, Pallas kernels for 0%

profile of v10, /device:TPU:8, one launch (start us, length us, event | category | flops | bytes accessed | tf_op | source)
XLA Modules:
  0.0 306.0 jit_solution(11884834248916185036)
XLA Ops:
  0.0 1.4 copy-done.10
  2.1 1.3 fusion.12
  3.8 0.7 fusion.27
  4.5 6.5 %fusion.30 = (bf16[160,2048]{1,0:T(8,128)(2,1)S(1)}, f32[160,2048]{1,0:T(8,128)}) fusion(bf16[160,2048]{1,0:T(8,128)(2,1)S(1)} %get-tuple-element.95, pred[]{:T(512)S(6)} %or.3, bf16[2048,2048]{1,0:T(8,128)(2,1)} %param.16, f32[2048]{0:T(1024)S(1)} %bitcast.26, f32[160]{0:T(256)S(1)} %add_rsqrt_fusion.4), kind=kOutput, calls=%fused_computation.56 | convolution fusion | flops 1346437120 | bytes 11018881 | tf_op jit(solution)/shard_map/dot_general | solution.py:31
  11.0 1.8 collective-permute-start
  12.8 1.7 collective-permute-done
  14.9 3.1 %fusion.34 = (bf16[160,2048]{1,0:T(8,128)(2,1)}, f32[160,2048]{1,0:T(8,128)}) fusion(bf16[160,2048]{1,0:T(8,128)(2,1)S(1)} %get-tuple-element.91, bf16[2048,2048]{1,0:T(8,128)(2,1)S(1)} %bitcast.21, f32[160]{0:T(256)S(1)} %add_rsqrt_fusion.3, f32[2048]{0:T(1024)S(1)} %bitcast.27), kind=kOutput, calls=%fused_computation.60 | convolution fusion | flops 1345781760 | bytes 11018880 | tf_op jit(solution)/shard_map/dot_general | solution.py:31
  18.0 1.5 collective-permute-start.1
  19.5 3.7 %fusion.20 = (f32[160]{0:T(256)}, bf16[160,2048]{1,0:T(8,128)(2,1)}, bf16[160,2048]{1,0:T(8,128)(2,1)S(1)}) fusion(bf16[160,2048]{1,0:T(8,128)(2,1)} %copy-done.7, bf16[160,2048]{1,0:T(8,128)(2,1)} %copy-done.6, pred[]{:T(512)S(6)} %or.3, pred[]{:T(512)S(6)} %and.34, pred[]{:T(512)S(6)} %and.33, pred[]{:T(512)S(6)} %and.30, ...), kind=kLoop, calls=%fused_computation.46 | loop fusion | flops 2621280 | bytes 3277444 | tf_op jit(solution)/shard_map/reduce_sum | solution.py:42
  23.5 6.2 %select_select_fusion = (f32[160,2048]{1,0:T(8,128)}, f32[160,2048]{1,0:T(8,128)S(1)}) fusion(f32[160,2048]{1,0:T(8,128)S(1)} %copy-done.15, f32[160,2048]{1,0:T(8,128)S(1)} %copy-done.14, pred[]{:T(512)S(6)} %and.34, pred[]{:T(512)S(6)} %and.33, pred[]{:T(512)S(6)} %and.30, bf16[2048,2048]{1,0:T(8,128)(2,1)} %param.16, ...), kind=kOutput, calls=%fused_computation.68 | convolution fusion | flops 1344471040 | bytes 14295683 | tf_op jit(solution)/shard_map/dot_general | solution.py:31
  29.7 1.2 multiply_reduce_fusion.1
  31.0 0.7 collective-permute-start.2
  31.7 0.9 broadcast_in_dim.41
  32.6 93.5 %all_to_all.15 = bf16[32,160,768]{2,1,0:T(8,128)(2,1)S(1)} all-to-all(bf16[32,160,768]{2,1,0:T(8,128)(2,1)S(1)} %broadcast_in_dim.41), channel_id=1, replica_groups=mesh['section'=4,'blk'=32] {'blk'}, dimensions={0} | all-to-all | bytes 15728640 | tf_op jit(solution)/shard_map/all_to_all | solution.py:22
  126.1 2.8 fusion.89
  129.7 0.7 collective-permute-start.3
  131.1 7.7 %all-to-all-start.1 = ((f32[32,160,1]{1,2,0:T(1,128)}), f32[32,160,1]{1,2,0:T(1,128)S(1)}, u32[]{:S(2)}, u32[]{:S(2)}) async-start(f32[32,160,1]{1,2,0:T(1,128)} %broadcast_in_dim.70), calls=%async_computation.1 | async-start | bytes 65536 | tf_op jit(solution)/shard_map/all_to_all | solution.py:22
  138.8 1.3 add_rsqrt_fusion.2
  140.1 5.9 %all-to-all-done.1 = f32[32,160,1]{1,2,0:T(1,128)S(1)} async-done(((f32[32,160,1]{1,2,0:T(1,128)}), f32[32,160,1]{1,2,0:T(1,128)S(1)}, u32[]{:S(2)}, u32[]{:S(2)}) %all-to-all-start.1) | async-done | bytes 20512 | tf_op jit(solution)/shard_map/all_to_all | solution.py:22
  146.0 0.7 reduce
  146.7 0.8 broadcast_in_dim.71
  147.6 5.1 %multiply_reduce_fusion = (f32[160]{0:T(256)S(1)}, f32[160,768]{1,0:T(8,128)S(1)}) fusion(f32[160,768]{1,0:T(8,128)} %copy-done.8, f32[160]{0:T(256)} %copy-done.20, bf16[160,768]{1,0:T(8,128)(2,1)S(1)} %collective-permute-done.2, bf16[5120,768]{1,0:T(8,128)(2,1)} %bitcast.19, f32[160,5120]{1,0:T(8,128)S(1)} %get-tuple-element.105, ...), kind=kOutput, calls=%fused_computation.106 | convolution fusion | flops 1261485952 | bytes 12392321 | tf_op jit(solution)/shard_map/dot_general | solution.py:143
  152.8 1.2 convolution_convert_fusion.1
  154.0 6.7 %fusion.14 = (f32[160]{0:T(256)S(1)}, f32[160,2048]{1,0:T(8,128)S(1)}) fusion(bf16[160,2048]{1,0:T(8,128)(2,1)S(1)} %copy-done.4, f32[160]{0:T(256)S(1)} %copy-done.22, f32[2048]{0:T(1024)S(1)} %bitcast.29, bf16[2048,2048]{1,0:T(8,128)(2,1)} %param.16, f32[160,2048]{1,0:T(8,128)S(1)} %copy-done.12, bf16[160,2048]{1,0:T(8,128)(2,1)S(1)} %convolution_convert_fusion.1, ...), kind=kOutput, calls=%fused_computation.40 | convolution fusion | flops 1347420032 | bytes 12330241 | tf_op jit(solution)/shard_map/dot_general | solution.py:49
  161.1 0.7 collective-permute-start.4
  161.9 3.1 %fusion.17 = (f32[160]{0:T(256)S(1)}, f32[160,2048]{1,0:T(8,128)S(1)}) fusion(bf16[160,2048]{1,0:T(8,128)(2,1)S(1)} %copy-done.4, f32[160]{0:T(256)S(1)} %copy-done.22, f32[2048]{0:T(1024)S(1)} %bitcast.30, bf16[2048,2048]{1,0:T(8,128)(2,1)S(1)} %bitcast.23, f32[160,2048]{1,0:T(8,128)S(1)} %copy-done.12, ...), kind=kOutput, calls=%fused_computation.43 | convolution fusion | flops 1347420032 | bytes 12985601 | tf_op jit(solution)/shard_map/dot_general | solution.py:49
  165.0 1.3 fusion.26
  166.3 1.5 collective-permute-start.5
  167.9 31.5 %collective-permute-done.5 = bf16[160,2048]{1,0:T(8,128)(2,1)} collective-permute-done((bf16[160,2048]{1,0:T(8,128)(2,1)}, bf16[160,2048]{1,0:T(8,128)(2,1)}, u32[]{:S(2)}, u32[]{:S(2)}) %collective-permute-start.5) | collective-permute-done | bytes 655392 | tf_op jit(solution)/shard_map/ppermute | solution.py:16
  199.4 3.9 %convolution_convert_fusion = bf16[2048,2048]{1,0:T(8,128)(2,1)S(1)} fusion(bf16[160,2048]{1,0:T(8,128)(2,1)S(1)} %copy-done.5, f32[160,2048]{1,0:T(8,128)S(1)} %copy-done.13, bf16[160,2048]{1,0:T(8,128)(2,1)S(1)} %convolution_convert_fusion.1, bf16[160,2048]{1,0:T(8,128)(2,1)} %collective-permute-done.5, f32[160]{0:T(256)S(1)} %copy-done.22, ...), kind=kOutput, calls=%fused_computation.1 | convolution fusion | flops 1356529664 | bytes 12329604 | tf_op jit(solution)/shard_map/dot_general | solution.py:170
  203.2 99.8 %all_to_all.16 = bf16[32,64,2048]{2,1,0:T(8,128)(2,1)S(1)} all-to-all(bf16[32,64,2048]{2,1,0:T(8,128)(2,1)S(1)} %bitcast.24), channel_id=1, replica_groups=mesh['section'=4,'blk'=32] {'blk'}, dimensions={0} | all-to-all | bytes 16777216 | tf_op jit(solution)/shard_map/all_to_all | solution.py:175
  303.1 2.9 convert_reduce_fusion
  (82 shorter events, 3.8 us)
Async XLA Ops:
  0.0 1.4 copy-start.10
  0.0 1.9 copy-start.11
  0.0 1.9 copy-start.16
  0.0 1.9 copy-start.17
  4.4 10.0 %copy-start.6 = (bf16[160,2048]{1,0:T(8,128)(2,1)}, bf16[160,2048]{1,0:T(8,128)(2,1)S(1)}, u32[]{:S(2)}) copy-start(bf16[160,2048]{1,0:T(8,128)(2,1)S(1)} %get-tuple-element.95) | copy-start | bytes 1966084
  4.5 10.4 %slice-start = ((s8[8388608]{0:T(1024)(128)(4,1)}), s8[4194304]{0:T(1024)(128)(4,1)S(1)}, s32[]{:S(2)}) async-start(s8[8388608]{0:T(1024)(128)(4,1)} %bitcast.20), calls=%async_computation.3 | async-start | bytes 8388608
  4.5 10.4 %slice-start.1 = ((s8[8388608]{0:T(1024)(128)(4,1)}), s8[4194304]{0:T(1024)(128)(4,1)S(1)}, s32[]{:S(2)}) async-start(s8[8388608]{0:T(1024)(128)(4,1)} %bitcast.20), calls=%async_computation.4 | async-start | bytes 8388608
  11.0 3.8 %copy-start.24 = (bf16[160,2048]{1,0:T(8,128)(2,1)}, bf16[160,2048]{1,0:T(8,128)(2,1)S(1)}, u32[]{:S(2)}) copy-start(bf16[160,2048]{1,0:T(8,128)(2,1)S(1)} %get-tuple-element.96) | copy-start | bytes 1966084
  11.0 3.4 %collective-permute-start = (bf16[160,2048]{1,0:T(8,128)(2,1)S(1)}, bf16[160,2048]{1,0:T(8,128)(2,1)S(1)}, u32[]{:S(2)}, u32[]{:S(2)}) collective-permute-start(bf16[160,2048]{1,0:T(8,128)(2,1)S(1)} %get-tuple-element.96), channel_id=1, source_target_pairs={{0,32},{1,33},{2,34},{3,35},{4,36},{5,37},{6,38},{7,39},{8,40},{9,... | collective-permute-start | bytes 1966088 | tf_op jit(solution)/shard_map/ppermute | solution.py:16
  14.8 3.2 %copy-start.7 = (bf16[160,2048]{1,0:T(8,128)(2,1)}, bf16[160,2048]{1,0:T(8,128)(2,1)S(1)}, u32[]{:S(2)}) copy-start(bf16[160,2048]{1,0:T(8,128)(2,1)S(1)} %get-tuple-element.91) | copy-start | bytes 1966084
  14.9 4.6 %copy-start.3 = (bf16[2048,768]{1,0:T(8,128)(2,1)S(1)}, bf16[2048,768]{1,0:T(8,128)(2,1)}, u32[]{:S(2)}) copy-start(bf16[2048,768]{1,0:T(8,128)(2,1)} %param.18) | copy-start | bytes 9437188
  18.0 1.5 collective-permute-start.1
  19.5 10.2 %copy-start.1 = (bf16[2048,768]{1,0:T(8,128)(2,1)}, bf16[2048,768]{1,0:T(8,128)(2,1)S(1)}, u32[]{:S(2)}) copy-start(bf16[2048,768]{1,0:T(8,128)(2,1)S(1)} %get-tuple-element.117) | copy-start | bytes 9437188
  19.5 4.0 %copy-start.14 = (f32[160,2048]{1,0:T(8,128)S(1)}, f32[160,2048]{1,0:T(8,128)}, u32[]{:S(2)}) copy-start(f32[160,2048]{1,0:T(8,128)} %get-tuple-element.97) | copy-start | bytes 3932164
  19.5 4.0 %copy-start.15 = (f32[160,2048]{1,0:T(8,128)S(1)}, f32[160,2048]{1,0:T(8,128)}, u32[]{:S(2)}) copy-start(f32[160,2048]{1,0:T(8,128)} %get-tuple-element.99) | copy-start | bytes 3932164
  23.5 6.2 %copy-start.25 = (bf16[160,2048]{1,0:T(8,128)(2,1)S(1)}, bf16[160,2048]{1,0:T(8,128)(2,1)}, u32[]{:S(2)}) copy-start(bf16[160,2048]{1,0:T(8,128)(2,1)} %copy-done.24) | copy-start | bytes 1966084
  31.0 0.7 collective-permute-start.2
  126.1 3.0 copy-start
  129.7 1.3 copy-start.23
  129.7 0.7 collective-permute-start.3
  131.1 14.9 %all-to-all-start.1 = ((f32[32,160,1]{1,2,0:T(1,128)}), f32[32,160,1]{1,2,0:T(1,128)S(1)}, u32[]{:S(2)}, u32[]{:S(2)}) async-start(f32[32,160,1]{1,2,0:T(1,128)} %broadcast_in_dim.70), calls=%async_computation.1 | async-start | bytes 65536 | tf_op jit(solution)/shard_map/all_to_all | solution.py:22
  147.5 5.2 %copy-start.2 = (bf16[2048,768]{1,0:T(8,128)(2,1)S(1)}, bf16[2048,768]{1,0:T(8,128)(2,1)}, u32[]{:S(2)}) copy-start(bf16[2048,768]{1,0:T(8,128)(2,1)} %copy-done.1) | copy-start | bytes 9437188
  147.5 5.2 %copy-start.9 = (f32[160,768]{1,0:T(8,128)S(1)}, f32[160,768]{1,0:T(8,128)}, u32[]{:S(2)}) copy-start(f32[160,768]{1,0:T(8,128)} %copy-done.8) | copy-start | bytes 1474564
  147.5 5.2 %copy-start.21 = (f32[160]{0:T(256)S(1)}, f32[160]{0:T(256)}, u32[]{:S(2)}) copy-start(f32[160]{0:T(256)} %copy-done.20) | copy-start | bytes 1924
  147.5 6.4 %copy-start.4 = (bf16[160,2048]{1,0:T(8,128)(2,1)S(1)}, bf16[160,2048]{1,0:T(8,128)(2,1)}, u32[]{:S(2)}) copy-start(bf16[160,2048]{1,0:T(8,128)(2,1)} %get-tuple-element.88) | copy-start | bytes 1966084
  147.5 6.4 %copy-start.12 = (f32[160,2048]{1,0:T(8,128)S(1)}, f32[160,2048]{1,0:T(8,128)}, u32[]{:S(2)}) copy-start(f32[160,2048]{1,0:T(8,128)} %get-tuple-element.100) | copy-start | bytes 3932164
  152.7 9.1 %slice-start.2 = ((s8[8388608]{0:T(1024)(128)(4,1)}), s8[4194304]{0:T(1024)(128)(4,1)S(1)}, s32[]{:S(2)}) async-start(s8[8388608]{0:T(1024)(128)(4,1)} %bitcast.22), calls=%async_computation.5 | async-start | bytes 8388608
  154.0 7.9 %slice-start.3 = ((s8[8388608]{0:T(1024)(128)(4,1)}), s8[4194304]{0:T(1024)(128)(4,1)S(1)}, s32[]{:S(2)}) async-start(s8[8388608]{0:T(1024)(128)(4,1)} %bitcast.22), calls=%async_computation.6 | async-start | bytes 8388608
  161.1 0.7 collective-permute-start.4
  165.0 34.4 %copy-start.5 = (bf16[160,2048]{1,0:T(8,128)(2,1)S(1)}, bf16[160,2048]{1,0:T(8,128)(2,1)}, u32[]{:S(2)}) copy-start(bf16[160,2048]{1,0:T(8,128)(2,1)} %get-tuple-element.88) | copy-start | bytes 1966084
  165.0 34.4 %copy-start.13 = (f32[160,2048]{1,0:T(8,128)S(1)}, f32[160,2048]{1,0:T(8,128)}, u32[]{:S(2)}) copy-start(f32[160,2048]{1,0:T(8,128)} %get-tuple-element.100) | copy-start | bytes 3932164
  166.3 33.0 %collective-permute-start.5 = (bf16[160,2048]{1,0:T(8,128)(2,1)}, bf16[160,2048]{1,0:T(8,128)(2,1)}, u32[]{:S(2)}, u32[]{:S(2)}) collective-permute-start(bf16[160,2048]{1,0:T(8,128)(2,1)} %fusion.26), channel_id=1, source_target_pairs={{32,0},{33,1},{34,2},{35,3},{36,4},{37,5},{38,6},{39,7},{40,8},{41... | collective-permute-start | bytes 1966088 | tf_op jit(solution)/shard_map/ppermute | solution.py:16
  (5 other events, 4.8 us)

commit v11 on v9

--- a/solution.py
+++ b/solution.py
@@ -5,7 +5,7 @@
 
 L = 256
 MICRO = 1
-DIGIT = 32
+DIGIT = 16
 
 
 logit_scale = 30.0

time: 304 us -> 304 us (level)
  no operation moved by 1% of the time
where the time goes in v11:
time: 304 us
  blocking collectives  192 us (63%)
  waiting for transfers between devices  41.4 us (14%)
  matrix products  40.8 us (13%)
  starting transfers between devices  13.5 us (4%)
  other arithmetic  9.92 us (3%)
  local copies, waits for them, and re-layouts  5.24 us (2%)
    all_to_all x1, blocking collectives, local(): landed = lax.all_to_all(pieces, 'blk', 0, 0, tiled=True)  99.8 us
    all_to_all x1, blocking collectives, gather_rows(): got = lax.all_to_all(spread, axis, 0, 0, tiled=True)  92.6 us
    ppermute x6, waiting for transfers between devices, shift_pairs(): return lambda value: lax.ppermute(value, axis, pairs)  35.5 us
    dot_general x3, matrix products, layer_parts(): mixed = jnp.dot(scaled, weight, preferred_element_type=jnp.float32)  14.9 us
    dot_general x2, matrix products, layer_backward(): lax.dot_general(dmixed, weight, (((1,), (1,)), ((), ())), preferred_eleme...  9.95 us
    all_to_all x1, starting transfers between devices, gather_rows(): got = lax.all_to_all(spread, axis, 0, 0, tiled=True)  7.48 us
  transfers between devices with their start and end apart: 7, of which 3 were waited for; matrix products, arithmetic and copies ran while one was open for 0% of the time, Pallas kernels for 0%

profile of v11, /device:TPU:8, one launch (start us, length us, event | category | flops | bytes accessed | tf_op | source)
XLA Modules:
  0.0 303.9 jit_solution(1672592768172714253)
XLA Ops:
  0.0 1.4 copy-done.2
  1.6 1.0 fusion.12
  2.6 0.7 copy.14
  4.1 5.4 %fusion.30 = (bf16[160,2048]{1,0:T(8,128)(2,1)S(1)}, f32[160,2048]{1,0:T(8,128)S(1)}) fusion(bf16[160,2048]{1,0:T(8,128)(2,1)S(1)} %get-tuple-element.84, pred[]{:T(512)S(6)} %or.3, bf16[2048,2048]{1,0:T(8,128)(2,1)} %param.14, f32[2048]{0:T(1024)S(1)} %bitcast.24, f32[160]{0:T(256)S(1)} %add_rsqrt_fusion.4), kind=kOutput, calls=%fused_computation.57 | convolution fusion | flops 1346437120 | bytes 11018881 | tf_op jit(solution)/shard_map/dot_general | solution.py:31
  9.4 1.8 collective-permute-start
  11.2 1.7 collective-permute-done
  13.2 3.2 %fusion.34 = (bf16[160,2048]{1,0:T(8,128)(2,1)}, f32[160,2048]{1,0:T(8,128)}) fusion(bf16[160,2048]{1,0:T(8,128)(2,1)S(1)} %get-tuple-element.80, bf16[2048,2048]{1,0:T(8,128)(2,1)S(1)} %bitcast.19, f32[160]{0:T(256)S(1)} %add_rsqrt_fusion.3, f32[2048]{0:T(1024)S(1)} %bitcast.25), kind=kOutput, calls=%fused_computation.61 | convolution fusion | flops 1345781760 | bytes 11018880 | tf_op jit(solution)/shard_map/dot_general | solution.py:31
  16.4 0.7 collective-permute-start.1
  17.2 1.9 fusion.20
  19.4 6.3 %select_select_fusion = (f32[160,2048]{1,0:T(8,128)}, f32[160,2048]{1,0:T(8,128)S(1)}) fusion(f32[160,2048]{1,0:T(8,128)S(1)} %copy-done.4, f32[160,2048]{1,0:T(8,128)S(1)} %get-tuple-element.86, pred[]{:T(512)S(6)} %and.34, pred[]{:T(512)S(6)} %and.33, pred[]{:T(512)S(6)} %and.30, bf16[2048,2048]{1,0:T(8,128)(2,1)} %param.14, ...), kind=kOutput, calls=%fused_computation.69 | convolution fusion | flops 1344471040 | bytes 14295683 | tf_op jit(solution)/shard_map/dot_general | solution.py:31
  25.7 1.3 multiply_reduce_fusion.1
  27.1 0.7 collective-permute-start.2
  27.8 0.9 broadcast_in_dim.41
  28.7 92.6 %all_to_all.15 = bf16[32,160,768]{2,1,0:T(8,128)(2,1)S(1)} all-to-all(bf16[32,160,768]{2,1,0:T(8,128)(2,1)S(1)} %broadcast_in_dim.41), channel_id=1, replica_groups=mesh['section'=4,'blk'=32] {'blk'}, dimensions={0} | all-to-all | bytes 15728640 | tf_op jit(solution)/shard_map/all_to_all | solution.py:22
  121.3 2.8 fusion.89
  125.0 0.7 collective-permute-start.3
  126.3 7.5 %all-to-all-start.1 = ((f32[32,160,1]{1,2,0:T(1,128)}), f32[32,160,1]{1,2,0:T(1,128)S(1)}, u32[]{:S(2)}, u32[]{:S(2)}) async-start(f32[32,160,1]{1,2,0:T(1,128)} %broadcast_in_dim.70), calls=%async_computation.1 | async-start | bytes 65536 | tf_op jit(solution)/shard_map/all_to_all | solution.py:22
  133.8 1.2 add_rsqrt_fusion.2
  135.0 6.0 %all-to-all-done.1 = f32[32,160,1]{1,2,0:T(1,128)S(1)} async-done(((f32[32,160,1]{1,2,0:T(1,128)}), f32[32,160,1]{1,2,0:T(1,128)S(1)}, u32[]{:S(2)}, u32[]{:S(2)}) %all-to-all-start.1) | async-done | bytes 20512 | tf_op jit(solution)/shard_map/all_to_all | solution.py:22
  140.9 0.7 reduce
  141.6 0.8 broadcast_in_dim.71
  142.5 5.1 %multiply_reduce_fusion = (f32[160]{0:T(256)S(1)}, f32[160,768]{1,0:T(8,128)S(1)}) fusion(f32[160,768]{1,0:T(8,128)} %copy-done.6, f32[160]{0:T(256)} %copy-done.12, bf16[160,768]{1,0:T(8,128)(2,1)S(1)} %collective-permute-done.2, bf16[5120,768]{1,0:T(8,128)(2,1)} %bitcast.17, f32[160,5120]{1,0:T(8,128)S(1)} %get-tuple-element.94, ...), kind=kOutput, calls=%fused_computation.107 | convolution fusion | flops 1261485952 | bytes 12392321 | tf_op jit(solution)/shard_map/dot_general | solution.py:143
  147.9 1.3 convolution_convert_fusion.1
  149.4 6.8 %fusion.14 = (f32[160]{0:T(256)S(1)}, f32[160,2048]{1,0:T(8,128)S(1)}) fusion(bf16[160,2048]{1,0:T(8,128)(2,1)S(1)} %copy-done.1, f32[160]{0:T(256)S(1)} %copy-done.11, f32[2048]{0:T(1024)S(1)} %bitcast.27, bf16[2048,2048]{1,0:T(8,128)(2,1)} %param.14, f32[160,2048]{1,0:T(8,128)S(1)} %copy-done.3, bf16[160,2048]{1,0:T(8,128)(2,1)S(1)} %convolution_convert_fusion.1, ...), kind=kOutput, calls=%fused_computation.41 | convolution fusion | flops 1347420032 | bytes 12330241 | tf_op jit(solution)/shard_map/dot_general | solution.py:49
  156.7 0.7 collective-permute-start.4
  157.4 3.1 %fusion.17 = (f32[160]{0:T(256)S(1)}, f32[160,2048]{1,0:T(8,128)S(1)}) fusion(bf16[160,2048]{1,0:T(8,128)(2,1)S(1)} %copy-done.1, f32[160]{0:T(256)S(1)} %copy-done.11, f32[2048]{0:T(1024)S(1)} %bitcast.28, bf16[2048,2048]{1,0:T(8,128)(2,1)S(1)} %bitcast.21, f32[160,2048]{1,0:T(8,128)S(1)} %copy-done.3, ...), kind=kOutput, calls=%fused_computation.44 | convolution fusion | flops 1347420032 | bytes 12985601 | tf_op jit(solution)/shard_map/dot_general | solution.py:49
  160.5 1.3 fusion.26
  161.9 1.5 collective-permute-start.5
  163.4 33.8 %collective-permute-done.5 = bf16[160,2048]{1,0:T(8,128)(2,1)} collective-permute-done((bf16[160,2048]{1,0:T(8,128)(2,1)}, bf16[160,2048]{1,0:T(8,128)(2,1)}, u32[]{:S(2)}, u32[]{:S(2)}) %collective-permute-start.5) | collective-permute-done | bytes 655392 | tf_op jit(solution)/shard_map/ppermute | solution.py:16
  197.2 3.9 %convolution_convert_fusion = bf16[2048,2048]{1,0:T(8,128)(2,1)S(1)} fusion(bf16[160,2048]{1,0:T(8,128)(2,1)S(1)} %copy-done.1, f32[160,2048]{1,0:T(8,128)S(1)} %copy-done.3, bf16[160,2048]{1,0:T(8,128)(2,1)S(1)} %convolution_convert_fusion.1, bf16[160,2048]{1,0:T(8,128)(2,1)} %collective-permute-done.5, f32[160]{0:T(256)S(1)} %copy-done.11, ...), kind=kOutput, calls=%fused_computation.1 | convolution fusion | flops 1356529664 | bytes 12329604 | tf_op jit(solution)/shard_map/dot_general | solution.py:170
  201.1 99.8 %all_to_all.16 = bf16[32,64,2048]{2,1,0:T(8,128)(2,1)S(1)} all-to-all(bf16[32,64,2048]{2,1,0:T(8,128)(2,1)S(1)} %bitcast.22), channel_id=1, replica_groups=mesh['section'=4,'blk'=32] {'blk'}, dimensions={0} | all-to-all | bytes 16777216 | tf_op jit(solution)/shard_map/all_to_all | solution.py:175
  300.9 2.9 convert_reduce_fusion
  (71 shorter events, 3.9 us)
Async XLA Ops:
  0.0 1.4 copy-start.2
  0.0 1.4 copy-start.5
  0.0 1.4 copy-start.8
  3.3 0.7 copy-start.9
  4.0 9.2 %slice-start = ((s8[8388608]{0:T(1024)(128)(4,1)}), s8[4194304]{0:T(1024)(128)(4,1)S(1)}, s32[]{:S(2)}) async-start(s8[8388608]{0:T(1024)(128)(4,1)} %bitcast.18), calls=%async_computation.3 | async-start | bytes 8388608
  4.0 9.2 %slice-start.1 = ((s8[8388608]{0:T(1024)(128)(4,1)}), s8[4194304]{0:T(1024)(128)(4,1)S(1)}, s32[]{:S(2)}) async-start(s8[8388608]{0:T(1024)(128)(4,1)} %bitcast.18), calls=%async_computation.4 | async-start | bytes 8388608
  9.4 1.8 copy-start.19
  9.4 3.5 %collective-permute-start = (bf16[160,2048]{1,0:T(8,128)(2,1)S(1)}, bf16[160,2048]{1,0:T(8,128)(2,1)S(1)}, u32[]{:S(2)}, u32[]{:S(2)}) collective-permute-start(bf16[160,2048]{1,0:T(8,128)(2,1)S(1)} %get-tuple-element.85), channel_id=1, source_target_pairs={{0,32},{1,33},{2,34},{3,35},{4,36},{5,37},{6,38},{7,39},{8,40},{9,... | collective-permute-start | bytes 1966088 | tf_op jit(solution)/shard_map/ppermute | solution.py:16
  16.4 0.7 collective-permute-start.1
  17.1 2.2 copy-start.4
  19.3 6.4 %copy-start.15 = (bf16[2048,768]{1,0:T(8,128)(2,1)S(1)}, bf16[2048,768]{1,0:T(8,128)(2,1)}, u32[]{:S(2)}) copy-start(bf16[2048,768]{1,0:T(8,128)(2,1)} %param.17) | copy-start | bytes 9437188
  19.3 6.3 %copy-start.17 = (bf16[2048,768]{1,0:T(8,128)(2,1)S(1)}, bf16[2048,768]{1,0:T(8,128)(2,1)}, u32[]{:S(2)}) copy-start(bf16[2048,768]{1,0:T(8,128)(2,1)} %param.16) | copy-start | bytes 9437188
  19.4 6.3 %copy-start.20 = (bf16[160,2048]{1,0:T(8,128)(2,1)S(1)}, bf16[160,2048]{1,0:T(8,128)(2,1)}, u32[]{:S(2)}) copy-start(bf16[160,2048]{1,0:T(8,128)(2,1)} %copy-done.19) | copy-start | bytes 1966084
  26.9 0.8 copy-start.6
  27.0 0.8 copy-start.12
  27.1 0.7 collective-permute-start.2
  121.3 3.1 %copy-start = (bf16[32,160,768]{2,1,0:T(8,128)(2,1)}, bf16[32,160,768]{2,1,0:T(8,128)(2,1)S(1)}, u32[]{:S(2)}) copy-start(bf16[32,160,768]{2,1,0:T(8,128)(2,1)S(1)} %all_to_all.15) | copy-start | bytes 23592964
  124.9 1.3 copy-start.14
  125.0 0.7 collective-permute-start.3
  126.3 14.7 %all-to-all-start.1 = ((f32[32,160,1]{1,2,0:T(1,128)}), f32[32,160,1]{1,2,0:T(1,128)S(1)}, u32[]{:S(2)}, u32[]{:S(2)}) async-start(f32[32,160,1]{1,2,0:T(1,128)} %broadcast_in_dim.70), calls=%async_computation.1 | async-start | bytes 65536 | tf_op jit(solution)/shard_map/all_to_all | solution.py:22
  142.5 5.2 %copy-start.7 = (f32[160,768]{1,0:T(8,128)S(1)}, f32[160,768]{1,0:T(8,128)}, u32[]{:S(2)}) copy-start(f32[160,768]{1,0:T(8,128)} %copy-done.6) | copy-start | bytes 1474564
  142.5 5.2 %copy-start.13 = (f32[160]{0:T(256)S(1)}, f32[160]{0:T(256)}, u32[]{:S(2)}) copy-start(f32[160]{0:T(256)} %copy-done.12) | copy-start | bytes 1924
  142.5 5.2 %copy-start.16 = (bf16[2048,768]{1,0:T(8,128)(2,1)S(1)}, bf16[2048,768]{1,0:T(8,128)(2,1)}, u32[]{:S(2)}) copy-start(bf16[2048,768]{1,0:T(8,128)(2,1)} %param.17) | copy-start | bytes 9437188
  142.5 5.4 %copy-start.18 = (bf16[2048,768]{1,0:T(8,128)(2,1)S(1)}, bf16[2048,768]{1,0:T(8,128)(2,1)}, u32[]{:S(2)}) copy-start(bf16[2048,768]{1,0:T(8,128)(2,1)} %param.16) | copy-start | bytes 9437188
  147.9 1.3 copy-start.1
  147.9 1.5 copy-start.3
  147.9 1.5 copy-start.10
  147.9 1.5 copy-start.11
  147.9 9.5 %slice-start.2 = ((s8[8388608]{0:T(1024)(128)(4,1)}), s8[4194304]{0:T(1024)(128)(4,1)S(1)}, s32[]{:S(2)}) async-start(s8[8388608]{0:T(1024)(128)(4,1)} %bitcast.20), calls=%async_computation.5 | async-start | bytes 8388608
  149.4 8.0 %slice-start.3 = ((s8[8388608]{0:T(1024)(128)(4,1)}), s8[4194304]{0:T(1024)(128)(4,1)S(1)}, s32[]{:S(2)}) async-start(s8[8388608]{0:T(1024)(128)(4,1)} %bitcast.20), calls=%async_computation.6 | async-start | bytes 8388608
  156.7 0.7 collective-permute-start.4
  161.9 35.3 %collective-permute-start.5 = (bf16[160,2048]{1,0:T(8,128)(2,1)}, bf16[160,2048]{1,0:T(8,128)(2,1)}, u32[]{:S(2)}, u32[]{:S(2)}) collective-permute-start(bf16[160,2048]{1,0:T(8,128)(2,1)} %fusion.26), channel_id=1, source_target_pairs={{32,0},{33,1},{34,2},{35,3},{36,4},{37,5},{38,6},{39,7},{40,8},{41... | collective-permute-start | bytes 1966088 | tf_op jit(solution)/shard_map/ppermute | solution.py:16
